TPU v7x, 32 devices: a whole 2x2x4 slice. The times are simulated.
32 devices in a mesh: grp: 1, tok: 32 (over z, y, x, core).
Axes of the slice: x: 2, y: 2, z: 4, core: 2. Of those that a mesh axis runs over, the one named last changes fastest.
Arguments:
- activations: bfloat16 [65536, 2048], P('tok')
- out_grads: bfloat16 [65536, 512], P('tok')
- v_bank: bfloat16 [2048, 65536], P('tok'), may hold values from -0.125 to 0.125
- u_bank: bfloat16 [512, 65536], P('tok'), may hold values from -0.25 to 0.25
- query_ids: int32 [16], P('grp'), may hold values from 0 to 2047, as said below
Outputs:
- influence: float32 [65536, 16], P('tok', 'grp')
Inputs may be any that keep to these rules, and one draw needn't show every extreme that they name: `query_ids`: the ids are distinct; both 0 and 2047 are among them.
All inputs are finite; a program needn't handle non-finite values.
Results may differ from a plain program's by a relative error of at most 0.0003.
Values may be sent and summed in bfloat16 or wider, within the bound.
No kernel may reach another device: no remote copies, remote signals or barrier semaphores. Data moves between devices by JAX's collectives and lax.ppermute only.
A program may use at most 128 MiB of HBM per device.

v0:
```python
import jax
import jax.numpy as jnp
from jax import lax
from jax.sharding import PartitionSpec as P

RANK = 32
QUERIES = 16
BANK = 2048


def select_columns(bank, query_ids):
    rows = bank.shape[0]
    shaped = bank.reshape(rows, BANK, RANK)
    picked = jnp.take(shaped, query_ids, axis=1)
    return picked.reshape(rows, QUERIES * RANK)


def folder(left, piece):
    return jnp.dot(left, piece, preferred_element_type=jnp.float32)


def on_device(activations, out_grads, v_bank, u_bank, query_ids):
    tok_rows = activations.shape[0]
    v_sel = select_columns(v_bank, query_ids)
    u_sel = select_columns(u_bank, query_ids)
    proj_in = folder(activations, lax.all_gather(v_sel, "tok", axis=0, tiled=True))
    proj_out = folder(out_grads, lax.all_gather(u_sel, "tok", axis=0, tiled=True))
    scores = (proj_in * proj_out).reshape(tok_rows, QUERIES, RANK).sum(axis=2)
    total = lax.psum(jnp.sum(scores * scores, axis=0), "tok")
    count = tok_rows * lax.axis_size("tok")
    scale = jnp.sqrt(total / count + 1e-06)
    return scores / scale[None, :]


def solution(mesh):
    return jax.shard_map(
        on_device,
        mesh=mesh,
        in_specs=(P("tok", None), P("tok", None), P("tok", None), P("tok", None), P("grp")),
        out_specs=P("tok", "grp"),
        check_vma=False,
    )
```

profile of v0, /device:TPU:0, one launch (start us, length us, event | category | flops | bytes accessed | tf_op | source)
XLA Modules:
  0.0 157.9 jit_solution(17299807252364943729)
XLA Ops:
  6.5 0.0 copy-start
  6.5 0.0 all-gather.2.cloned.1.call-start
  6.5 0.8 compare_and_fusion
  7.4 0.7 compare_select_fusion
  8.0 0.1 broadcast_in_dim.27
  8.1 0.1 broadcast_in_dim.28
  8.2 15.6 %copy.11 = bf16[64,65536]{0,1:T(8,128)(2,1)} copy(bf16[64,65536]{1,0:T(8,128)(2,1)} %param.7) | data formatting | bytes 16777216 | tf_op args[2]
  23.8 6.3 %gather_fusion = bf16[16,64,32]{1,2,0:T(8,128)(2,1)S(1)} fusion(bf16[64,2048,32]{0,2,1:T(8,128)(2,1)} %bitcast.14, s32[1024]{0:T(1024)S(1)} %pad_clamp_fusion), kind=kCustom, calls=%fused_computation | custom fusion | bytes 131136 | tf_op jit(solution)/shard_map/jit(_take)/gather | solution.py:14
  30.1 0.1 bitcast_select_fusion
  30.2 0.7 copy.12
  31.0 0.0 all-gather.2.cloned.1.call-update
  31.0 9.5 %reshape.22 = bf16[16,2048,32]{2,1,0:T(8,128)(2,1)} reshape(bf16[16,65536]{1,0:T(8,128)(2,1)} %param.8) | data formatting | bytes 4194304 | tf_op jit(solution)/shard_map/reshape | solution.py:13
  40.5 10.4 %copy.13 = bf16[16,2048,32]{2,0,1:T(8,128)(2,1)} copy(bf16[16,2048,32]{2,1,0:T(8,128)(2,1)} %reshape.22) | data formatting | bytes 4194304 | tf_op jit(solution)/shard_map/reshape | solution.py:13
  50.9 4.0 %gather_fusion.1 = bf16[16,16,32]{2,1,0:T(8,128)(2,1)S(1)} fusion(bf16[16,2048,32]{2,0,1:T(8,128)(2,1)} %copy.13, s32[1024]{0:T(1024)S(1)} %pad_clamp_fusion), kind=kCustom, calls=%fused_computation.1 | custom fusion | bytes 32832 | tf_op jit(solution)/shard_map/jit(_take)/gather | solution.py:14
  54.8 0.1 gather.15
  55.0 45.3 %all_gather.7 = bf16[512,512]{1,0:T(8,128)(2,1)S(1)} all-gather(bf16[16,512]{1,0:T(8,128)(2,1)S(1)} %broadcast_select_fusion), channel_id=1, replica_groups=mesh['grp'=1,'tok'=32] {'tok'}, dimensions={0}, use_global_device_ids=true | all-gather | bytes 540672 | tf_op jit(solution)/shard_map/all_gather | solution.py:27
  100.3 0.0 copy-done
  100.3 3.2 %fusion = f32[512,2048]{1,0:T(8,128)} fusion(bf16[512,512]{1,0:T(8,128)(2,1)S(1)} %all_gather.7, bf16[2048,512]{1,0:T(8,128)(2,1)S(1)} %copy-done), kind=kOutput, calls=%fused_computation.12 | convolution fusion | flops 1073741824 | bytes 6815744 | tf_op jit(solution)/shard_map/dot_general | solution.py:19
  103.5 0.0 all-gather.2.cloned.1.call-done
  103.5 9.8 %bitcast_reduce_fusion = f32[2048,16]{0,1:T(8,128)S(1)} fusion(f32[512,2048]{1,0:T(8,128)} %fusion, bf16[2048,512]{1,0:T(8,128)(2,1)} %all-gather.2.cloned.1.call-done, bf16[2048,2048]{1,0:T(8,128)(2,1)} %param.5), kind=kOutput, calls=%fused_computation.2 | convolution fusion | flops 4297031680 | bytes 14811136 | tf_op jit(solution)/shard_map/dot_general | solution.py:19
  113.3 0.1 multiply_reduce_fusion
  113.4 36.9 %psum.7 = f32[16]{0:T(128)S(1)} all-reduce(f32[16]{0:T(128)S(1)} %multiply_reduce_fusion), channel_id=1, replica_groups=mesh['grp'=1,'tok'=32] {'tok'}, use_global_device_ids=true, to_apply=%region_2.3 | all-reduce | flops 16 | bytes 128 | tf_op jit(solution)/shard_map/psum | solution.py:29
  150.3 0.7 broadcast_divide_fusion
  (4 shorter events, 0.0 us)
Async XLA Ops:
  6.5 93.7 %copy-start = (bf16[2048,512]{1,0:T(8,128)(2,1)S(1)}, bf16[2048,512]{1,0:T(8,128)(2,1)}, u32[]{:S(2)}) copy-start(bf16[2048,512]{1,0:T(8,128)(2,1)} %param.6) | copy-start | bytes 6291460
  6.5 97.0 %all-gather.2.cloned.1.call-start = ((), (), s32[]{:S(2)}) async-start(), calls=%async_computation | async-start | bytes 2162688 | tf_op jit(solution)/shard_map/all_gather | solution.py:26
Sparse Core Ops, SparseCore 0:
  31.1 59.8 all-gather.1
where the time goes:
time: 159 us; the launch traced here: 158 us
  blocking collectives  82.2 us (52%)
  local copies, waits for them, and re-layouts  46.8 us (29%)
  between operations  13.4 us (8%)
  matrix products  13 us (8%)
  other arithmetic  2.5 us (2%)
    all_gather x1, blocking collectives, on_device(): lax.all_gather(u_sel, 'tok', axis=0, tiled=True)  45.3 us
    psum x1, blocking collectives, on_device(): total = lax.psum(jnp.sum(scores * scores, axis=0), 'tok')  36.9 us
    reshape x2, local copies, waits for them, and re-layouts, select_columns(): shaped = bank.reshape(rows, BANK, RANK)  19.9 us
    unnamed x3, local copies, waits for them, and re-layouts  15.6 us
    dot_general x2, matrix products, folder(): return jnp.dot(left, piece, preferred_element_type=jnp.float32)  13 us
    gather x4, local copies, waits for them, and re-layouts, select_columns(): picked = jnp.take(shaped, query_ids, axis=1)  10.4 us
  transfers between devices with their start and end apart: 1, of which 0 were waited for; matrix products, arithmetic and copies ran while one was open for 17% of the time, Pallas kernels for 0%

commit v1 on v0

v1 whole, which is shorter than its diff:
```python
import jax
import jax.numpy as jnp
from jax import lax
from jax.sharding import PartitionSpec as P

RANK = 32


def select_columns(bank, query_ids):
    pieces = [
        lax.dynamic_slice_in_dim(bank, query_ids[q] * RANK, RANK, axis=1)
        for q in range(query_ids.shape[0])
    ]
    return jnp.concatenate(pieces, axis=1)


def folder(left, piece):
    return jnp.dot(left, piece, preferred_element_type=jnp.float32)


def total_over(x, axis):
    n = lax.axis_size(axis)
    copies = jnp.broadcast_to(x[None], (n,) + x.shape)
    return lax.all_to_all(copies, axis, 0, 0, tiled=False).sum(axis=0)


def on_device(activations, out_grads, v_bank, u_bank, query_ids):
    tok_rows = activations.shape[0]
    queries = query_ids.shape[0]
    v_sel = select_columns(v_bank, query_ids)
    u_sel = select_columns(u_bank, query_ids)
    proj_in = folder(activations, lax.all_gather(v_sel, "tok", axis=0, tiled=True))
    proj_out = folder(out_grads, lax.all_gather(u_sel, "tok", axis=0, tiled=True))
    scores = (proj_in * proj_out).reshape(tok_rows, queries, RANK).sum(axis=2)
    total = total_over(jnp.sum(scores * scores, axis=0), "tok")
    count = tok_rows * lax.axis_size("tok")
    scale = jnp.sqrt(total / count + 1e-06)
    return scores / scale[None, :]


def solution(mesh):
    return jax.shard_map(
        on_device,
        mesh=mesh,
        in_specs=(P("tok", None), P("tok", None), P("tok", None), P("tok", None), P("grp")),
        out_specs=P("tok", "grp"),
        check_vma=False,
    )
```

time: 159 us -> 108 us (0.68)
  local copies, waits for them, and re-layouts: 46.8 us -> 4.99 us
  blocking collectives: 82.2 us -> 55.4 us
  between operations: 13.4 us -> 23.5 us
  waiting for transfers between devices: 0.02 us -> 10.1 us
    psum x1 -> x0, blocking collectives: 36.9 us -> none  [on_device(): total = lax.psum(jnp.sum(scores * scores, axis=0), 'tok')]
    reshape x2 -> x0, local copies, waits for them, and re-layouts: 19.9 us -> none  [select_columns(): shaped = bank.reshape(rows, BANK, RANK)]
    unnamed x3 -> x2, local copies, waits for them, and re-layouts: 15.6 us -> 0.01 us
    gather x4 -> x0, local copies, waits for them, and re-layouts: 10.4 us -> none  [select_columns(): picked = jnp.take(shaped, query_ids, axis=1)]
    all_to_all x0 -> x1, blocking collectives: none -> 10.4 us  [total_over(): return lax.all_to_all(copies, axis, 0, 0, tiled=False).sum(axis=0)]
    all_gather x1, waiting for transfers between devices: 0.01 us -> 10.1 us  [on_device(): lax.all_gather(v_sel, 'tok', axis=0, tiled=True)]
    dynamic_slice x0 -> x2, local copies, waits for them, and re-layouts: none -> 2.13 us  [select_columns(): lax.dynamic_slice_in_dim(bank, query_ids[q] * RANK, RANK, axis=1)]
    slice x0 -> x1, local copies, waits for them, and re-layouts: none -> 1.96 us  [select_columns(): query_ids[q] * RANK]
  transfers between devices with their start and end apart: 1 -> 1, of which waited for: 0 -> 1; matrix products, arithmetic and copies ran while one was open for 17% -> 4% of each run, Pallas kernels for 0% -> 0%
where the time goes in v1:
time: 108 us
  blocking collectives  55.4 us (51%)
  between operations  23.5 us (22%)
  matrix products  13 us (12%)
  waiting for transfers between devices  10.1 us (9%)
  local copies, waits for them, and re-layouts  4.99 us (5%)
    all_gather x1, blocking collectives, on_device(): lax.all_gather(u_sel, 'tok', axis=0, tiled=True)  45 us
    dot_general x2, matrix products, folder(): return jnp.dot(left, piece, preferred_element_type=jnp.float32)  13 us
    all_to_all x1, blocking collectives, total_over(): return lax.all_to_all(copies, axis, 0, 0, tiled=False).sum(axis=0)  10.4 us
    all_gather x1, waiting for transfers between devices, on_device(): lax.all_gather(v_sel, 'tok', axis=0, tiled=True)  10.1 us
  transfers between devices with their start and end apart: 1, of which 1 were waited for; matrix products, arithmetic and copies ran while one was open for 4% of the time, Pallas kernels for 0%

profile of v1, /device:TPU:0, one launch (start us, length us, event | category | flops | bytes accessed | tf_op | source)
XLA Modules:
  0.0 108.0 jit_solution(6873853208284179090)
XLA Ops:
  6.5 0.0 copy-start
  6.5 0.0 all-gather.2.cloned.1.call-start
  6.5 2.0 %fusion = (s32[1]{0:T(128)}, s32[1]{0:T(128)}, s32[1]{0:T(128)}, s32[1]{0:T(128)}, s32[1]{0:T(128)}, /*index=5*/s32[1]{0:T(128)}, s32[1]{0:T(128)}, s32[1]{0:T(1...) fusion(s32[16]{0:T(128)} %param.9), kind=kLoop, calls=%fused_computation.37 | loop fusion | bytes 128 | tf_op jit(solution)/shard_map/slice | solution.py:11
  18.6 1.1 %constant_dynamic-slice_fusion.16 = (bf16[64,32]{1,0:T(8,128)(2,1)S(1)}, bf16[64,32]{1,0:T(8,128)(2,1)S(1)}, bf16[64,32]{1,0:T(8,128)(2,1)S(1)}, bf16[64,32]{1,0...) fusion(bf16[64,65536]{1,0:T(8,128)(2,1)} %param.7, ...), kind=kLoop, calls=%fused_computation.20 | loop fusion | bytes 131136 | tf_op jit(solution)/shard_map/dynamic_slice | solution.py:11
  19.7 0.8 concatenate.6
  20.5 0.0 all-gather.2.cloned.1.call-update
  20.5 1.0 constant_dynamic-slice_fusion
  21.5 0.1 concatenate.7
  21.7 45.0 %all_gather.7 = bf16[512,512]{1,0:T(8,128)(2,1)S(1)} all-gather(bf16[16,512]{1,0:T(8,128)(2,1)S(1)} %concatenate.7), channel_id=1, replica_groups=mesh['grp'=1,'tok'=32] {'tok'}, dimensions={0}, use_global_device_ids=true | all-gather | bytes 540672 | tf_op jit(solution)/shard_map/all_gather | solution.py:33
  66.6 0.0 copy-done
  66.7 3.2 %fusion.1 = f32[512,2048]{1,0:T(8,128)} fusion(bf16[512,512]{1,0:T(8,128)(2,1)S(1)} %all_gather.7, bf16[2048,512]{1,0:T(8,128)(2,1)S(1)} %copy-done), kind=kOutput, calls=%fused_computation.38 | convolution fusion | flops 1073741824 | bytes 6815744 | tf_op jit(solution)/shard_map/dot_general | solution.py:18
  69.9 10.1 %all-gather.2.cloned.1.call-done = bf16[2048,512]{1,0:T(8,128)(2,1)} async-done(((bf16[64,512]{1,0:T(8,128)(2,1)}), bf16[2048,512]{1,0:T(8,128)(2,1)}) %all-gather.2.cloned.1.call-update) | async-done | bytes 2097168 | tf_op jit(solution)/shard_map/all_gather | solution.py:32
  80.0 9.8 %bitcast_reduce_fusion = f32[2048,16]{0,1:T(8,128)S(1)} fusion(f32[512,2048]{1,0:T(8,128)} %fusion.1, bf16[2048,512]{1,0:T(8,128)(2,1)} %all-gather.2.cloned.1.call-done, bf16[2048,2048]{1,0:T(8,128)(2,1)} %param.5), kind=kOutput, calls=%fused_computation | convolution fusion | flops 4297031680 | bytes 14811136 | tf_op jit(solution)/shard_map/dot_general | solution.py:18
  89.8 0.1 multiply_reduce_fusion
  89.9 10.4 %all_to_all.6 = f32[32,1,16]{2,1,0:T(1,128)S(1)} all-to-all(f32[32,1,16]{2,1,0:T(1,128)S(1)} %broadcast_in_dim.2), channel_id=1, replica_groups=mesh['grp'=1,'tok'=32] {'tok'}, dimensions={0} | all-to-all | bytes 4096 | tf_op jit(solution)/shard_map/all_to_all | solution.py:24
  100.3 0.1 reduce_sum.29
  100.4 0.7 broadcast_divide_fusion
  (2 shorter events, 0.0 us)
Async XLA Ops:
  6.5 60.1 %copy-start = (bf16[2048,512]{1,0:T(8,128)(2,1)S(1)}, bf16[2048,512]{1,0:T(8,128)(2,1)}, u32[]{:S(2)}) copy-start(bf16[2048,512]{1,0:T(8,128)(2,1)} %param.6) | copy-start | bytes 6291460
  6.5 73.5 %all-gather.2.cloned.1.call-start = ((), (), s32[]{:S(2)}) async-start(), calls=%async_computation.1 | async-start | bytes 2162688 | tf_op jit(solution)/shard_map/all_gather | solution.py:32
Sparse Core Ops, SparseCore 0:
  20.6 59.3 all-gather.1

commit v2 on v1

--- a/solution.py
+++ b/solution.py
@@ -2,16 +2,55 @@
 import jax.numpy as jnp
 from jax import lax
 from jax.sharding import PartitionSpec as P
+from jax.experimental import pallas as pl
+from jax.experimental.pallas import tpu as pltpu
 
 RANK = 32
+LANES = 128
+PER_TILE = LANES // RANK
 
 
-def select_columns(bank, query_ids):
-    pieces = [
-        lax.dynamic_slice_in_dim(bank, query_ids[q] * RANK, RANK, axis=1)
-        for q in range(query_ids.shape[0])
-    ]
-    return jnp.concatenate(pieces, axis=1)
+def pick_kernel(ids_ref, bank_ref, out_ref, buf, sems):
+    g = pl.program_id(0)
+    rows = out_ref.shape[0]
+    copies = []
+    for j in range(PER_TILE):
+        qid = ids_ref[g * PER_TILE + j]
+        tile = jnp.minimum(jnp.maximum(qid // PER_TILE, 0), bank_ref.shape[1] // LANES - 1)
+        start = pl.multiple_of(tile * LANES, LANES)
+        copy = pltpu.make_async_copy(bank_ref.at[:, pl.ds(start, LANES)], buf.at[j], sems.at[j])
+        copy.start()
+        copies.append(copy)
+    lane = lax.broadcasted_iota(jnp.int32, (rows, LANES), 1)
+    acc = jnp.zeros((rows, LANES), jnp.float32)
+    for j in range(PER_TILE):
+        copies[j].wait()
+        x = buf[j].astype(jnp.float32)
+        off = (ids_ref[g * PER_TILE + j] % PER_TILE) * RANK
+        shift = (RANK * j - off + LANES) % LANES
+        moved = x
+        for s in range(RANK, LANES, RANK):
+            moved = jnp.where(shift == s, pltpu.roll(x, s, 1), moved)
+        keep = (lane >= RANK * j) & (lane < RANK * (j + 1))
+        acc = jnp.where(keep, moved, acc)
+    out_ref[...] = acc.astype(out_ref.dtype)
+
+
+def pick_columns(bank, query_ids):
+    rows = bank.shape[0]
+    queries = query_ids.shape[0]
+    assert queries % PER_TILE == 0
+    return pl.pallas_call(
+        pick_kernel,
+        out_shape=jax.ShapeDtypeStruct((rows, queries * RANK), bank.dtype),
+        grid_spec=pltpu.PrefetchScalarGridSpec(
+            num_scalar_prefetch=1,
+            grid=(queries // PER_TILE,),
+            in_specs=[pl.BlockSpec(memory_space=pl.ANY)],
+            out_specs=pl.BlockSpec((rows, LANES), lambda g, ids: (0, g)),
+            scratch_shapes=[pltpu.VMEM((PER_TILE, rows, LANES), bank.dtype), pltpu.SemaphoreType.DMA((PER_TILE,))],
+        ),
+    )(query_ids, bank)
 
 
 def folder(left, piece):
@@ -27,8 +66,8 @@
 def on_device(activations, out_grads, v_bank, u_bank, query_ids):
     tok_rows = activations.shape[0]
     queries = query_ids.shape[0]
-    v_sel = select_columns(v_bank, query_ids)
-    u_sel = select_columns(u_bank, query_ids)
+    v_sel = pick_columns(v_bank, query_ids)
+    u_sel = pick_columns(u_bank, query_ids)
     proj_in = folder(activations, lax.all_gather(v_sel, "tok", axis=0, tiled=True))
     proj_out = folder(out_grads, lax.all_gather(u_sel, "tok", axis=0, tiled=True))
     scores = (proj_in * proj_out).reshape(tok_rows, queries, RANK).sum(axis=2)

time: 108 us -> 101 us (0.935)
  Pallas kernels: 0 us -> 11 us
  between operations: 23.5 us -> 13.4 us
  local copies, waits for them, and re-layouts: 4.99 us -> 0.02 us
  waiting for transfers between devices: 10.1 us -> 6.17 us
    pallas_call x0 -> x2, Pallas kernels: none -> 11 us  [pick_columns(): pl.pallas_call(pick_kernel, out_shape=jax.ShapeDtypeStruct((rows, queries...]
    all_gather x1, waiting for transfers between devices: 10.1 us -> 6.15 us  [on_device(): lax.all_gather(v_sel, 'tok', axis=0, tiled=True)]
    dynamic_slice x2 -> x0, local copies, waits for them, and re-layouts: 2.13 us -> none  [select_columns(): lax.dynamic_slice_in_dim(bank, query_ids[q] * RANK, RANK, axis=1)]
    slice x1 -> x0, local copies, waits for them, and re-layouts: 1.96 us -> none  [select_columns(): query_ids[q] * RANK]
  transfers between devices with their start and end apart: 1 -> 1, of which waited for: 1 -> 1; matrix products, arithmetic and copies ran while one was open for 4% -> 3% of each run, Pallas kernels for 0% -> 5%
where the time goes in v2:
time: 101 us; the launch traced here: 100 us
  blocking collectives  55.7 us (55%)
  between operations  13.4 us (13%)
  matrix products  13 us (13%)
  Pallas kernels  11 us (11%)
  waiting for transfers between devices  6.17 us (6%)
    all_gather x1, blocking collectives, on_device(): lax.all_gather(u_sel, 'tok', axis=0, tiled=True)  45.4 us
    dot_general x2, matrix products, folder(): return jnp.dot(left, piece, preferred_element_type=jnp.float32)  13 us
    pallas_call x2, Pallas kernels, pick_columns(): pl.pallas_call(pick_kernel, out_shape=jax.ShapeDtypeStruct((rows, queries...  11 us
    all_to_all x1, blocking collectives, total_over(): return lax.all_to_all(copies, axis, 0, 0, tiled=False).sum(axis=0)  10.4 us
    all_gather x1, waiting for transfers between devices, on_device(): lax.all_gather(v_sel, 'tok', axis=0, tiled=True)  6.15 us
  transfers between devices with their start and end apart: 1, of which 1 were waited for; matrix products, arithmetic and copies ran while one was open for 3% of the time, Pallas kernels for 5%

profile of v2, /device:TPU:0, one launch (start us, length us, event | category | flops | bytes accessed | tf_op | source)
XLA Modules:
  0.0 100.3 jit_solution(13623749440194431385)
XLA Ops:
  6.5 0.0 copy-start
  6.5 0.0 all-gather.2.cloned.1.call-start
  6.5 5.7 %shard_map.55 = bf16[64,512]{1,0:T(8,128)(2,1)} custom-call(s32[16]{0:T(128)} %ids_ref.3, bf16[64,65536]{1,0:T(8,128)(2,1)} %bank_ref.2), custom_call_target="tpu_custom_call" | custom-call | tf_op jit(solution)/shard_map/pallas_call | solution.py:43
  12.3 0.0 all-gather.2.cloned.1.call-update
  12.3 5.3 %shard_map.56 = bf16[16,512]{1,0:T(8,128)(2,1)} custom-call(s32[16]{0:T(128)} %ids_ref.3, bf16[16,65536]{1,0:T(8,128)(2,1)} %bank_ref.3), custom_call_target="tpu_custom_call" | custom-call | tf_op jit(solution)/shard_map/pallas_call | solution.py:43
  17.6 45.4 %all_gather.7 = bf16[512,512]{1,0:T(8,128)(2,1)S(1)} all-gather(bf16[16,512]{1,0:T(8,128)(2,1)} %shard_map.56), channel_id=1, replica_groups=mesh['grp'=1,'tok'=32] {'tok'}, dimensions={0}, use_global_device_ids=true | all-gather | bytes 540672 | tf_op jit(solution)/shard_map/all_gather | solution.py:72
  62.9 0.0 copy-done
  63.0 3.2 %fusion = f32[512,2048]{1,0:T(8,128)} fusion(bf16[512,512]{1,0:T(8,128)(2,1)S(1)} %all_gather.7, bf16[2048,512]{1,0:T(8,128)(2,1)S(1)} %copy-done), kind=kOutput, calls=%fused_computation.5 | convolution fusion | flops 1073741824 | bytes 6815744 | tf_op jit(solution)/shard_map/dot_general | solution.py:57
  66.2 6.1 %all-gather.2.cloned.1.call-done = bf16[2048,512]{1,0:T(8,128)(2,1)} async-done(((bf16[64,512]{1,0:T(8,128)(2,1)}), bf16[2048,512]{1,0:T(8,128)(2,1)}) %all-gather.2.cloned.1.call-update) | async-done | bytes 2097168 | tf_op jit(solution)/shard_map/all_gather | solution.py:71
  72.3 9.8 %bitcast_reduce_fusion = f32[2048,16]{0,1:T(8,128)S(1)} fusion(f32[512,2048]{1,0:T(8,128)} %fusion, bf16[2048,512]{1,0:T(8,128)(2,1)} %all-gather.2.cloned.1.call-done, bf16[2048,2048]{1,0:T(8,128)(2,1)} %param.5), kind=kOutput, calls=%fused_computation | convolution fusion | flops 4297031680 | bytes 14811136 | tf_op jit(solution)/shard_map/dot_general | solution.py:57
  82.1 0.1 multiply_reduce_fusion
  82.2 10.4 %all_to_all.6 = f32[32,1,16]{2,1,0:T(1,128)S(1)} all-to-all(f32[32,1,16]{2,1,0:T(1,128)S(1)} %broadcast_in_dim.2), channel_id=1, replica_groups=mesh['grp'=1,'tok'=32] {'tok'}, dimensions={0} | all-to-all | bytes 4096 | tf_op jit(solution)/shard_map/all_to_all | solution.py:63
  92.6 0.1 reduce_sum.29
  92.7 0.7 broadcast_divide_fusion
  (2 shorter events, 0.0 us)
Async XLA Ops:
  6.5 56.4 %copy-start = (bf16[2048,512]{1,0:T(8,128)(2,1)S(1)}, bf16[2048,512]{1,0:T(8,128)(2,1)}, u32[]{:S(2)}) copy-start(bf16[2048,512]{1,0:T(8,128)(2,1)} %param.6) | copy-start | bytes 6291460
  6.5 65.8 %all-gather.2.cloned.1.call-start = ((), (), s32[]{:S(2)}) async-start(), calls=%async_computation.1 | async-start | bytes 2162688 | tf_op jit(solution)/shard_map/all_gather | solution.py:71
Sparse Core Ops, SparseCore 0:
  12.4 59.8 all-gather.1

commit v3 on v1

v3 whole, which is shorter than its diff:
```python
import jax
import jax.numpy as jnp
from jax import lax
from jax.sharding import Mesh, PartitionSpec as P
from jax.experimental import pallas as pl
from jax.experimental.pallas import tpu as pltpu

RANK = 32
LANES = 128
PER_TILE = LANES // RANK


def pick_kernel(ids_ref, v_ref, u_ref, v_out, u_out, v_buf, u_buf, sems):
    queries = ids_ref.shape[0]
    copies = []
    for k, (bank, buf) in enumerate(((v_ref, v_buf), (u_ref, u_buf))):
        last = bank.shape[1] // LANES - 1
        for q in range(queries):
            tile = jnp.minimum(jnp.maximum(ids_ref[q] // PER_TILE, 0), last)
            start = pl.multiple_of(tile * LANES, LANES)
            copy = pltpu.make_async_copy(bank.at[:, pl.ds(start, LANES)], buf.at[q], sems.at[k, q])
            copy.start()
            copies.append(copy)
    for k, (buf, out) in enumerate(((v_buf, v_out), (u_buf, u_out))):
        rows = out.shape[0]
        lane = lax.broadcasted_iota(jnp.int32, (rows, LANES), 1)
        for g in range(queries // PER_TILE):
            acc = jnp.zeros((rows, LANES), jnp.float32)
            for j in range(PER_TILE):
                q = g * PER_TILE + j
                copies[k * queries + q].wait()
                x = buf[q].astype(jnp.float32)
                off = (ids_ref[q] % PER_TILE) * RANK
                shift = (RANK * j - off + LANES) % LANES
                moved = x
                for s in range(RANK, LANES, RANK):
                    moved = jnp.where(shift == s, pltpu.roll(x, s, 1), moved)
                keep = (lane >= RANK * j) & (lane < RANK * (j + 1))
                acc = jnp.where(keep, moved, acc)
            out[:, g * LANES:(g + 1) * LANES] = acc.astype(out.dtype)


def pick_columns(v_bank, u_bank, query_ids):
    queries = query_ids.shape[0]
    assert queries % PER_TILE == 0
    vmem = pl.BlockSpec(memory_space=pltpu.VMEM)
    return pl.pallas_call(
        pick_kernel,
        out_shape=(
            jax.ShapeDtypeStruct((v_bank.shape[0], queries * RANK), v_bank.dtype),
            jax.ShapeDtypeStruct((u_bank.shape[0], queries * RANK), u_bank.dtype),
        ),
        in_specs=[
            pl.BlockSpec(memory_space=pltpu.SMEM),
            pl.BlockSpec(memory_space=pl.ANY),
            pl.BlockSpec(memory_space=pl.ANY),
        ],
        out_specs=(vmem, vmem),
        scratch_shapes=[
            pltpu.VMEM((queries, v_bank.shape[0], LANES), v_bank.dtype),
            pltpu.VMEM((queries, u_bank.shape[0], LANES), u_bank.dtype),
            pltpu.SemaphoreType.DMA((2, queries)),
        ],
    )(query_ids, v_bank, u_bank)


OUTER = "tok_o"
INNER = "tok_i"
TOK = (OUTER, INNER)


def folder(left, piece):
    return jnp.dot(left, piece, preferred_element_type=jnp.float32)


def total_over(x, axis, n):
    copies = jnp.broadcast_to(x[None], (n,) + x.shape)
    return lax.all_to_all(copies, axis, 0, 0, tiled=False).sum(axis=0)


def gather_factors(v_sel, u_sel):
    rows_v = v_sel.shape[0]
    both = jnp.concatenate([v_sel, u_sel], axis=0)
    held = lax.all_gather(both, OUTER, axis=0, tiled=False)
    held = lax.all_gather(held, INNER, axis=0, tiled=False)
    held = jnp.swapaxes(held, 0, 1)
    cols = both.shape[1]
    return held[:, :, :rows_v].reshape(-1, cols), held[:, :, rows_v:].reshape(-1, cols)


def on_device(activations, out_grads, v_bank, u_bank, query_ids):
    tok_rows = activations.shape[0]
    queries = query_ids.shape[0]
    n = lax.axis_size(OUTER) * lax.axis_size(INNER)
    v_sel, u_sel = pick_columns(v_bank, u_bank, query_ids)
    v_full, u_full = gather_factors(v_sel, u_sel)
    proj_in = folder(activations, v_full)
    proj_out = folder(out_grads, u_full)
    scores = (proj_in * proj_out).reshape(tok_rows, queries, RANK).sum(axis=2)
    total = total_over(jnp.sum(scores * scores, axis=0), TOK, n)
    scale = jnp.sqrt(total / (tok_rows * n) + 1e-06)
    return scores / scale[None, :]


def split_mesh(mesh):
    grp, tok = mesh.devices.shape
    inner = 8 if tok % 8 == 0 and tok > 8 else tok
    return Mesh(mesh.devices.reshape(grp, tok // inner, inner), ("grp", OUTER, INNER))


def solution(mesh):
    rows = P(TOK, None)
    return jax.shard_map(
        on_device,
        mesh=split_mesh(mesh),
        in_specs=(rows, rows, rows, rows, P("grp")),
        out_specs=P(TOK, "grp"),
        check_vma=False,
    )
```

time: 108 us -> 91.1 us (0.84)
  blocking collectives: 55.4 us -> 28 us
  waiting for transfers between devices: 10.1 us -> 32.1 us
  between operations: 23.5 us -> 13.5 us
  matrix products: 13 us -> 6.12 us
  Pallas kernels: 0 us -> 4.98 us
    all_gather x1, blocking collectives: 45 us -> 16.4 us  [gather_factors(): held = lax.all_gather(both, OUTER, axis=0, tiled=False)]
    all_gather x1, waiting for transfers between devices: 10.1 us -> 32.1 us  [gather_factors(): held = lax.all_gather(held, INNER, axis=0, tiled=False)]
    dot_general x2, matrix products: 13 us -> 6.12 us  [folder(): return jnp.dot(left, piece, preferred_element_type=jnp.float32)]
    pallas_call x0 -> x1, Pallas kernels: none -> 4.98 us  [pick_columns(): pl.pallas_call(pick_kernel, out_shape=(jax.ShapeDtypeStruct((v_bank.shape...]
    dynamic_slice x2 -> x0, local copies, waits for them, and re-layouts: 2.13 us -> none  [select_columns(): lax.dynamic_slice_in_dim(bank, query_ids[q] * RANK, RANK, axis=1)]
    slice x1 -> x4, local copies, waits for them, and re-layouts: 1.96 us -> 3.3 us  [the longest x2 2.18 us: gather_factors(): held[:, :, :rows_v].reshape(-1, cols)]
    all_to_all x1, blocking collectives: 10.4 us -> 11.6 us  [total_over(): return lax.all_to_all(copies, axis, 0, 0, tiled=False).sum(axis=0)]
  transfers between devices with their start and end apart: 1 -> 1, of which waited for: 1 -> 1; matrix products, arithmetic and copies ran while one was open for 4% -> 0% of each run, Pallas kernels for 0% -> 0%
where the time goes in v3:
time: 91.1 us; the launch traced here: 90.8 us
  waiting for transfers between devices  32.1 us (35%)
  blocking collectives  28 us (31%)
  between operations  13.5 us (15%)
  matrix products  6.12 us (7%)
  Pallas kernels  4.98 us (5%)
  local copies, waits for them, and re-layouts  4.29 us (5%)
  other arithmetic  1.8 us (2%)
    all_gather x1, waiting for transfers between devices, gather_factors(): held = lax.all_gather(held, INNER, axis=0, tiled=False)  32.1 us
    all_gather x1, blocking collectives, gather_factors(): held = lax.all_gather(both, OUTER, axis=0, tiled=False)  16.4 us
    all_to_all x1, blocking collectives, total_over(): return lax.all_to_all(copies, axis, 0, 0, tiled=False).sum(axis=0)  11.6 us
    dot_general x2, matrix products, folder(): return jnp.dot(left, piece, preferred_element_type=jnp.float32)  6.12 us
    pallas_call x1, Pallas kernels, pick_columns(): pl.pallas_call(pick_kernel, out_shape=(jax.ShapeDtypeStruct((v_bank.shape...  4.98 us
    slice x2, local copies, waits for them, and re-layouts, gather_factors(): held[:, :, :rows_v].reshape(-1, cols)  2.18 us
  transfers between devices with their start and end apart: 1, of which 1 were waited for; matrix products, arithmetic and copies ran while one was open for 0% of the time, Pallas kernels for 0%

profile of v3, /device:TPU:0, one launch (start us, length us, event | category | flops | bytes accessed | tf_op | source)
XLA Modules:
  0.0 90.8 jit_solution(11357754798774532275)
XLA Ops:
  6.5 0.0 copy-start
  6.5 0.0 all-gather.4.cloned.1.call-start
  6.5 5.0 %shard_map.55 = (bf16[64,512]{1,0:T(8,128)(2,1)}, bf16[16,512]{1,0:T(8,128)(2,1)}) custom-call(s32[16]{0:T(128)} %ids_ref.1, bf16[64,65536]{1,0:T(8,128)(2,1)} %v_ref.1, bf16[16,65536]{1,0:T(8,128)(2,1)} %u_ref.1), custom_call_target="tpu_custom_call" | custom-call | tf_op jit(solution)/shard_map/pallas_call | solution.py:47
  11.5 0.9 pad_maximum_fusion
  12.4 16.4 %all-gather = bf16[320,512]{1,0:T(8,128)(2,1)} all-gather(bf16[80,512]{1,0:T(8,128)(2,1)S(1)} %pad_maximum_fusion), channel_id=2, replica_groups=mesh['grp'=1,'tok_o'=4,'tok_i'=8] {'tok_o'}, dimensions={0}, use_global_device_ids=true | all-gather | bytes 409600 | tf_op jit(solution)/shard_map/all_gather | solution.py:84
  28.8 0.0 all-gather.4.cloned.1.call-update
  28.8 32.1 %all-gather.4.cloned.1.call-done = bf16[32,80,512]{2,1,0:T(8,128)(2,1)} async-done(((bf16[4,80,512]{2,1,0:T(8,128)(2,1)}), bf16[32,80,512]{2,1,0:T(8,128)(2,1)}) %all-gather.4.cloned.1.call-update) | async-done | bytes 2621456 | tf_op jit(solution)/shard_map/all_gather | solution.py:85
  61.0 1.1 %slice.9 = bf16[4,8,16,512]{3,2,0,1:T(8,128)(2,1)S(1)} slice(bf16[4,8,80,512]{3,2,0,1:T(8,128)(2,1)} %bitcast.15), slice={[0:4], [0:8], [64:80], [0:512]} | slice | bytes 1048576 | tf_op jit(solution)/shard_map/slice | solution.py:88
  62.1 0.0 slice-start
  62.1 2.0 %slice.8 = bf16[4,8,64,512]{3,2,0,1:T(8,128)(2,1)S(1)} slice(bf16[4,8,80,512]{3,2,0,1:T(8,128)(2,1)} %bitcast.16), slice={[0:4], [0:8], [0:64], [0:512]} | slice | bytes 4194304 | tf_op jit(solution)/shard_map/slice | solution.py:88
  64.0 0.2 copy.12
  64.3 0.0 slice-start.1
  64.3 0.0 copy-done
  64.3 1.3 %fusion = f32[512,2048]{1,0:T(8,128)S(1)} fusion(bf16[512,512]{1,0:T(8,128)(2,1)S(1)} %bitcast.14, bf16[2048,512]{1,0:T(8,128)(2,1)S(1)} %copy-done), kind=kOutput, calls=%fused_computation.6 | convolution fusion | flops 1073741824 | bytes 6815744 | tf_op jit(solution)/shard_map/dot_general | solution.py:73
  65.6 0.0 slice-done
  65.7 1.0 %slice-done.1 = s8[4194304]{0:T(1024)(128)(4,1)S(1)} async-done(((s8[8388608]{0:T(1024)(128)(4,1)}), s8[4194304]{0:T(1024)(128)(4,1)S(1)}, s32[]{:S(2)}) %slice-start.1) | async-done | bytes 4194328
  66.6 4.8 %bitcast_reduce_fusion = f32[2048,16]{0,1:T(8,128)S(1)} fusion(f32[512,2048]{1,0:T(8,128)S(1)} %fusion, bf16[2048,512]{1,0:T(8,128)(2,1)S(1)} %bitcast.17, bf16[2048,2048]{1,0:T(8,128)(2,1)S(1)} %bitcast.20), kind=kOutput, calls=%fused_computation | convolution fusion | flops 4297031680 | bytes 14811136 | tf_op jit(solution)/shard_map/dot_general | solution.py:73
  71.4 0.1 multiply_reduce_fusion
  71.6 11.6 %all_to_all.6 = f32[32,1,16]{2,1,0:T(1,128)S(1)} all-to-all(f32[32,1,16]{2,1,0:T(1,128)S(1)} %broadcast_in_dim.2), channel_id=1, replica_groups=mesh['grp'=1,'tok_o'=4,'tok_i'=8] {'tok_o','tok_i'}, dimensions={0} | all-to-all | bytes 4096 | tf_op jit(solution)/shard_map/all_to_all | solution.py:78
  83.1 0.1 reduce_sum.29
  83.2 0.7 broadcast_divide_fusion
  (4 shorter events, 0.1 us)
Async XLA Ops:
  6.5 57.8 %copy-start = (bf16[2048,512]{1,0:T(8,128)(2,1)S(1)}, bf16[2048,512]{1,0:T(8,128)(2,1)}, u32[]{:S(2)}) copy-start(bf16[2048,512]{1,0:T(8,128)(2,1)} %param.6) | copy-start | bytes 6291460
  6.5 54.4 %all-gather.4.cloned.1.call-start = ((), (), s32[]{:S(2)}) async-start(), calls=%async_computation.1 | async-start | bytes 2949120 | tf_op jit(solution)/shard_map/all_gather | solution.py:85
  62.1 3.6 %slice-start = ((s8[8388608]{0:T(1024)(128)(4,1)}), s8[4194304]{0:T(1024)(128)(4,1)S(1)}, s32[]{:S(2)}) async-start(s8[8388608]{0:T(1024)(128)(4,1)} %bitcast.19), calls=%async_computation.2 | async-start | bytes 8388608
  64.3 2.3 %slice-start.1 = ((s8[8388608]{0:T(1024)(128)(4,1)}), s8[4194304]{0:T(1024)(128)(4,1)S(1)}, s32[]{:S(2)}) async-start(s8[8388608]{0:T(1024)(128)(4,1)} %bitcast.19), calls=%async_computation.3 | async-start | bytes 8388608
Sparse Core Ops, SparseCore 0:
  29.0 31.9 all-gather.3

commit v4 on v3

--- a/solution.py
+++ b/solution.py
@@ -65,8 +65,9 @@
 
 
 OUTER = "tok_o"
-INNER = "tok_i"
-TOK = (OUTER, INNER)
+MIDDLE = "tok_m"
+CORE = "tok_c"
+TOK = (OUTER, MIDDLE, CORE)
 
 
 def folder(left, piece):
@@ -78,20 +79,27 @@
     return lax.all_to_all(copies, axis, 0, 0, tiled=False).sum(axis=0)
 
 
+def spread(x, axis):
+    k = lax.axis_size(axis)
+    copies = jnp.broadcast_to(x[None], (k,) + x.shape)
+    return lax.all_to_all(copies, axis, 0, 0, tiled=False)
+
+
 def gather_factors(v_sel, u_sel):
     rows_v = v_sel.shape[0]
+    cols = v_sel.shape[1]
     both = jnp.concatenate([v_sel, u_sel], axis=0)
     held = lax.all_gather(both, OUTER, axis=0, tiled=False)
-    held = lax.all_gather(held, INNER, axis=0, tiled=False)
-    held = jnp.swapaxes(held, 0, 1)
-    cols = both.shape[1]
-    return held[:, :, :rows_v].reshape(-1, cols), held[:, :, rows_v:].reshape(-1, cols)
+    held = spread(held, MIDDLE)
+    held = spread(held, CORE)
+    held = jnp.transpose(held, (2, 1, 0, 3, 4))
+    return held[:, :, :, :rows_v].reshape(-1, cols), held[:, :, :, rows_v:].reshape(-1, cols)
 
 
 def on_device(activations, out_grads, v_bank, u_bank, query_ids):
     tok_rows = activations.shape[0]
     queries = query_ids.shape[0]
-    n = lax.axis_size(OUTER) * lax.axis_size(INNER)
+    n = lax.axis_size(OUTER) * lax.axis_size(MIDDLE) * lax.axis_size(CORE)
     v_sel, u_sel = pick_columns(v_bank, u_bank, query_ids)
     v_full, u_full = gather_factors(v_sel, u_sel)
     proj_in = folder(activations, v_full)
@@ -104,8 +112,8 @@
 
 def split_mesh(mesh):
     grp, tok = mesh.devices.shape
-    inner = 8 if tok % 8 == 0 and tok > 8 else tok
-    return Mesh(mesh.devices.reshape(grp, tok // inner, inner), ("grp", OUTER, INNER))
+    assert tok % 8 == 0
+    return Mesh(mesh.devices.reshape(grp, tok // 8, 4, 2), ("grp",) + TOK)
 
 
 def solution(mesh):

time: 91.1 us -> 66.4 us (0.73)
  waiting for transfers between devices: 32.1 us -> 0 us
  blocking collectives: 28 us -> 50.3 us
  between operations: 13.5 us -> 0.09 us
  local copies, waits for them, and re-layouts: 4.29 us -> 2.74 us
    all_gather x1 -> x0, waiting for transfers between devices: 32.1 us -> none  [gather_factors(): held = lax.all_gather(held, INNER, axis=0, tiled=False)]
    all_to_all x0 -> x2, blocking collectives: none -> 24.3 us  [spread(): return lax.all_to_all(copies, axis, 0, 0, tiled=False)]
    slice x4 -> x2, local copies, waits for them, and re-layouts: 3.3 us -> 0.17 us  [the longest x1 0.14 us: gather_factors(): held[:, :, :, :rows_v].reshape(-1, cols)]
    all_to_all x1, blocking collectives: 11.6 us -> 10.2 us  [total_over(): return lax.all_to_all(copies, axis, 0, 0, tiled=False).sum(axis=0)]
  transfers between devices with their start and end apart: 1 -> 0, of which waited for: 1 -> 0; matrix products, arithmetic and copies ran while one was open for 0% -> 0% of each run, Pallas kernels for 0% -> 0%
where the time goes in v4:
time: 66.4 us; the launch traced here: 66.1 us
  blocking collectives  50.3 us (76%)
  matrix products  6.12 us (9%)
  Pallas kernels  4.97 us (7%)
  local copies, waits for them, and re-layouts  2.74 us (4%)
  other arithmetic  1.8 us (3%)
    all_to_all x2, blocking collectives, spread(): return lax.all_to_all(copies, axis, 0, 0, tiled=False)  24.3 us
    all_gather x1, blocking collectives, gather_factors(): held = lax.all_gather(both, OUTER, axis=0, tiled=False)  15.8 us
    all_to_all x1, blocking collectives, total_over(): return lax.all_to_all(copies, axis, 0, 0, tiled=False).sum(axis=0)  10.2 us
    dot_general x2, matrix products, folder(): return jnp.dot(left, piece, preferred_element_type=jnp.float32)  6.12 us
    pallas_call x1, Pallas kernels, pick_columns(): pl.pallas_call(pick_kernel, out_shape=(jax.ShapeDtypeStruct((v_bank.shape...  4.97 us
    unnamed x6, local copies, waits for them, and re-layouts  1.77 us

profile of v4, /device:TPU:0, one launch (start us, length us, event | category | flops | bytes accessed | tf_op | source)
XLA Modules:
  0.0 66.1 jit_solution(4740480965880810162)
XLA Ops:
  0.0 0.0 copy-start
  0.0 5.0 %shard_map.55 = (bf16[64,512]{1,0:T(8,128)(2,1)}, bf16[16,512]{1,0:T(8,128)(2,1)}) custom-call(s32[16]{0:T(128)} %ids_ref.1, bf16[64,65536]{1,0:T(8,128)(2,1)} %v_ref.1, bf16[16,65536]{1,0:T(8,128)(2,1)} %u_ref.1), custom_call_target="tpu_custom_call" | custom-call | tf_op jit(solution)/shard_map/pallas_call | solution.py:47
  5.0 0.9 %pad_maximum_fusion = bf16[80,512]{1,0:T(8,128)(2,1)S(1)} fusion(bf16[16,512]{1,0:T(8,128)(2,1)} %get-tuple-element.8, bf16[64,512]{1,0:T(8,128)(2,1)} %get-tuple-element.7), kind=kLoop, calls=%fused_computation.4 | loop fusion | flops 163840 | bytes 163840 | tf_op jit(solution)/shard_map/concatenate | solution.py:91
  5.8 15.8 %all-gather = bf16[320,512]{1,0:T(8,128)(2,1)S(1)} all-gather(bf16[80,512]{1,0:T(8,128)(2,1)S(1)} %pad_maximum_fusion), channel_id=2, replica_groups=mesh['grp'=1,'tok_o'=4,'tok_m'=4,'tok_c'=2] {'tok_o'}, dimensions={0}, use_global_device_ids=true | all-gather | bytes 409600 | tf_op jit(solution)/shard_map/all_gather | solution.py:92
  21.7 0.1 broadcast_in_dim.6
  21.8 18.5 %all_to_all.16 = bf16[4,4,80,512]{3,2,1,0:T(8,128)(2,1)S(1)} all-to-all(bf16[4,4,80,512]{3,2,1,0:T(8,128)(2,1)S(1)} %broadcast_in_dim.6), channel_id=1, replica_groups=mesh['grp'=1,'tok_o'=4,'tok_m'=4,'tok_c'=2] {'tok_m'}, dimensions={0} | all-to-all | bytes 2621440 | tf_op jit(solution)/shard_map/all_to_all | solution.py:85
  40.3 0.1 copy.10
  40.4 0.3 broadcast_in_dim.7
  40.7 5.8 %all_to_all.17 = bf16[2,4,4,80,512]{4,3,1,2,0:T(8,128)(2,1)S(1)} all-to-all(bf16[2,4,4,80,512]{4,3,1,2,0:T(8,128)(2,1)S(1)} %broadcast_in_dim.7), channel_id=1, replica_groups=mesh['grp'=1,'tok_o'=4,'tok_m'=4,'tok_c'=2] {'tok_c'}, dimensions={0} | all-to-all | bytes 5242880 | tf_op jit(solution)/shard_map/all_to_all | solution.py:85
  46.5 0.0 slice-start
  46.6 0.3 copy.15
  46.9 0.0 slice-start.1
  46.9 0.1 slice.8
  47.0 0.0 copy-done
  47.0 1.3 %fusion = f32[512,2048]{1,0:T(8,128)S(1)} fusion(bf16[512,512]{1,0:T(8,128)(2,1)S(1)} %bitcast.16, bf16[2048,512]{1,0:T(8,128)(2,1)S(1)} %copy-done), kind=kOutput, calls=%fused_computation.7 | convolution fusion | flops 1073741824 | bytes 6815744 | tf_op jit(solution)/shard_map/dot_general | solution.py:74
  48.3 0.4 slice-done
  48.7 1.4 %slice-done.1 = s8[4194304]{0:T(1024)(128)(4,1)S(1)} async-done(((s8[8388608]{0:T(1024)(128)(4,1)}), s8[4194304]{0:T(1024)(128)(4,1)S(1)}, s32[]{:S(2)}) %slice-start.1) | async-done | bytes 4194328
  50.1 4.8 %bitcast_reduce_fusion = f32[2048,16]{0,1:T(8,128)S(1)} fusion(f32[512,2048]{1,0:T(8,128)S(1)} %fusion, bf16[2048,512]{1,0:T(8,128)(2,1)S(1)} %bitcast.17, bf16[2048,2048]{1,0:T(8,128)(2,1)S(1)} %bitcast.20), kind=kOutput, calls=%fused_computation | convolution fusion | flops 4297031680 | bytes 14811136 | tf_op jit(solution)/shard_map/dot_general | solution.py:74
  54.9 0.1 multiply_reduce_fusion
  55.1 10.2 %all_to_all.18 = f32[32,1,16]{2,1,0:T(1,128)S(1)} all-to-all(f32[32,1,16]{2,1,0:T(1,128)S(1)} %broadcast_in_dim.8), channel_id=1, replica_groups=mesh['grp'=1,'tok_o'=4,'tok_m'=4,'tok_c'=2] {'tok_o','tok_m','tok_c'}, dimensions={0} | all-to-all | bytes 4096 | tf_op jit(solution)/shard_map/all_to_all | solution.py:79
  65.3 0.1 reduce_sum.29
  65.3 0.7 %broadcast_divide_fusion = f32[2048,16]{0,1:T(8,128)} fusion(f32[2048,16]{0,1:T(8,128)S(1)} %bitcast_reduce_fusion, f32[16]{0:T(128)S(1)} %add_sqrt_fusion), kind=kLoop, calls=%fused_computation.5 | loop fusion | flops 32768 | bytes 262208 | tf_op jit(solution)/shard_map/div | solution.py:110
  (4 shorter events, 0.1 us)
Async XLA Ops:
  0.0 47.0 %copy-start = (bf16[2048,512]{1,0:T(8,128)(2,1)S(1)}, bf16[2048,512]{1,0:T(8,128)(2,1)}, u32[]{:S(2)}) copy-start(bf16[2048,512]{1,0:T(8,128)(2,1)} %param.6) | copy-start | bytes 6291460
  46.5 2.2 %slice-start = ((s8[8388608]{0:T(1024)(128)(4,1)}), s8[4194304]{0:T(1024)(128)(4,1)S(1)}, s32[]{:S(2)}) async-start(s8[8388608]{0:T(1024)(128)(4,1)} %bitcast.19), calls=%async_computation.3 | async-start | bytes 8388608
  46.9 3.2 %slice-start.1 = ((s8[8388608]{0:T(1024)(128)(4,1)}), s8[4194304]{0:T(1024)(128)(4,1)S(1)}, s32[]{:S(2)}) async-start(s8[8388608]{0:T(1024)(128)(4,1)} %bitcast.19), calls=%async_computation.4 | async-start | bytes 8388608

commit v5 on v4

--- a/solution.py
+++ b/solution.py
@@ -10,7 +10,7 @@
 PER_TILE = LANES // RANK
 
 
-def pick_kernel(ids_ref, v_ref, u_ref, v_out, u_out, v_buf, u_buf, sems):
+def pick_kernel(ids_ref, v_ref, u_ref, out, v_buf, u_buf, sems):
     queries = ids_ref.shape[0]
     copies = []
     for k, (bank, buf) in enumerate(((v_ref, v_buf), (u_ref, u_buf))):
@@ -21,8 +21,10 @@
             copy = pltpu.make_async_copy(bank.at[:, pl.ds(start, LANES)], buf.at[q], sems.at[k, q])
             copy.start()
             copies.append(copy)
-    for k, (buf, out) in enumerate(((v_buf, v_out), (u_buf, u_out))):
-        rows = out.shape[0]
+    bases = (0, v_buf.shape[1])
+    for k, buf in enumerate((v_buf, u_buf)):
+        rows = buf.shape[1]
+        base = bases[k]
         lane = lax.broadcasted_iota(jnp.int32, (rows, LANES), 1)
         for g in range(queries // PER_TILE):
             acc = jnp.zeros((rows, LANES), jnp.float32)
@@ -37,7 +39,7 @@
                     moved = jnp.where(shift == s, pltpu.roll(x, s, 1), moved)
                 keep = (lane >= RANK * j) & (lane < RANK * (j + 1))
                 acc = jnp.where(keep, moved, acc)
-            out[:, g * LANES:(g + 1) * LANES] = acc.astype(out.dtype)
+            out[base:base + rows, g * LANES:(g + 1) * LANES] = acc.astype(out.dtype)
 
 
 def pick_columns(v_bank, u_bank, query_ids):
@@ -46,16 +48,13 @@
     vmem = pl.BlockSpec(memory_space=pltpu.VMEM)
     return pl.pallas_call(
         pick_kernel,
-        out_shape=(
-            jax.ShapeDtypeStruct((v_bank.shape[0], queries * RANK), v_bank.dtype),
-            jax.ShapeDtypeStruct((u_bank.shape[0], queries * RANK), u_bank.dtype),
-        ),
+        out_shape=jax.ShapeDtypeStruct((v_bank.shape[0] + u_bank.shape[0], queries * RANK), v_bank.dtype),
         in_specs=[
             pl.BlockSpec(memory_space=pltpu.SMEM),
             pl.BlockSpec(memory_space=pl.ANY),
             pl.BlockSpec(memory_space=pl.ANY),
         ],
-        out_specs=(vmem, vmem),
+        out_specs=vmem,
         scratch_shapes=[
             pltpu.VMEM((queries, v_bank.shape[0], LANES), v_bank.dtype),
             pltpu.VMEM((queries, u_bank.shape[0], LANES), u_bank.dtype),
@@ -79,20 +78,17 @@
     return lax.all_to_all(copies, axis, 0, 0, tiled=False).sum(axis=0)
 
 
-def spread(x, axis):
+def spread(x, axis, at):
     k = lax.axis_size(axis)
-    copies = jnp.broadcast_to(x[None], (k,) + x.shape)
-    return lax.all_to_all(copies, axis, 0, 0, tiled=False)
+    copies = jnp.broadcast_to(jnp.expand_dims(x, at), x.shape[:at] + (k,) + x.shape[at:])
+    return lax.all_to_all(copies, axis, at, at, tiled=True)
 
 
-def gather_factors(v_sel, u_sel):
-    rows_v = v_sel.shape[0]
-    cols = v_sel.shape[1]
-    both = jnp.concatenate([v_sel, u_sel], axis=0)
+def gather_factors(both, rows_v):
+    cols = both.shape[1]
     held = lax.all_gather(both, OUTER, axis=0, tiled=False)
-    held = spread(held, MIDDLE)
-    held = spread(held, CORE)
-    held = jnp.transpose(held, (2, 1, 0, 3, 4))
+    held = spread(held, MIDDLE, 1)
+    held = spread(held, CORE, 2)
     return held[:, :, :, :rows_v].reshape(-1, cols), held[:, :, :, rows_v:].reshape(-1, cols)
 
 
@@ -100,8 +96,8 @@
     tok_rows = activations.shape[0]
     queries = query_ids.shape[0]
     n = lax.axis_size(OUTER) * lax.axis_size(MIDDLE) * lax.axis_size(CORE)
-    v_sel, u_sel = pick_columns(v_bank, u_bank, query_ids)
-    v_full, u_full = gather_factors(v_sel, u_sel)
+    both = pick_columns(v_bank, u_bank, query_ids)
+    v_full, u_full = gather_factors(both, v_bank.shape[0])
     proj_in = folder(activations, v_full)
     proj_out = folder(out_grads, u_full)
     scores = (proj_in * proj_out).reshape(tok_rows, queries, RANK).sum(axis=2)

time: 66.4 us -> 65.9 us (level)
  other arithmetic: 1.8 us -> 0.94 us
    concatenate x1 -> x0, other arithmetic: 0.87 us -> none  [gather_factors(): both = jnp.concatenate([v_sel, u_sel], axis=0)]
    unnamed x6 -> x8, local copies, waits for them, and re-layouts: 1.77 us -> 2.16 us
where the time goes in v5:
time: 65.9 us; the launch traced here: 65.6 us
  blocking collectives  50.6 us (77%)
  matrix products  6.12 us (9%)
  Pallas kernels  5.01 us (8%)
  local copies, waits for them, and re-layouts  2.91 us (4%)
  other arithmetic  0.94 us (1%)
    all_to_all x2, blocking collectives, spread(): return lax.all_to_all(copies, axis, at, at, tiled=True)  24.3 us
    all_gather x1, blocking collectives, gather_factors(): held = lax.all_gather(both, OUTER, axis=0, tiled=False)  16.1 us
    all_to_all x1, blocking collectives, total_over(): return lax.all_to_all(copies, axis, 0, 0, tiled=False).sum(axis=0)  10.2 us
    dot_general x2, matrix products, folder(): return jnp.dot(left, piece, preferred_element_type=jnp.float32)  6.12 us
    pallas_call x1, Pallas kernels, pick_columns(): pl.pallas_call(pick_kernel, out_shape=jax.ShapeDtypeStruct((v_bank.shape[...  5.01 us
    unnamed x8, local copies, waits for them, and re-layouts  2.16 us

profile of v5, /device:TPU:0, one launch (start us, length us, event | category | flops | bytes accessed | tf_op | source)
XLA Modules:
  0.0 65.6 jit_solution(15966614793381188107)
XLA Ops:
  0.0 0.0 copy-start
  0.0 5.0 %shard_map.55 = bf16[80,512]{1,0:T(8,128)(2,1)} custom-call(s32[16]{0:T(128)} %ids_ref.1, bf16[64,65536]{1,0:T(8,128)(2,1)} %v_ref.1, bf16[16,65536]{1,0:T(8,128)(2,1)} %u_ref.1), custom_call_target="tpu_custom_call" | custom-call | tf_op jit(solution)/shard_map/pallas_call | solution.py:49
  5.0 16.1 %all-gather = bf16[320,512]{1,0:T(8,128)(2,1)S(1)} all-gather(bf16[80,512]{1,0:T(8,128)(2,1)} %shard_map.55), channel_id=2, replica_groups=mesh['grp'=1,'tok_o'=4,'tok_m'=4,'tok_c'=2] {'tok_o'}, dimensions={0}, use_global_device_ids=true | all-gather | bytes 409600 | tf_op jit(solution)/shard_map/all_gather | solution.py:89
  21.1 0.1 broadcast_in_dim.6
  21.2 18.5 %all_to_all.16 = bf16[4,4,80,512]{3,2,0,1:T(8,128)(2,1)S(1)} all-to-all(bf16[4,4,80,512]{3,2,0,1:T(8,128)(2,1)S(1)} %broadcast_in_dim.6), channel_id=1, replica_groups=mesh['grp'=1,'tok_o'=4,'tok_m'=4,'tok_c'=2] {'tok_m'}, dimensions={1} | all-to-all | bytes 2621440 | tf_op jit(solution)/shard_map/all_to_all | solution.py:84
  39.7 0.1 copy.13
  39.8 0.3 broadcast_in_dim.7
  40.1 5.8 %all_to_all.17 = bf16[4,4,2,80,512]{4,3,1,0,2:T(8,128)(2,1)S(1)} all-to-all(bf16[4,4,2,80,512]{4,3,1,0,2:T(8,128)(2,1)S(1)} %broadcast_in_dim.7), channel_id=1, replica_groups=mesh['grp'=1,'tok_o'=4,'tok_m'=4,'tok_c'=2] {'tok_c'}, dimensions={2} | all-to-all | bytes 5242880 | tf_op jit(solution)/shard_map/all_to_all | solution.py:84
  45.9 0.2 slice.8
  46.1 0.0 slice-start
  46.1 0.2 copy.18
  46.4 0.0 copy-done
  46.5 0.0 slice-start.1
  46.5 1.3 %fusion = f32[512,2048]{1,0:T(8,128)S(1)} fusion(bf16[512,512]{1,0:T(8,128)(2,1)S(1)} %bitcast.11, bf16[2048,512]{1,0:T(8,128)(2,1)S(1)} %copy-done), kind=kOutput, calls=%fused_computation.5 | convolution fusion | flops 1073741824 | bytes 6815744 | tf_op jit(solution)/shard_map/dot_general | solution.py:73
  47.8 0.5 slice-done
  48.3 1.4 %slice-done.1 = s8[4194304]{0:T(1024)(128)(4,1)S(1)} async-done(((s8[8388608]{0:T(1024)(128)(4,1)}), s8[4194304]{0:T(1024)(128)(4,1)S(1)}, s32[]{:S(2)}) %slice-start.1) | async-done | bytes 4194328
  49.7 4.8 %bitcast_reduce_fusion = f32[2048,16]{0,1:T(8,128)S(1)} fusion(f32[512,2048]{1,0:T(8,128)S(1)} %fusion, bf16[2048,512]{1,0:T(8,128)(2,1)S(1)} %bitcast.12, bf16[2048,2048]{1,0:T(8,128)(2,1)S(1)} %bitcast.15), kind=kOutput, calls=%fused_computation | convolution fusion | flops 4297031680 | bytes 14811136 | tf_op jit(solution)/shard_map/dot_general | solution.py:73
  54.5 0.1 multiply_reduce_fusion
  54.6 10.2 %all_to_all.18 = f32[32,1,16]{2,1,0:T(1,128)S(1)} all-to-all(f32[32,1,16]{2,1,0:T(1,128)S(1)} %broadcast_in_dim.8), channel_id=1, replica_groups=mesh['grp'=1,'tok_o'=4,'tok_m'=4,'tok_c'=2] {'tok_o','tok_m','tok_c'}, dimensions={0} | all-to-all | bytes 4096 | tf_op jit(solution)/shard_map/all_to_all | solution.py:78
  64.8 0.1 reduce_sum.29
  64.9 0.7 %broadcast_divide_fusion = f32[2048,16]{0,1:T(8,128)} fusion(f32[2048,16]{0,1:T(8,128)S(1)} %bitcast_reduce_fusion, f32[16]{0:T(128)S(1)} %add_sqrt_fusion), kind=kLoop, calls=%fused_computation.3 | loop fusion | flops 32768 | bytes 262208 | tf_op jit(solution)/shard_map/div | solution.py:106
  (5 shorter events, 0.1 us)
Async XLA Ops:
  0.0 46.4 %copy-start = (bf16[2048,512]{1,0:T(8,128)(2,1)S(1)}, bf16[2048,512]{1,0:T(8,128)(2,1)}, u32[]{:S(2)}) copy-start(bf16[2048,512]{1,0:T(8,128)(2,1)} %param.6) | copy-start | bytes 6291460
  46.1 2.2 %slice-start = ((s8[8388608]{0:T(1024)(128)(4,1)}), s8[4194304]{0:T(1024)(128)(4,1)S(1)}, s32[]{:S(2)}) async-start(s8[8388608]{0:T(1024)(128)(4,1)} %bitcast.14), calls=%async_computation.3 | async-start | bytes 8388608
  46.5 3.2 %slice-start.1 = ((s8[8388608]{0:T(1024)(128)(4,1)}), s8[4194304]{0:T(1024)(128)(4,1)S(1)}, s32[]{:S(2)}) async-start(s8[8388608]{0:T(1024)(128)(4,1)} %bitcast.14), calls=%async_computation.4 | async-start | bytes 8388608

commit v6 on v5

--- a/solution.py
+++ b/solution.py
@@ -84,10 +84,20 @@
     return lax.all_to_all(copies, axis, at, at, tiled=True)
 
 
+def shifted(x, axis, at):
+    k = lax.axis_size(axis)
+    if k > 4:
+        return spread(x, axis, at)
+    me = lax.axis_index(axis)
+    got = [x] + [lax.ppermute(x, axis, [(j, (j + s) % k) for j in range(k)]) for s in range(1, k)]
+    back = jnp.stack(got[::-1] + got[::-1], axis=at)
+    return lax.dynamic_slice_in_dim(back, (k - 1 - me) % k, k, axis=at)
+
+
 def gather_factors(both, rows_v):
     cols = both.shape[1]
-    held = lax.all_gather(both, OUTER, axis=0, tiled=False)
-    held = spread(held, MIDDLE, 1)
+    held = shifted(both, OUTER, 0)
+    held = shifted(held, MIDDLE, 1)
     held = spread(held, CORE, 2)
     return held[:, :, :, :rows_v].reshape(-1, cols), held[:, :, :, rows_v:].reshape(-1, cols)
 

time: 65.9 us -> 65.5 us (level)
  blocking collectives: 50.6 us -> 18.3 us
  waiting for transfers between devices: 0 us -> 19.3 us
  starting transfers between devices: 0 us -> 9.66 us
  local copies, waits for them, and re-layouts: 2.91 us -> 5.69 us
    ppermute x0 -> x6, waiting for transfers between devices: none -> 19.3 us  [shifted(): lax.ppermute(x, axis, [(j, (j + s) % k) for j in range(k)])]
    all_to_all x2 -> x1, blocking collectives: 24.3 us -> 5.84 us  [spread(): return lax.all_to_all(copies, axis, at, at, tiled=True)]
    all_gather x1 -> x0, blocking collectives: 16.1 us -> none  [gather_factors(): held = lax.all_gather(both, OUTER, axis=0, tiled=False)]
    ppermute x0 -> x6, starting transfers between devices: none -> 9.66 us  [shifted(): lax.ppermute(x, axis, [(j, (j + s) % k) for j in range(k)])]
    all_to_all x1, blocking collectives: 10.2 us -> 12.5 us  [total_over(): return lax.all_to_all(copies, axis, 0, 0, tiled=False).sum(axis=0)]
    unnamed x8 -> x22, local copies, waits for them, and re-layouts: 2.16 us -> 3.27 us
    dynamic_slice x0 -> x3, local copies, waits for them, and re-layouts: none -> 0.98 us  [shifted(): return lax.dynamic_slice_in_dim(back, (k - 1 - me) % k, k, axis=at)]
    another operation x0 -> x2, local copies, waits for them, and re-layouts: none -> 0.93 us  [shifted(): back = jnp.stack(got[::-1] + got[::-1], axis=at)]
  transfers between devices with their start and end apart: 0 -> 6, of which waited for: 0 -> 4; matrix products, arithmetic and copies ran while one was open for 0% -> 0% of each run, Pallas kernels for 0% -> 0%
where the time goes in v6:
time: 65.5 us; the launch traced here: 65.3 us
  waiting for transfers between devices  19.3 us (29%)
  blocking collectives  18.3 us (28%)
  starting transfers between devices  9.66 us (15%)
  matrix products  6.12 us (9%)
  local copies, waits for them, and re-layouts  5.69 us (9%)
  Pallas kernels  5.01 us (8%)
  other arithmetic  0.94 us (1%)
    ppermute x6, waiting for transfers between devices, shifted(): lax.ppermute(x, axis, [(j, (j + s) % k) for j in range(k)])  19.3 us
    all_to_all x1, blocking collectives, total_over(): return lax.all_to_all(copies, axis, 0, 0, tiled=False).sum(axis=0)  12.5 us
    ppermute x6, starting transfers between devices, shifted(): lax.ppermute(x, axis, [(j, (j + s) % k) for j in range(k)])  9.66 us
    dot_general x2, matrix products, folder(): return jnp.dot(left, piece, preferred_element_type=jnp.float32)  6.12 us
    all_to_all x1, blocking collectives, spread(): return lax.all_to_all(copies, axis, at, at, tiled=True)  5.84 us
    pallas_call x1, Pallas kernels, pick_columns(): pl.pallas_call(pick_kernel, out_shape=jax.ShapeDtypeStruct((v_bank.shape[...  5.01 us
    unnamed x22, local copies, waits for them, and re-layouts  3.27 us
  transfers between devices with their start and end apart: 6, of which 4 were waited for; matrix products, arithmetic and copies ran while one was open for 0% of the time, Pallas kernels for 0%

profile of v6, /device:TPU:0, one launch (start us, length us, event | category | flops | bytes accessed | tf_op | source)
XLA Modules:
  0.0 65.3 jit_solution(5213521333770548318)
XLA Ops:
  0.0 0.0 copy-start
  0.0 5.0 %shard_map.55 = bf16[80,512]{1,0:T(8,128)(2,1)} custom-call(s32[16]{0:T(128)} %ids_ref.1, bf16[64,65536]{1,0:T(8,128)(2,1)} %v_ref.1, bf16[16,65536]{1,0:T(8,128)(2,1)} %u_ref.1), custom_call_target="tpu_custom_call" | custom-call | tf_op jit(solution)/shard_map/pallas_call | solution.py:49
  5.0 5.1 %collective-permute-start = (bf16[80,512]{1,0:T(8,128)(2,1)}, bf16[80,512]{1,0:T(8,128)(2,1)S(1)}, u32[]{:S(2)}, u32[]{:S(2)}) collective-permute-start(bf16[80,512]{1,0:T(8,128)(2,1)} %shard_map.55), channel_id=1, source_target_pairs={{0,24},{8,0},{16,8},{24,16},{1,25},{9,1},{17,9},{25,17},{2,26},{10... | collective-permute-start | bytes 245768 | tf_op jit(solution)/shard_map/ppermute | solution.py:92
  10.1 0.0 collective-permute-start.2
  10.1 1.0 %collective-permute-start.1 = (bf16[80,512]{1,0:T(8,128)(2,1)}, bf16[80,512]{1,0:T(8,128)(2,1)S(1)}, u32[]{:S(2)}, u32[]{:S(2)}) collective-permute-start(bf16[80,512]{1,0:T(8,128)(2,1)} %shard_map.55), channel_id=1, source_target_pairs={{0,16},{8,24},{16,0},{24,8},{1,17},{9,25},{17,1},{25,9},{2,18},{10... | collective-permute-start | bytes 245768 | tf_op jit(solution)/shard_map/ppermute | solution.py:92
  11.1 2.2 %collective-permute-done = bf16[80,512]{1,0:T(8,128)(2,1)S(1)} collective-permute-done((bf16[80,512]{1,0:T(8,128)(2,1)}, bf16[80,512]{1,0:T(8,128)(2,1)S(1)}, u32[]{:S(2)}, u32[]{:S(2)}) %collective-permute-start) | collective-permute-done | bytes 81952 | tf_op jit(solution)/shard_map/ppermute | solution.py:92
  13.3 5.4 %collective-permute-done.1 = bf16[80,512]{1,0:T(8,128)(2,1)S(1)} collective-permute-done((bf16[80,512]{1,0:T(8,128)(2,1)}, bf16[80,512]{1,0:T(8,128)(2,1)S(1)}, u32[]{:S(2)}, u32[]{:S(2)}) %collective-permute-start.1) | collective-permute-done | bytes 81952 | tf_op jit(solution)/shard_map/ppermute | solution.py:92
  18.7 0.0 collective-permute-done.2
  18.7 0.9 %bitcast_dynamic-update-slice_fusion.8 = bf16[8,80,512]{2,1,0:T(8,128)(2,1)S(1)} fusion(bf16[8,80,512]{2,1,0:T(8,128)(2,1)S(1)} %bitcast_dynamic-update-slice_fusion.10, bf16[80,512]{1,0:T(8,128)(2,1)} %shard_map.55), kind=kLoop, calls=%fused_computation.11 | loop fusion | bytes 163840
  19.6 0.9 %bitcast_dynamic-update-slice_fusion.9 = bf16[8,80,512]{2,1,0:T(8,128)(2,1)S(1)} fusion(bf16[8,80,512]{2,1,0:T(8,128)(2,1)S(1)} %bitcast_dynamic-update-slice_fusion.11, bf16[80,512]{1,0:T(8,128)(2,1)} %shard_map.55), kind=kLoop, calls=%fused_computation.12 | loop fusion | bytes 163840 | tf_op jit(solution)/shard_map/stack | solution.py:93
  20.5 0.7 %constant_dynamic-slice_fusion.1 = bf16[4,80,512]{2,1,0:T(8,128)(2,1)} fusion(bf16[8,80,512]{2,1,0:T(8,128)(2,1)S(1)} %bitcast_dynamic-update-slice_fusion.9, s32[]{:T(128)S(6)} %select_n.18), kind=kLoop, calls=%fused_computation.22 | loop fusion | bytes 655364 | tf_op jit(solution)/shard_map/dynamic_slice | solution.py:94
  21.3 2.4 %collective-permute-start.3 = (bf16[4,80,512]{2,1,0:T(8,128)(2,1)}, bf16[4,80,512]{2,1,0:T(8,128)(2,1)S(1)}, u32[]{:S(2)}, u32[]{:S(2)}) collective-permute-start(bf16[4,80,512]{2,1,0:T(8,128)(2,1)} %constant_dynamic-slice_fusion.1), channel_id=1, source_target_pairs={{0,6},{2,0},{4,2},{6,4},{1,7},{3,1},{5,3},{7,5},{8,14},{10,8},{12,... | collective-permute-start | bytes 983048 | tf_op jit(solution)/shard_map/ppermute | solution.py:92
  23.7 0.5 collective-permute-start.4
  24.2 0.6 collective-permute-start.5
  24.8 6.3 %collective-permute-done.3 = bf16[4,80,512]{2,1,0:T(8,128)(2,1)S(1)} collective-permute-done((bf16[4,80,512]{2,1,0:T(8,128)(2,1)}, bf16[4,80,512]{2,1,0:T(8,128)(2,1)S(1)}, u32[]{:S(2)}, u32[]{:S(2)}) %collective-permute-start.3) | collective-permute-done | bytes 327712 | tf_op jit(solution)/shard_map/ppermute | solution.py:92
  31.1 5.5 %collective-permute-done.4 = bf16[4,80,512]{2,1,0:T(8,128)(2,1)S(1)} collective-permute-done((bf16[4,80,512]{2,1,0:T(8,128)(2,1)}, bf16[4,80,512]{2,1,0:T(8,128)(2,1)S(1)}, u32[]{:S(2)}, u32[]{:S(2)}) %collective-permute-start.4) | collective-permute-done | bytes 327712 | tf_op jit(solution)/shard_map/ppermute | solution.py:92
  36.6 0.0 collective-permute-done.5
  36.9 0.1 constant_dynamic-slice_fusion
  37.0 0.1 copy.14
  37.1 0.3 broadcast_in_dim.4
  37.4 5.8 %all_to_all.11 = bf16[4,4,2,80,512]{4,3,1,0,2:T(8,128)(2,1)S(1)} all-to-all(bf16[4,4,2,80,512]{4,3,1,0,2:T(8,128)(2,1)S(1)} %broadcast_in_dim.4), channel_id=1, replica_groups=mesh['grp'=1,'tok_o'=4,'tok_m'=4,'tok_c'=2] {'tok_c'}, dimensions={2} | all-to-all | bytes 5242880 | tf_op jit(solution)/shard_map/all_to_all | solution.py:84
  43.3 0.2 slice.8
  43.4 0.0 slice-start
  43.5 0.2 copy.19
  43.8 0.0 copy-done
  43.8 0.0 slice-start.1
  43.8 1.3 %fusion = f32[512,2048]{1,0:T(8,128)S(1)} fusion(bf16[512,512]{1,0:T(8,128)(2,1)S(1)} %bitcast.34, bf16[2048,512]{1,0:T(8,128)(2,1)S(1)} %copy-done), kind=kOutput, calls=%fused_computation.23 | convolution fusion | flops 1073741824 | bytes 6815744 | tf_op jit(solution)/shard_map/dot_general | solution.py:73
  45.1 0.5 slice-done
  45.6 1.4 %slice-done.1 = s8[4194304]{0:T(1024)(128)(4,1)S(1)} async-done(((s8[8388608]{0:T(1024)(128)(4,1)}), s8[4194304]{0:T(1024)(128)(4,1)S(1)}, s32[]{:S(2)}) %slice-start.1) | async-done | bytes 4194328
  47.0 4.8 %bitcast_reduce_fusion = f32[2048,16]{0,1:T(8,128)S(1)} fusion(f32[512,2048]{1,0:T(8,128)S(1)} %fusion, bf16[2048,512]{1,0:T(8,128)(2,1)S(1)} %bitcast.35, bf16[2048,2048]{1,0:T(8,128)(2,1)S(1)} %bitcast.37), kind=kOutput, calls=%fused_computation | convolution fusion | flops 4297031680 | bytes 14811136 | tf_op jit(solution)/shard_map/dot_general | solution.py:73
  51.8 0.1 multiply_reduce_fusion
  52.0 12.5 %all_to_all.12 = f32[32,1,16]{2,1,0:T(1,128)S(1)} all-to-all(f32[32,1,16]{2,1,0:T(1,128)S(1)} %broadcast_in_dim.5), channel_id=1, replica_groups=mesh['grp'=1,'tok_o'=4,'tok_m'=4,'tok_c'=2] {'tok_o','tok_m','tok_c'}, dimensions={0} | all-to-all | bytes 4096 | tf_op jit(solution)/shard_map/all_to_all | solution.py:78
  64.5 0.1 reduce_sum.29
  64.5 0.7 %broadcast_divide_fusion = f32[2048,16]{0,1:T(8,128)} fusion(f32[2048,16]{0,1:T(8,128)S(1)} %bitcast_reduce_fusion, f32[16]{0:T(128)S(1)} %add_sqrt_fusion), kind=kLoop, calls=%fused_computation.19 | loop fusion | flops 32768 | bytes 262208 | tf_op jit(solution)/shard_map/div | solution.py:116
  (19 shorter events, 0.3 us)
Async XLA Ops:
  0.0 43.8 %copy-start = (bf16[2048,512]{1,0:T(8,128)(2,1)S(1)}, bf16[2048,512]{1,0:T(8,128)(2,1)}, u32[]{:S(2)}) copy-start(bf16[2048,512]{1,0:T(8,128)(2,1)} %param.6) | copy-start | bytes 6291460
  5.0 8.3 %collective-permute-start = (bf16[80,512]{1,0:T(8,128)(2,1)}, bf16[80,512]{1,0:T(8,128)(2,1)S(1)}, u32[]{:S(2)}, u32[]{:S(2)}) collective-permute-start(bf16[80,512]{1,0:T(8,128)(2,1)} %shard_map.55), channel_id=1, source_target_pairs={{0,24},{8,0},{16,8},{24,16},{1,25},{9,1},{17,9},{25,17},{2,26},{10... | collective-permute-start | bytes 245768 | tf_op jit(solution)/shard_map/ppermute | solution.py:92
  10.1 8.6 %collective-permute-start.2 = (bf16[80,512]{1,0:T(8,128)(2,1)}, bf16[80,512]{1,0:T(8,128)(2,1)S(1)}, u32[]{:S(2)}, u32[]{:S(2)}) collective-permute-start(bf16[80,512]{1,0:T(8,128)(2,1)} %shard_map.55), channel_id=1, source_target_pairs={{0,8},{8,16},{16,24},{24,0},{1,9},{9,17},{17,25},{25,1},{2,10},{10... | collective-permute-start | bytes 245768 | tf_op jit(solution)/shard_map/ppermute | solution.py:92
  10.1 8.5 %collective-permute-start.1 = (bf16[80,512]{1,0:T(8,128)(2,1)}, bf16[80,512]{1,0:T(8,128)(2,1)S(1)}, u32[]{:S(2)}, u32[]{:S(2)}) collective-permute-start(bf16[80,512]{1,0:T(8,128)(2,1)} %shard_map.55), channel_id=1, source_target_pairs={{0,16},{8,24},{16,0},{24,8},{1,17},{9,25},{17,1},{25,9},{2,18},{10... | collective-permute-start | bytes 245768 | tf_op jit(solution)/shard_map/ppermute | solution.py:92
  21.3 9.8 %collective-permute-start.3 = (bf16[4,80,512]{2,1,0:T(8,128)(2,1)}, bf16[4,80,512]{2,1,0:T(8,128)(2,1)S(1)}, u32[]{:S(2)}, u32[]{:S(2)}) collective-permute-start(bf16[4,80,512]{2,1,0:T(8,128)(2,1)} %constant_dynamic-slice_fusion.1), channel_id=1, source_target_pairs={{0,6},{2,0},{4,2},{6,4},{1,7},{3,1},{5,3},{7,5},{8,14},{10,8},{12,... | collective-permute-start | bytes 983048 | tf_op jit(solution)/shard_map/ppermute | solution.py:92
  23.7 12.9 %collective-permute-start.4 = (bf16[4,80,512]{2,1,0:T(8,128)(2,1)}, bf16[4,80,512]{2,1,0:T(8,128)(2,1)S(1)}, u32[]{:S(2)}, u32[]{:S(2)}) collective-permute-start(bf16[4,80,512]{2,1,0:T(8,128)(2,1)} %constant_dynamic-slice_fusion.1), channel_id=1, source_target_pairs={{0,4},{2,6},{4,0},{6,2},{1,5},{3,7},{5,1},{7,3},{8,12},{10,14},{12... | collective-permute-start | bytes 983048 | tf_op jit(solution)/shard_map/ppermute | solution.py:92
  24.2 12.4 %collective-permute-start.5 = (bf16[4,80,512]{2,1,0:T(8,128)(2,1)}, bf16[4,80,512]{2,1,0:T(8,128)(2,1)S(1)}, u32[]{:S(2)}, u32[]{:S(2)}) collective-permute-start(bf16[4,80,512]{2,1,0:T(8,128)(2,1)} %constant_dynamic-slice_fusion.1), channel_id=1, source_target_pairs={{0,2},{2,4},{4,6},{6,0},{1,3},{3,5},{5,7},{7,1},{8,10},{10,12},{12... | collective-permute-start | bytes 983048 | tf_op jit(solution)/shard_map/ppermute | solution.py:92
  43.4 2.2 %slice-start = ((s8[8388608]{0:T(1024)(128)(4,1)}), s8[4194304]{0:T(1024)(128)(4,1)S(1)}, s32[]{:S(2)}) async-start(s8[8388608]{0:T(1024)(128)(4,1)} %bitcast.36), calls=%async_computation.2 | async-start | bytes 8388608
  43.8 3.2 %slice-start.1 = ((s8[8388608]{0:T(1024)(128)(4,1)}), s8[4194304]{0:T(1024)(128)(4,1)S(1)}, s32[]{:S(2)}) async-start(s8[8388608]{0:T(1024)(128)(4,1)} %bitcast.36), calls=%async_computation.3 | async-start | bytes 8388608

commit v7 on v6

--- a/solution.py
+++ b/solution.py
@@ -34,9 +34,7 @@
                 x = buf[q].astype(jnp.float32)
                 off = (ids_ref[q] % PER_TILE) * RANK
                 shift = (RANK * j - off + LANES) % LANES
-                moved = x
-                for s in range(RANK, LANES, RANK):
-                    moved = jnp.where(shift == s, pltpu.roll(x, s, 1), moved)
+                moved = pltpu.roll(x, shift, 1)
                 keep = (lane >= RANK * j) & (lane < RANK * (j + 1))
                 acc = jnp.where(keep, moved, acc)
             out[base:base + rows, g * LANES:(g + 1) * LANES] = acc.astype(out.dtype)

time: 65.5 us -> 65.4 us (level)
  no operation moved by 1% of the time
where the time goes in v7:
time: 65.4 us; the launch traced here: 65.1 us
  waiting for transfers between devices  19.3 us (30%)
  blocking collectives  18.3 us (28%)
  starting transfers between devices  9.66 us (15%)
  matrix products  6.12 us (9%)
  local copies, waits for them, and re-layouts  5.7 us (9%)
  Pallas kernels  4.81 us (7%)
  other arithmetic  0.94 us (1%)
    ppermute x6, waiting for transfers between devices, shifted(): lax.ppermute(x, axis, [(j, (j + s) % k) for j in range(k)])  19.3 us
    all_to_all x1, blocking collectives, total_over(): return lax.all_to_all(copies, axis, 0, 0, tiled=False).sum(axis=0)  12.5 us
    ppermute x6, starting transfers between devices, shifted(): lax.ppermute(x, axis, [(j, (j + s) % k) for j in range(k)])  9.66 us
    dot_general x2, matrix products, folder(): return jnp.dot(left, piece, preferred_element_type=jnp.float32)  6.12 us
    all_to_all x1, blocking collectives, spread(): return lax.all_to_all(copies, axis, at, at, tiled=True)  5.84 us
    pallas_call x1, Pallas kernels, pick_columns(): pl.pallas_call(pick_kernel, out_shape=jax.ShapeDtypeStruct((v_bank.shape[...  4.81 us
    unnamed x22, local copies, waits for them, and re-layouts  3.27 us
  transfers between devices with their start and end apart: 6, of which 4 were waited for; matrix products, arithmetic and copies ran while one was open for 0% of the time, Pallas kernels for 0%

profile of v7, /device:TPU:0, one launch (start us, length us, event | category | flops | bytes accessed | tf_op | source)
XLA Modules:
  0.0 65.1 jit_solution(15039483143214449214)
XLA Ops:
  0.0 0.0 copy-start
  0.0 4.8 %shard_map.55 = bf16[80,512]{1,0:T(8,128)(2,1)} custom-call(s32[16]{0:T(128)} %ids_ref.1, bf16[64,65536]{1,0:T(8,128)(2,1)} %v_ref.1, bf16[16,65536]{1,0:T(8,128)(2,1)} %u_ref.1), custom_call_target="tpu_custom_call" | custom-call | tf_op jit(solution)/shard_map/pallas_call | solution.py:47
  4.8 5.1 %collective-permute-start = (bf16[80,512]{1,0:T(8,128)(2,1)}, bf16[80,512]{1,0:T(8,128)(2,1)S(1)}, u32[]{:S(2)}, u32[]{:S(2)}) collective-permute-start(bf16[80,512]{1,0:T(8,128)(2,1)} %shard_map.55), channel_id=1, source_target_pairs={{0,24},{8,0},{16,8},{24,16},{1,25},{9,1},{17,9},{25,17},{2,26},{10... | collective-permute-start | bytes 245768 | tf_op jit(solution)/shard_map/ppermute | solution.py:90
  9.9 0.0 collective-permute-start.2
  9.9 1.0 %collective-permute-start.1 = (bf16[80,512]{1,0:T(8,128)(2,1)}, bf16[80,512]{1,0:T(8,128)(2,1)S(1)}, u32[]{:S(2)}, u32[]{:S(2)}) collective-permute-start(bf16[80,512]{1,0:T(8,128)(2,1)} %shard_map.55), channel_id=1, source_target_pairs={{0,16},{8,24},{16,0},{24,8},{1,17},{9,25},{17,1},{25,9},{2,18},{10... | collective-permute-start | bytes 245768 | tf_op jit(solution)/shard_map/ppermute | solution.py:90
  10.9 2.2 %collective-permute-done = bf16[80,512]{1,0:T(8,128)(2,1)S(1)} collective-permute-done((bf16[80,512]{1,0:T(8,128)(2,1)}, bf16[80,512]{1,0:T(8,128)(2,1)S(1)}, u32[]{:S(2)}, u32[]{:S(2)}) %collective-permute-start) | collective-permute-done | bytes 81952 | tf_op jit(solution)/shard_map/ppermute | solution.py:90
  13.1 5.4 %collective-permute-done.1 = bf16[80,512]{1,0:T(8,128)(2,1)S(1)} collective-permute-done((bf16[80,512]{1,0:T(8,128)(2,1)}, bf16[80,512]{1,0:T(8,128)(2,1)S(1)}, u32[]{:S(2)}, u32[]{:S(2)}) %collective-permute-start.1) | collective-permute-done | bytes 81952 | tf_op jit(solution)/shard_map/ppermute | solution.py:90
  18.5 0.0 collective-permute-done.2
  18.5 0.9 %bitcast_dynamic-update-slice_fusion.8 = bf16[8,80,512]{2,1,0:T(8,128)(2,1)S(1)} fusion(bf16[8,80,512]{2,1,0:T(8,128)(2,1)S(1)} %bitcast_dynamic-update-slice_fusion.10, bf16[80,512]{1,0:T(8,128)(2,1)} %shard_map.55), kind=kLoop, calls=%fused_computation.11 | loop fusion | bytes 163840
  19.4 0.9 %bitcast_dynamic-update-slice_fusion.9 = bf16[8,80,512]{2,1,0:T(8,128)(2,1)S(1)} fusion(bf16[8,80,512]{2,1,0:T(8,128)(2,1)S(1)} %bitcast_dynamic-update-slice_fusion.11, bf16[80,512]{1,0:T(8,128)(2,1)} %shard_map.55), kind=kLoop, calls=%fused_computation.12 | loop fusion | bytes 163840 | tf_op jit(solution)/shard_map/stack | solution.py:91
  20.3 0.7 %constant_dynamic-slice_fusion.1 = bf16[4,80,512]{2,1,0:T(8,128)(2,1)} fusion(bf16[8,80,512]{2,1,0:T(8,128)(2,1)S(1)} %bitcast_dynamic-update-slice_fusion.9, s32[]{:T(128)S(6)} %select_n.18), kind=kLoop, calls=%fused_computation.22 | loop fusion | bytes 655364 | tf_op jit(solution)/shard_map/dynamic_slice | solution.py:92
  21.1 2.4 %collective-permute-start.3 = (bf16[4,80,512]{2,1,0:T(8,128)(2,1)}, bf16[4,80,512]{2,1,0:T(8,128)(2,1)S(1)}, u32[]{:S(2)}, u32[]{:S(2)}) collective-permute-start(bf16[4,80,512]{2,1,0:T(8,128)(2,1)} %constant_dynamic-slice_fusion.1), channel_id=1, source_target_pairs={{0,6},{2,0},{4,2},{6,4},{1,7},{3,1},{5,3},{7,5},{8,14},{10,8},{12,... | collective-permute-start | bytes 983048 | tf_op jit(solution)/shard_map/ppermute | solution.py:90
  23.5 0.5 collective-permute-start.4
  24.0 0.6 collective-permute-start.5
  24.6 6.3 %collective-permute-done.3 = bf16[4,80,512]{2,1,0:T(8,128)(2,1)S(1)} collective-permute-done((bf16[4,80,512]{2,1,0:T(8,128)(2,1)}, bf16[4,80,512]{2,1,0:T(8,128)(2,1)S(1)}, u32[]{:S(2)}, u32[]{:S(2)}) %collective-permute-start.3) | collective-permute-done | bytes 327712 | tf_op jit(solution)/shard_map/ppermute | solution.py:90
  30.9 5.5 %collective-permute-done.4 = bf16[4,80,512]{2,1,0:T(8,128)(2,1)S(1)} collective-permute-done((bf16[4,80,512]{2,1,0:T(8,128)(2,1)}, bf16[4,80,512]{2,1,0:T(8,128)(2,1)S(1)}, u32[]{:S(2)}, u32[]{:S(2)}) %collective-permute-start.4) | collective-permute-done | bytes 327712 | tf_op jit(solution)/shard_map/ppermute | solution.py:90
  36.4 0.0 collective-permute-done.5
  36.7 0.1 constant_dynamic-slice_fusion
  36.8 0.1 copy.14
  36.9 0.3 broadcast_in_dim.4
  37.2 5.8 %all_to_all.11 = bf16[4,4,2,80,512]{4,3,1,0,2:T(8,128)(2,1)S(1)} all-to-all(bf16[4,4,2,80,512]{4,3,1,0,2:T(8,128)(2,1)S(1)} %broadcast_in_dim.4), channel_id=1, replica_groups=mesh['grp'=1,'tok_o'=4,'tok_m'=4,'tok_c'=2] {'tok_c'}, dimensions={2} | all-to-all | bytes 5242880 | tf_op jit(solution)/shard_map/all_to_all | solution.py:82
  43.1 0.2 slice.8
  43.2 0.0 slice-start
  43.3 0.2 copy.19
  43.6 0.0 copy-done
  43.6 0.0 slice-start.1
  43.6 1.3 %fusion = f32[512,2048]{1,0:T(8,128)S(1)} fusion(bf16[512,512]{1,0:T(8,128)(2,1)S(1)} %bitcast.34, bf16[2048,512]{1,0:T(8,128)(2,1)S(1)} %copy-done), kind=kOutput, calls=%fused_computation.23 | convolution fusion | flops 1073741824 | bytes 6815744 | tf_op jit(solution)/shard_map/dot_general | solution.py:71
  44.9 0.5 slice-done
  45.4 1.4 %slice-done.1 = s8[4194304]{0:T(1024)(128)(4,1)S(1)} async-done(((s8[8388608]{0:T(1024)(128)(4,1)}), s8[4194304]{0:T(1024)(128)(4,1)S(1)}, s32[]{:S(2)}) %slice-start.1) | async-done | bytes 4194328
  46.8 4.8 %bitcast_reduce_fusion = f32[2048,16]{0,1:T(8,128)S(1)} fusion(f32[512,2048]{1,0:T(8,128)S(1)} %fusion, bf16[2048,512]{1,0:T(8,128)(2,1)S(1)} %bitcast.35, bf16[2048,2048]{1,0:T(8,128)(2,1)S(1)} %bitcast.37), kind=kOutput, calls=%fused_computation | convolution fusion | flops 4297031680 | bytes 14811136 | tf_op jit(solution)/shard_map/dot_general | solution.py:71
  51.6 0.1 multiply_reduce_fusion
  51.8 12.5 %all_to_all.12 = f32[32,1,16]{2,1,0:T(1,128)S(1)} all-to-all(f32[32,1,16]{2,1,0:T(1,128)S(1)} %broadcast_in_dim.5), channel_id=1, replica_groups=mesh['grp'=1,'tok_o'=4,'tok_m'=4,'tok_c'=2] {'tok_o','tok_m','tok_c'}, dimensions={0} | all-to-all | bytes 4096 | tf_op jit(solution)/shard_map/all_to_all | solution.py:76
  64.3 0.1 reduce_sum.29
  64.3 0.7 %broadcast_divide_fusion = f32[2048,16]{0,1:T(8,128)} fusion(f32[2048,16]{0,1:T(8,128)S(1)} %bitcast_reduce_fusion, f32[16]{0:T(128)S(1)} %add_sqrt_fusion), kind=kLoop, calls=%fused_computation.19 | loop fusion | flops 32768 | bytes 262208 | tf_op jit(solution)/shard_map/div | solution.py:114
  (19 shorter events, 0.3 us)
Async XLA Ops:
  0.0 43.6 %copy-start = (bf16[2048,512]{1,0:T(8,128)(2,1)S(1)}, bf16[2048,512]{1,0:T(8,128)(2,1)}, u32[]{:S(2)}) copy-start(bf16[2048,512]{1,0:T(8,128)(2,1)} %param.6) | copy-start | bytes 6291460
  4.8 8.3 %collective-permute-start = (bf16[80,512]{1,0:T(8,128)(2,1)}, bf16[80,512]{1,0:T(8,128)(2,1)S(1)}, u32[]{:S(2)}, u32[]{:S(2)}) collective-permute-start(bf16[80,512]{1,0:T(8,128)(2,1)} %shard_map.55), channel_id=1, source_target_pairs={{0,24},{8,0},{16,8},{24,16},{1,25},{9,1},{17,9},{25,17},{2,26},{10... | collective-permute-start | bytes 245768 | tf_op jit(solution)/shard_map/ppermute | solution.py:90
  9.9 8.6 %collective-permute-start.2 = (bf16[80,512]{1,0:T(8,128)(2,1)}, bf16[80,512]{1,0:T(8,128)(2,1)S(1)}, u32[]{:S(2)}, u32[]{:S(2)}) collective-permute-start(bf16[80,512]{1,0:T(8,128)(2,1)} %shard_map.55), channel_id=1, source_target_pairs={{0,8},{8,16},{16,24},{24,0},{1,9},{9,17},{17,25},{25,1},{2,10},{10... | collective-permute-start | bytes 245768 | tf_op jit(solution)/shard_map/ppermute | solution.py:90
  9.9 8.5 %collective-permute-start.1 = (bf16[80,512]{1,0:T(8,128)(2,1)}, bf16[80,512]{1,0:T(8,128)(2,1)S(1)}, u32[]{:S(2)}, u32[]{:S(2)}) collective-permute-start(bf16[80,512]{1,0:T(8,128)(2,1)} %shard_map.55), channel_id=1, source_target_pairs={{0,16},{8,24},{16,0},{24,8},{1,17},{9,25},{17,1},{25,9},{2,18},{10... | collective-permute-start | bytes 245768 | tf_op jit(solution)/shard_map/ppermute | solution.py:90
  21.1 9.8 %collective-permute-start.3 = (bf16[4,80,512]{2,1,0:T(8,128)(2,1)}, bf16[4,80,512]{2,1,0:T(8,128)(2,1)S(1)}, u32[]{:S(2)}, u32[]{:S(2)}) collective-permute-start(bf16[4,80,512]{2,1,0:T(8,128)(2,1)} %constant_dynamic-slice_fusion.1), channel_id=1, source_target_pairs={{0,6},{2,0},{4,2},{6,4},{1,7},{3,1},{5,3},{7,5},{8,14},{10,8},{12,... | collective-permute-start | bytes 983048 | tf_op jit(solution)/shard_map/ppermute | solution.py:90
  23.5 12.9 %collective-permute-start.4 = (bf16[4,80,512]{2,1,0:T(8,128)(2,1)}, bf16[4,80,512]{2,1,0:T(8,128)(2,1)S(1)}, u32[]{:S(2)}, u32[]{:S(2)}) collective-permute-start(bf16[4,80,512]{2,1,0:T(8,128)(2,1)} %constant_dynamic-slice_fusion.1), channel_id=1, source_target_pairs={{0,4},{2,6},{4,0},{6,2},{1,5},{3,7},{5,1},{7,3},{8,12},{10,14},{12... | collective-permute-start | bytes 983048 | tf_op jit(solution)/shard_map/ppermute | solution.py:90
  24.0 12.4 %collective-permute-start.5 = (bf16[4,80,512]{2,1,0:T(8,128)(2,1)}, bf16[4,80,512]{2,1,0:T(8,128)(2,1)S(1)}, u32[]{:S(2)}, u32[]{:S(2)}) collective-permute-start(bf16[4,80,512]{2,1,0:T(8,128)(2,1)} %constant_dynamic-slice_fusion.1), channel_id=1, source_target_pairs={{0,2},{2,4},{4,6},{6,0},{1,3},{3,5},{5,7},{7,1},{8,10},{10,12},{12... | collective-permute-start | bytes 983048 | tf_op jit(solution)/shard_map/ppermute | solution.py:90
  43.2 2.2 %slice-start = ((s8[8388608]{0:T(1024)(128)(4,1)}), s8[4194304]{0:T(1024)(128)(4,1)S(1)}, s32[]{:S(2)}) async-start(s8[8388608]{0:T(1024)(128)(4,1)} %bitcast.36), calls=%async_computation.2 | async-start | bytes 8388608
  43.6 3.2 %slice-start.1 = ((s8[8388608]{0:T(1024)(128)(4,1)}), s8[4194304]{0:T(1024)(128)(4,1)S(1)}, s32[]{:S(2)}) async-start(s8[8388608]{0:T(1024)(128)(4,1)} %bitcast.36), calls=%async_computation.3 | async-start | bytes 8388608

commit v8 on v7

--- a/solution.py
+++ b/solution.py
@@ -92,6 +92,11 @@
     return lax.dynamic_slice_in_dim(back, (k - 1 - me) % k, k, axis=at)
 
 
+def ring_step(x, axis):
+    k = lax.axis_size(axis)
+    return lax.ppermute(x, axis, [(j, (j + 1) % k) for j in range(k)])
+
+
 def gather_factors(both, rows_v):
     cols = both.shape[1]
     held = shifted(both, OUTER, 0)
@@ -104,12 +109,15 @@
     tok_rows = activations.shape[0]
     queries = query_ids.shape[0]
     n = lax.axis_size(OUTER) * lax.axis_size(MIDDLE) * lax.axis_size(CORE)
+    warm = [ring_step(activations[:8, :128], axis) for axis in (OUTER, MIDDLE)]
     both = pick_columns(v_bank, u_bank, query_ids)
+    both, warm = lax.optimization_barrier((both, warm))
     v_full, u_full = gather_factors(both, v_bank.shape[0])
     proj_in = folder(activations, v_full)
     proj_out = folder(out_grads, u_full)
     scores = (proj_in * proj_out).reshape(tok_rows, queries, RANK).sum(axis=2)
     total = total_over(jnp.sum(scores * scores, axis=0), TOK, n)
+    total = total + 0.0 * sum(w[0, 0].astype(jnp.float32) for w in warm)
     scale = jnp.sqrt(total / (tok_rows * n) + 1e-06)
     return scores / scale[None, :]
 

time: 65.4 us -> 68.8 us (1.052)
  blocking collectives: 18.3 us -> 5.84 us
  starting transfers between devices: 9.66 us -> 18.9 us
  waiting for transfers between devices: 19.3 us -> 22.2 us
  local copies, waits for them, and re-layouts: 5.7 us -> 8.25 us
  between operations: 0.21 us -> 1.49 us
    all_to_all x1 -> x0, blocking collectives: 12.5 us -> none  [total_over(): return lax.all_to_all(copies, axis, 0, 0, tiled=False).sum(axis=0)]
    all_to_all x0 -> x1, starting transfers between devices: none -> 6.2 us  [total_over(): return lax.all_to_all(copies, axis, 0, 0, tiled=False).sum(axis=0)]
    all_to_all x0 -> x1, waiting for transfers between devices: none -> 4.72 us  [total_over(): return lax.all_to_all(copies, axis, 0, 0, tiled=False).sum(axis=0)]
    ppermute x0 -> x2, starting transfers between devices: none -> 4.51 us  [ring_step(): return lax.ppermute(x, axis, [(j, (j + 1) % k) for j in range(k)])]
    slice x0 -> x3, local copies, waits for them, and re-layouts: none -> 1.93 us  [the longest x2 1.1 us: on_device(): total = total + 0.0 * sum((w[0, 0].astype(jnp.float32) for w in warm))]
    ppermute x6, waiting for transfers between devices: 19.3 us -> 17.5 us  [shifted(): lax.ppermute(x, axis, [(j, (j + s) % k) for j in range(k)])]
    ppermute x6, starting transfers between devices: 9.66 us -> 8.21 us  [shifted(): lax.ppermute(x, axis, [(j, (j + s) % k) for j in range(k)])]
  transfers between devices with their start and end apart: 6 -> 9, of which waited for: 4 -> 5; matrix products, arithmetic and copies ran while one was open for 0% -> 2% of each run, Pallas kernels for 0% -> 7%
where the time goes in v8:
time: 68.8 us; the launch traced here: 68.4 us
  waiting for transfers between devices  22.2 us (32%)
  starting transfers between devices  18.9 us (27%)
  local copies, waits for them, and re-layouts  8.25 us (12%)
  matrix products  6.12 us (9%)
  blocking collectives  5.84 us (8%)
  Pallas kernels  4.68 us (7%)
  between operations  1.49 us (2%)
  other arithmetic  0.94 us (1%)
    ppermute x6, waiting for transfers between devices, shifted(): lax.ppermute(x, axis, [(j, (j + s) % k) for j in range(k)])  17.5 us
    ppermute x6, starting transfers between devices, shifted(): lax.ppermute(x, axis, [(j, (j + s) % k) for j in range(k)])  8.21 us
    all_to_all x1, starting transfers between devices, total_over(): return lax.all_to_all(copies, axis, 0, 0, tiled=False).sum(axis=0)  6.2 us
    dot_general x2, matrix products, folder(): return jnp.dot(left, piece, preferred_element_type=jnp.float32)  6.12 us
    all_to_all x1, blocking collectives, spread(): return lax.all_to_all(copies, axis, at, at, tiled=True)  5.84 us
    all_to_all x1, waiting for transfers between devices, total_over(): return lax.all_to_all(copies, axis, 0, 0, tiled=False).sum(axis=0)  4.72 us
    pallas_call x1, Pallas kernels, pick_columns(): pl.pallas_call(pick_kernel, out_shape=jax.ShapeDtypeStruct((v_bank.shape[...  4.68 us
    ppermute x2, starting transfers between devices, ring_step(): return lax.ppermute(x, axis, [(j, (j + 1) % k) for j in range(k)])  4.51 us
  transfers between devices with their start and end apart: 9, of which 5 were waited for; matrix products, arithmetic and copies ran while one was open for 2% of the time, Pallas kernels for 7%

profile of v8, /device:TPU:0, one launch (start us, length us, event | category | flops | bytes accessed | tf_op | source)
XLA Modules:
  0.0 68.4 jit_solution(18272561703458485594)
XLA Ops:
  0.0 0.0 copy-start
  0.0 0.8 %slice.16 = bf16[8,128]{1,0:T(8,128)(2,1)S(1)} slice(bf16[2048,2048]{1,0:T(8,128)(2,1)} %param.5), slice={[0:8], [0:128]} | slice | bytes 4096 | tf_op jit(solution)/shard_map/slice | solution.py:112
  0.8 2.9 %collective-permute-start.1 = (bf16[8,128]{1,0:T(8,128)(2,1)S(1)}, bf16[8,128]{1,0:T(8,128)(2,1)S(1)}, u32[]{:S(2)}, u32[]{:S(2)}) collective-permute-start(bf16[8,128]{1,0:T(8,128)(2,1)S(1)} %slice.16), channel_id=1, source_target_pairs={{0,2},{2,4},{4,6},{6,0},{1,3},{3,5},{5,7},{7,1},{8,10},{10,12},{12... | collective-permute-start | bytes 6152 | tf_op jit(solution)/shard_map/ppermute | solution.py:97
  3.8 1.6 %collective-permute-start = (bf16[8,128]{1,0:T(8,128)(2,1)S(1)}, bf16[8,128]{1,0:T(8,128)(2,1)S(1)}, u32[]{:S(2)}, u32[]{:S(2)}) collective-permute-start(bf16[8,128]{1,0:T(8,128)(2,1)S(1)} %slice.16), channel_id=1, source_target_pairs={{0,8},{8,16},{16,24},{24,0},{1,9},{9,17},{17,25},{25,1},{2,10},{10... | collective-permute-start | bytes 6152 | tf_op jit(solution)/shard_map/ppermute | solution.py:97
  5.4 4.7 %shard_map.55 = bf16[80,512]{1,0:T(8,128)(2,1)} custom-call(s32[16]{0:T(128)} %ids_ref.1, bf16[64,65536]{1,0:T(8,128)(2,1)} %v_ref.1, bf16[16,65536]{1,0:T(8,128)(2,1)} %u_ref.1), custom_call_target="tpu_custom_call" | custom-call | tf_op jit(solution)/shard_map/pallas_call | solution.py:47
  10.0 0.0 collective-permute-done.1
  10.1 0.0 collective-permute-done
  10.1 2.3 %collective-permute-start.2 = (bf16[80,512]{1,0:T(8,128)(2,1)}, bf16[80,512]{1,0:T(8,128)(2,1)S(1)}, u32[]{:S(2)}, u32[]{:S(2)}) collective-permute-start(bf16[80,512]{1,0:T(8,128)(2,1)} %shard_map.55), channel_id=1, source_target_pairs={{0,24},{8,0},{16,8},{24,16},{1,25},{9,1},{17,9},{25,17},{2,26},{10... | collective-permute-start | bytes 245768 | tf_op jit(solution)/shard_map/ppermute | solution.py:90
  12.4 0.0 collective-permute-start.4
  12.4 2.4 %collective-permute-start.3 = (bf16[80,512]{1,0:T(8,128)(2,1)}, bf16[80,512]{1,0:T(8,128)(2,1)S(1)}, u32[]{:S(2)}, u32[]{:S(2)}) collective-permute-start(bf16[80,512]{1,0:T(8,128)(2,1)} %shard_map.55), channel_id=1, source_target_pairs={{0,16},{8,24},{16,0},{24,8},{1,17},{9,25},{17,1},{25,9},{2,18},{10... | collective-permute-start | bytes 245768 | tf_op jit(solution)/shard_map/ppermute | solution.py:90
  14.7 0.9 %collective-permute-done.2 = bf16[80,512]{1,0:T(8,128)(2,1)S(1)} collective-permute-done((bf16[80,512]{1,0:T(8,128)(2,1)}, bf16[80,512]{1,0:T(8,128)(2,1)S(1)}, u32[]{:S(2)}, u32[]{:S(2)}) %collective-permute-start.2) | collective-permute-done | bytes 81952 | tf_op jit(solution)/shard_map/ppermute | solution.py:90
  15.6 5.4 %collective-permute-done.3 = bf16[80,512]{1,0:T(8,128)(2,1)S(1)} collective-permute-done((bf16[80,512]{1,0:T(8,128)(2,1)}, bf16[80,512]{1,0:T(8,128)(2,1)S(1)}, u32[]{:S(2)}, u32[]{:S(2)}) %collective-permute-start.3) | collective-permute-done | bytes 81952 | tf_op jit(solution)/shard_map/ppermute | solution.py:90
  21.1 0.0 collective-permute-done.4
  21.1 0.9 %bitcast_dynamic-update-slice_fusion.8 = bf16[8,80,512]{2,1,0:T(8,128)(2,1)S(1)} fusion(bf16[8,80,512]{2,1,0:T(8,128)(2,1)S(1)} %bitcast_dynamic-update-slice_fusion.10, bf16[80,512]{1,0:T(8,128)(2,1)} %shard_map.55), kind=kLoop, calls=%fused_computation.11 | loop fusion | bytes 163840
  22.0 0.9 %bitcast_dynamic-update-slice_fusion.9 = bf16[8,80,512]{2,1,0:T(8,128)(2,1)S(1)} fusion(bf16[8,80,512]{2,1,0:T(8,128)(2,1)S(1)} %bitcast_dynamic-update-slice_fusion.11, bf16[80,512]{1,0:T(8,128)(2,1)} %shard_map.55), kind=kLoop, calls=%fused_computation.12 | loop fusion | bytes 163840 | tf_op jit(solution)/shard_map/stack | solution.py:91
  22.9 0.8 %constant_dynamic-slice_fusion.1 = bf16[4,80,512]{2,1,0:T(8,128)(2,1)} fusion(bf16[8,80,512]{2,1,0:T(8,128)(2,1)S(1)} %bitcast_dynamic-update-slice_fusion.9, s32[]{:T(128)S(6)} %select_n.18), kind=kLoop, calls=%fused_computation.22 | loop fusion | bytes 655364 | tf_op jit(solution)/shard_map/dynamic_slice | solution.py:92
  23.7 1.4 %collective-permute-start.5 = (bf16[4,80,512]{2,1,0:T(8,128)(2,1)}, bf16[4,80,512]{2,1,0:T(8,128)(2,1)S(1)}, u32[]{:S(2)}, u32[]{:S(2)}) collective-permute-start(bf16[4,80,512]{2,1,0:T(8,128)(2,1)} %constant_dynamic-slice_fusion.1), channel_id=1, source_target_pairs={{0,6},{2,0},{4,2},{6,4},{1,7},{3,1},{5,3},{7,5},{8,14},{10,8},{12,... | collective-permute-start | bytes 983048 | tf_op jit(solution)/shard_map/ppermute | solution.py:90
  25.1 1.5 %collective-permute-start.6 = (bf16[4,80,512]{2,1,0:T(8,128)(2,1)}, bf16[4,80,512]{2,1,0:T(8,128)(2,1)S(1)}, u32[]{:S(2)}, u32[]{:S(2)}) collective-permute-start(bf16[4,80,512]{2,1,0:T(8,128)(2,1)} %constant_dynamic-slice_fusion.1), channel_id=1, source_target_pairs={{0,4},{2,6},{4,0},{6,2},{1,5},{3,7},{5,1},{7,3},{8,12},{10,14},{12... | collective-permute-start | bytes 983048 | tf_op jit(solution)/shard_map/ppermute | solution.py:90
  26.6 0.6 collective-permute-start.7
  27.2 6.4 %collective-permute-done.5 = bf16[4,80,512]{2,1,0:T(8,128)(2,1)S(1)} collective-permute-done((bf16[4,80,512]{2,1,0:T(8,128)(2,1)}, bf16[4,80,512]{2,1,0:T(8,128)(2,1)S(1)}, u32[]{:S(2)}, u32[]{:S(2)}) %collective-permute-start.5) | collective-permute-done | bytes 327712 | tf_op jit(solution)/shard_map/ppermute | solution.py:90
  33.6 4.8 %collective-permute-done.6 = bf16[4,80,512]{2,1,0:T(8,128)(2,1)S(1)} collective-permute-done((bf16[4,80,512]{2,1,0:T(8,128)(2,1)}, bf16[4,80,512]{2,1,0:T(8,128)(2,1)S(1)}, u32[]{:S(2)}, u32[]{:S(2)}) %collective-permute-start.6) | collective-permute-done | bytes 327712 | tf_op jit(solution)/shard_map/ppermute | solution.py:90
  38.4 0.0 collective-permute-done.7
  38.6 0.1 constant_dynamic-slice_fusion
  38.8 0.1 copy.14
  38.9 0.3 broadcast_in_dim.4
  39.2 5.8 %all_to_all.11 = bf16[4,4,2,80,512]{4,3,1,0,2:T(8,128)(2,1)S(1)} all-to-all(bf16[4,4,2,80,512]{4,3,1,0,2:T(8,128)(2,1)S(1)} %broadcast_in_dim.4), channel_id=1, replica_groups=mesh['grp'=1,'tok_o'=4,'tok_m'=4,'tok_c'=2] {'tok_c'}, dimensions={2} | all-to-all | bytes 5242880 | tf_op jit(solution)/shard_map/all_to_all | solution.py:82
  45.0 0.2 slice.21
  45.2 0.0 slice-start
  45.2 0.2 copy.19
  45.5 0.0 copy-done
  45.6 0.0 slice-start.1
  45.6 1.3 %fusion = f32[512,2048]{1,0:T(8,128)S(1)} fusion(bf16[512,512]{1,0:T(8,128)(2,1)S(1)} %bitcast.35, bf16[2048,512]{1,0:T(8,128)(2,1)S(1)} %copy-done), kind=kOutput, calls=%fused_computation.23 | convolution fusion | flops 1073741824 | bytes 6815744 | tf_op jit(solution)/shard_map/dot_general | solution.py:71
  46.9 0.5 slice-done
  47.4 1.4 %slice-done.1 = s8[4194304]{0:T(1024)(128)(4,1)S(1)} async-done(((s8[8388608]{0:T(1024)(128)(4,1)}), s8[4194304]{0:T(1024)(128)(4,1)S(1)}, s32[]{:S(2)}) %slice-start.1) | async-done | bytes 4194328
  48.8 4.8 %bitcast_reduce_fusion = f32[2048,16]{0,1:T(8,128)S(1)} fusion(f32[512,2048]{1,0:T(8,128)S(1)} %fusion, bf16[2048,512]{1,0:T(8,128)(2,1)S(1)} %bitcast.36, bf16[2048,2048]{1,0:T(8,128)(2,1)S(1)} %bitcast.38), kind=kOutput, calls=%fused_computation | convolution fusion | flops 4297031680 | bytes 14811136 | tf_op jit(solution)/shard_map/dot_general | solution.py:71
  53.6 0.1 multiply_reduce_fusion
  53.7 0.6 broadcast_in_dim.5
  54.3 6.2 %all-to-all-start.1 = ((f32[32,1,16]{2,1,0:T(1,128)}), f32[32,1,16]{2,1,0:T(1,128)S(1)}, u32[]{:S(2)}, u32[]{:S(2)}) async-start(f32[32,1,16]{2,1,0:T(1,128)} %broadcast_in_dim.5), calls=%async_computation.1 | async-start | bytes 32768 | tf_op jit(solution)/shard_map/all_to_all | solution.py:76
  60.6 0.5 slice.20
  61.1 0.6 slice.19
  62.9 4.7 %all-to-all-done.1 = f32[32,1,16]{2,1,0:T(1,128)S(1)} async-done(((f32[32,1,16]{2,1,0:T(1,128)}), f32[32,1,16]{2,1,0:T(1,128)S(1)}, u32[]{:S(2)}, u32[]{:S(2)}) %all-to-all-start.1) | async-done | bytes 2080 | tf_op jit(solution)/shard_map/all_to_all | solution.py:76
  67.6 0.1 reduce_sum.29
  67.7 0.7 %broadcast_divide_fusion = f32[2048,16]{0,1:T(8,128)} fusion(f32[2048,16]{0,1:T(8,128)S(1)} %bitcast_reduce_fusion, f32[16]{0:T(128)S(1)} %add_sqrt_fusion), kind=kLoop, calls=%fused_computation.19 | loop fusion | flops 32768 | bytes 262208 | tf_op jit(solution)/shard_map/div | solution.py:122
  (18 shorter events, 0.3 us)
Async XLA Ops:
  0.0 45.5 %copy-start = (bf16[2048,512]{1,0:T(8,128)(2,1)S(1)}, bf16[2048,512]{1,0:T(8,128)(2,1)}, u32[]{:S(2)}) copy-start(bf16[2048,512]{1,0:T(8,128)(2,1)} %param.6) | copy-start | bytes 6291460
  0.8 9.2 %collective-permute-start.1 = (bf16[8,128]{1,0:T(8,128)(2,1)S(1)}, bf16[8,128]{1,0:T(8,128)(2,1)S(1)}, u32[]{:S(2)}, u32[]{:S(2)}) collective-permute-start(bf16[8,128]{1,0:T(8,128)(2,1)S(1)} %slice.16), channel_id=1, source_target_pairs={{0,2},{2,4},{4,6},{6,0},{1,3},{3,5},{5,7},{7,1},{8,10},{10,12},{12... | collective-permute-start | bytes 6152 | tf_op jit(solution)/shard_map/ppermute | solution.py:97
  3.8 6.3 %collective-permute-start = (bf16[8,128]{1,0:T(8,128)(2,1)S(1)}, bf16[8,128]{1,0:T(8,128)(2,1)S(1)}, u32[]{:S(2)}, u32[]{:S(2)}) collective-permute-start(bf16[8,128]{1,0:T(8,128)(2,1)S(1)} %slice.16), channel_id=1, source_target_pairs={{0,8},{8,16},{16,24},{24,0},{1,9},{9,17},{17,25},{25,1},{2,10},{10... | collective-permute-start | bytes 6152 | tf_op jit(solution)/shard_map/ppermute | solution.py:97
  10.1 5.6 %collective-permute-start.2 = (bf16[80,512]{1,0:T(8,128)(2,1)}, bf16[80,512]{1,0:T(8,128)(2,1)S(1)}, u32[]{:S(2)}, u32[]{:S(2)}) collective-permute-start(bf16[80,512]{1,0:T(8,128)(2,1)} %shard_map.55), channel_id=1, source_target_pairs={{0,24},{8,0},{16,8},{24,16},{1,25},{9,1},{17,9},{25,17},{2,26},{10... | collective-permute-start | bytes 245768 | tf_op jit(solution)/shard_map/ppermute | solution.py:90
  12.4 8.7 %collective-permute-start.4 = (bf16[80,512]{1,0:T(8,128)(2,1)}, bf16[80,512]{1,0:T(8,128)(2,1)S(1)}, u32[]{:S(2)}, u32[]{:S(2)}) collective-permute-start(bf16[80,512]{1,0:T(8,128)(2,1)} %shard_map.55), channel_id=1, source_target_pairs={{0,8},{8,16},{16,24},{24,0},{1,9},{9,17},{17,25},{25,1},{2,10},{10... | collective-permute-start | bytes 245768 | tf_op jit(solution)/shard_map/ppermute | solution.py:90
  12.4 8.7 %collective-permute-start.3 = (bf16[80,512]{1,0:T(8,128)(2,1)}, bf16[80,512]{1,0:T(8,128)(2,1)S(1)}, u32[]{:S(2)}, u32[]{:S(2)}) collective-permute-start(bf16[80,512]{1,0:T(8,128)(2,1)} %shard_map.55), channel_id=1, source_target_pairs={{0,16},{8,24},{16,0},{24,8},{1,17},{9,25},{17,1},{25,9},{2,18},{10... | collective-permute-start | bytes 245768 | tf_op jit(solution)/shard_map/ppermute | solution.py:90
  23.7 9.9 %collective-permute-start.5 = (bf16[4,80,512]{2,1,0:T(8,128)(2,1)}, bf16[4,80,512]{2,1,0:T(8,128)(2,1)S(1)}, u32[]{:S(2)}, u32[]{:S(2)}) collective-permute-start(bf16[4,80,512]{2,1,0:T(8,128)(2,1)} %constant_dynamic-slice_fusion.1), channel_id=1, source_target_pairs={{0,6},{2,0},{4,2},{6,4},{1,7},{3,1},{5,3},{7,5},{8,14},{10,8},{12,... | collective-permute-start | bytes 983048 | tf_op jit(solution)/shard_map/ppermute | solution.py:90
  25.1 13.3 %collective-permute-start.6 = (bf16[4,80,512]{2,1,0:T(8,128)(2,1)}, bf16[4,80,512]{2,1,0:T(8,128)(2,1)S(1)}, u32[]{:S(2)}, u32[]{:S(2)}) collective-permute-start(bf16[4,80,512]{2,1,0:T(8,128)(2,1)} %constant_dynamic-slice_fusion.1), channel_id=1, source_target_pairs={{0,4},{2,6},{4,0},{6,2},{1,5},{3,7},{5,1},{7,3},{8,12},{10,14},{12... | collective-permute-start | bytes 983048 | tf_op jit(solution)/shard_map/ppermute | solution.py:90
  26.6 11.8 %collective-permute-start.7 = (bf16[4,80,512]{2,1,0:T(8,128)(2,1)}, bf16[4,80,512]{2,1,0:T(8,128)(2,1)S(1)}, u32[]{:S(2)}, u32[]{:S(2)}) collective-permute-start(bf16[4,80,512]{2,1,0:T(8,128)(2,1)} %constant_dynamic-slice_fusion.1), channel_id=1, source_target_pairs={{0,2},{2,4},{4,6},{6,0},{1,3},{3,5},{5,7},{7,1},{8,10},{10,12},{12... | collective-permute-start | bytes 983048 | tf_op jit(solution)/shard_map/ppermute | solution.py:90
  45.2 2.2 %slice-start = ((s8[8388608]{0:T(1024)(128)(4,1)}), s8[4194304]{0:T(1024)(128)(4,1)S(1)}, s32[]{:S(2)}) async-start(s8[8388608]{0:T(1024)(128)(4,1)} %bitcast.37), calls=%async_computation.2 | async-start | bytes 8388608
  45.6 3.2 %slice-start.1 = ((s8[8388608]{0:T(1024)(128)(4,1)}), s8[4194304]{0:T(1024)(128)(4,1)S(1)}, s32[]{:S(2)}) async-start(s8[8388608]{0:T(1024)(128)(4,1)} %bitcast.37), calls=%async_computation.3 | async-start | bytes 8388608
  54.3 13.3 %all-to-all-start.1 = ((f32[32,1,16]{2,1,0:T(1,128)}), f32[32,1,16]{2,1,0:T(1,128)S(1)}, u32[]{:S(2)}, u32[]{:S(2)}) async-start(f32[32,1,16]{2,1,0:T(1,128)} %broadcast_in_dim.5), calls=%async_computation.1 | async-start | bytes 32768 | tf_op jit(solution)/shard_map/all_to_all | solution.py:76

commit v9 on v7

--- a/solution.py
+++ b/solution.py
@@ -27,17 +27,17 @@
         base = bases[k]
         lane = lax.broadcasted_iota(jnp.int32, (rows, LANES), 1)
         for g in range(queries // PER_TILE):
-            acc = jnp.zeros((rows, LANES), jnp.float32)
+            acc = jnp.zeros((rows, LANES), buf.dtype)
             for j in range(PER_TILE):
                 q = g * PER_TILE + j
                 copies[k * queries + q].wait()
-                x = buf[q].astype(jnp.float32)
+                x = buf[q]
                 off = (ids_ref[q] % PER_TILE) * RANK
                 shift = (RANK * j - off + LANES) % LANES
                 moved = pltpu.roll(x, shift, 1)
                 keep = (lane >= RANK * j) & (lane < RANK * (j + 1))
                 acc = jnp.where(keep, moved, acc)
-            out[base:base + rows, g * LANES:(g + 1) * LANES] = acc.astype(out.dtype)
+            out[base:base + rows, g * LANES:(g + 1) * LANES] = acc
 
 
 def pick_columns(v_bank, u_bank, query_ids):
@@ -88,8 +88,13 @@
         return spread(x, axis, at)
     me = lax.axis_index(axis)
     got = [x] + [lax.ppermute(x, axis, [(j, (j + s) % k) for j in range(k)]) for s in range(1, k)]
-    back = jnp.stack(got[::-1] + got[::-1], axis=at)
-    return lax.dynamic_slice_in_dim(back, (k - 1 - me) % k, k, axis=at)
+    slots = []
+    for o in range(k):
+        value = got[0]
+        for s in range(1, k):
+            value = jnp.where((me - s + k) % k == o, got[s], value)
+        slots.append(value)
+    return jnp.stack(slots, axis=at)
 
 
 def gather_factors(both, rows_v):

time: 65.4 us -> 62.9 us (0.962)
  local copies, waits for them, and re-layouts: 5.7 us -> 2.79 us
  other arithmetic: 0.94 us -> 3 us
  starting transfers between devices: 9.66 us -> 11.5 us
  waiting for transfers between devices: 19.3 us -> 17.6 us
  blocking collectives: 18.3 us -> 16.9 us
    another operation x0 -> x5, other arithmetic: none -> 2.07 us  [shifted(): return jnp.stack(slots, axis=at)]
    ppermute x6, starting transfers between devices: 9.66 us -> 11.5 us  [shifted(): lax.ppermute(x, axis, [(j, (j + s) % k) for j in range(k)])]
    ppermute x6, waiting for transfers between devices: 19.3 us -> 17.6 us  [shifted(): lax.ppermute(x, axis, [(j, (j + s) % k) for j in range(k)])]
    all_to_all x1, blocking collectives: 12.5 us -> 11 us  [total_over(): return lax.all_to_all(copies, axis, 0, 0, tiled=False).sum(axis=0)]
    unnamed x22 -> x8, local copies, waits for them, and re-layouts: 3.27 us -> 2.16 us
    dynamic_slice x3 -> x0, local copies, waits for them, and re-layouts: 0.98 us -> none  [shifted(): return lax.dynamic_slice_in_dim(back, (k - 1 - me) % k, k, axis=at)]
    another operation x2 -> x1, local copies, waits for them, and re-layouts: 0.93 us -> 0.11 us  [shifted(): return jnp.stack(slots, axis=at)]
  transfers between devices with their start and end apart: 6 -> 6, of which waited for: 4 -> 5; matrix products, arithmetic and copies ran while one was open for 0% -> 0% of each run, Pallas kernels for 0% -> 0%
where the time goes in v9:
time: 62.9 us; the launch traced here: 62.7 us
  waiting for transfers between devices  17.6 us (28%)
  blocking collectives  16.9 us (27%)
  starting transfers between devices  11.5 us (18%)
  matrix products  6.12 us (10%)
  Pallas kernels  4.73 us (8%)
  other arithmetic  3 us (5%)
  local copies, waits for them, and re-layouts  2.79 us (4%)
    ppermute x6, waiting for transfers between devices, shifted(): lax.ppermute(x, axis, [(j, (j + s) % k) for j in range(k)])  17.6 us
    ppermute x6, starting transfers between devices, shifted(): lax.ppermute(x, axis, [(j, (j + s) % k) for j in range(k)])  11.5 us
    all_to_all x1, blocking collectives, total_over(): return lax.all_to_all(copies, axis, 0, 0, tiled=False).sum(axis=0)  11 us
    dot_general x2, matrix products, folder(): return jnp.dot(left, piece, preferred_element_type=jnp.float32)  6.12 us
    all_to_all x1, blocking collectives, spread(): return lax.all_to_all(copies, axis, at, at, tiled=True)  5.84 us
    pallas_call x1, Pallas kernels, pick_columns(): pl.pallas_call(pick_kernel, out_shape=jax.ShapeDtypeStruct((v_bank.shape[...  4.73 us
    unnamed x8, local copies, waits for them, and re-layouts  2.16 us
    another operation x5, other arithmetic, shifted(): return jnp.stack(slots, axis=at)  2.07 us
  transfers between devices with their start and end apart: 6, of which 5 were waited for; matrix products, arithmetic and copies ran while one was open for 0% of the time, Pallas kernels for 0%

profile of v9, /device:TPU:0, one launch (start us, length us, event | category | flops | bytes accessed | tf_op | source)
XLA Modules:
  0.0 62.7 jit_solution(13944777105909408820)
XLA Ops:
  0.0 0.0 copy-start
  0.0 4.7 %shard_map.55 = bf16[80,512]{1,0:T(8,128)(2,1)} custom-call(s32[16]{0:T(128)} %ids_ref.1, bf16[64,65536]{1,0:T(8,128)(2,1)} %v_ref.1, bf16[16,65536]{1,0:T(8,128)(2,1)} %u_ref.1), custom_call_target="tpu_custom_call" | custom-call | tf_op jit(solution)/shard_map/pallas_call | solution.py:47
  4.7 3.1 %collective-permute-start.2 = (bf16[80,512]{1,0:T(8,128)(2,1)}, bf16[80,512]{1,0:T(8,128)(2,1)S(1)}, u32[]{:S(2)}, u32[]{:S(2)}) collective-permute-start(bf16[80,512]{1,0:T(8,128)(2,1)} %shard_map.55), channel_id=1, source_target_pairs={{0,8},{8,16},{16,24},{24,0},{1,9},{9,17},{17,25},{25,1},{2,10},{10... | collective-permute-start | bytes 245768 | tf_op jit(solution)/shard_map/ppermute | solution.py:90
  7.8 2.6 %collective-permute-start.1 = (bf16[80,512]{1,0:T(8,128)(2,1)}, bf16[80,512]{1,0:T(8,128)(2,1)S(1)}, u32[]{:S(2)}, u32[]{:S(2)}) collective-permute-start(bf16[80,512]{1,0:T(8,128)(2,1)} %shard_map.55), channel_id=1, source_target_pairs={{0,16},{8,24},{16,0},{24,8},{1,17},{9,25},{17,1},{25,9},{2,18},{10... | collective-permute-start | bytes 245768 | tf_op jit(solution)/shard_map/ppermute | solution.py:90
  10.4 1.3 %collective-permute-start = (bf16[80,512]{1,0:T(8,128)(2,1)}, bf16[80,512]{1,0:T(8,128)(2,1)S(1)}, u32[]{:S(2)}, u32[]{:S(2)}) collective-permute-start(bf16[80,512]{1,0:T(8,128)(2,1)} %shard_map.55), channel_id=1, source_target_pairs={{0,24},{8,0},{16,8},{24,16},{1,25},{9,1},{17,9},{25,17},{2,26},{10... | collective-permute-start | bytes 245768 | tf_op jit(solution)/shard_map/ppermute | solution.py:90
  11.8 1.3 %collective-permute-done.2 = bf16[80,512]{1,0:T(8,128)(2,1)S(1)} collective-permute-done((bf16[80,512]{1,0:T(8,128)(2,1)}, bf16[80,512]{1,0:T(8,128)(2,1)S(1)}, u32[]{:S(2)}, u32[]{:S(2)}) %collective-permute-start.2) | collective-permute-done | bytes 81952 | tf_op jit(solution)/shard_map/ppermute | solution.py:90
  13.1 3.0 %collective-permute-done.1 = bf16[80,512]{1,0:T(8,128)(2,1)S(1)} collective-permute-done((bf16[80,512]{1,0:T(8,128)(2,1)}, bf16[80,512]{1,0:T(8,128)(2,1)S(1)}, u32[]{:S(2)}, u32[]{:S(2)}) %collective-permute-start.1) | collective-permute-done | bytes 81952 | tf_op jit(solution)/shard_map/ppermute | solution.py:90
  16.1 0.2 collective-permute-done
  16.3 0.9 %select_bitcast_fusion.7 = (bf16[1,80,512]{2,1,0:T(8,128)(2,1)S(1)}, bf16[1,80,512]{2,1,0:T(8,128)(2,1)S(1)}, bf16[1,80,512]{2,1,0:T(8,128)(2,1)S(1)}, bf16[1,80,512]{2,1,0:T(8,128)(2,1)S(1)}) fusion(bf16[80,512]{1,0:T(8,128)(2,1)S(1)} %collective-permute-done, bf16[80,512]{1,0:T(8,128)(2,1)S(1)} %collective-permute-done.1, ...), kind=kLoop, calls=%fused_computation.12 | loop fusion | flops 491520 | bytes 655372 | tf_op jit(solution)/shard_map/stack | solution.py:97
  17.3 0.8 %pad_maximum_fusion.1 = bf16[4,80,512]{2,1,0:T(8,128)(2,1)} fusion(bf16[1,80,512]{2,1,0:T(8,128)(2,1)S(1)} %get-tuple-element.10, bf16[1,80,512]{2,1,0:T(8,128)(2,1)S(1)} %get-tuple-element.11, bf16[1,80,512]{2,1,0:T(8,128)(2,1)S(1)} %get-tuple-element.12, bf16[1,80,512]{2,1,0:T(8,128)(2,1)S(1)} %get-tuple-element.9), kind=kLoop, calls=%fused_computation.3 | loop fusion | flops 491520 | bytes 655360 | tf_op jit(solution)/shard_map/stack | solution.py:97
  18.0 1.5 %collective-permute-start.5 = (bf16[4,80,512]{2,1,0:T(8,128)(2,1)}, bf16[4,80,512]{2,1,0:T(8,128)(2,1)S(1)}, u32[]{:S(2)}, u32[]{:S(2)}) collective-permute-start(bf16[4,80,512]{2,1,0:T(8,128)(2,1)} %pad_maximum_fusion.1), channel_id=1, source_target_pairs={{0,2},{2,4},{4,6},{6,0},{1,3},{3,5},{5,7},{7,1},{8,10},{10,12},{12... | collective-permute-start | bytes 983048 | tf_op jit(solution)/shard_map/ppermute | solution.py:90
  19.5 1.5 %collective-permute-start.4 = (bf16[4,80,512]{2,1,0:T(8,128)(2,1)}, bf16[4,80,512]{2,1,0:T(8,128)(2,1)S(1)}, u32[]{:S(2)}, u32[]{:S(2)}) collective-permute-start(bf16[4,80,512]{2,1,0:T(8,128)(2,1)} %pad_maximum_fusion.1), channel_id=1, source_target_pairs={{0,4},{2,6},{4,0},{6,2},{1,5},{3,7},{5,1},{7,3},{8,12},{10,14},{12... | collective-permute-start | bytes 983048 | tf_op jit(solution)/shard_map/ppermute | solution.py:90
  21.0 1.4 %collective-permute-start.3 = (bf16[4,80,512]{2,1,0:T(8,128)(2,1)}, bf16[4,80,512]{2,1,0:T(8,128)(2,1)S(1)}, u32[]{:S(2)}, u32[]{:S(2)}) collective-permute-start(bf16[4,80,512]{2,1,0:T(8,128)(2,1)} %pad_maximum_fusion.1), channel_id=1, source_target_pairs={{0,6},{2,0},{4,2},{6,4},{1,7},{3,1},{5,3},{7,5},{8,14},{10,8},{12,... | collective-permute-start | bytes 983048 | tf_op jit(solution)/shard_map/ppermute | solution.py:90
  22.5 7.3 %collective-permute-done.5 = bf16[4,80,512]{2,1,0:T(8,128)(2,1)S(1)} collective-permute-done((bf16[4,80,512]{2,1,0:T(8,128)(2,1)}, bf16[4,80,512]{2,1,0:T(8,128)(2,1)S(1)}, u32[]{:S(2)}, u32[]{:S(2)}) %collective-permute-start.5) | collective-permute-done | bytes 327712 | tf_op jit(solution)/shard_map/ppermute | solution.py:90
  29.8 5.7 %collective-permute-done.4 = bf16[4,80,512]{2,1,0:T(8,128)(2,1)S(1)} collective-permute-done((bf16[4,80,512]{2,1,0:T(8,128)(2,1)}, bf16[4,80,512]{2,1,0:T(8,128)(2,1)S(1)}, u32[]{:S(2)}, u32[]{:S(2)}) %collective-permute-start.4) | collective-permute-done | bytes 327712 | tf_op jit(solution)/shard_map/ppermute | solution.py:90
  35.5 0.0 collective-permute-done.3
  35.5 0.1 select_bitcast_fusion.2
  35.6 0.1 select_bitcast_fusion.3
  35.7 0.2 pad_maximum_fusion
  35.9 0.1 copy.14
  36.0 0.3 broadcast_in_dim.4
  36.3 5.8 %all_to_all.11 = bf16[4,4,2,80,512]{4,3,1,0,2:T(8,128)(2,1)S(1)} all-to-all(bf16[4,4,2,80,512]{4,3,1,0,2:T(8,128)(2,1)S(1)} %broadcast_in_dim.4), channel_id=1, replica_groups=mesh['grp'=1,'tok_o'=4,'tok_m'=4,'tok_c'=2] {'tok_c'}, dimensions={2} | all-to-all | bytes 5242880 | tf_op jit(solution)/shard_map/all_to_all | solution.py:82
  42.1 0.2 slice.8
  42.3 0.0 slice-start
  42.3 0.2 copy.19
  42.6 0.0 copy-done
  42.6 0.0 slice-start.1
  42.7 1.3 %fusion = f32[512,2048]{1,0:T(8,128)S(1)} fusion(bf16[512,512]{1,0:T(8,128)(2,1)S(1)} %bitcast.26, bf16[2048,512]{1,0:T(8,128)(2,1)S(1)} %copy-done), kind=kOutput, calls=%fused_computation.15 | convolution fusion | flops 1073741824 | bytes 6815744 | tf_op jit(solution)/shard_map/dot_general | solution.py:71
  44.0 0.5 slice-done
  44.5 1.4 %slice-done.1 = s8[4194304]{0:T(1024)(128)(4,1)S(1)} async-done(((s8[8388608]{0:T(1024)(128)(4,1)}), s8[4194304]{0:T(1024)(128)(4,1)S(1)}, s32[]{:S(2)}) %slice-start.1) | async-done | bytes 4194328
  45.9 4.8 %bitcast_reduce_fusion = f32[2048,16]{0,1:T(8,128)S(1)} fusion(f32[512,2048]{1,0:T(8,128)S(1)} %fusion, bf16[2048,512]{1,0:T(8,128)(2,1)S(1)} %bitcast.27, bf16[2048,2048]{1,0:T(8,128)(2,1)S(1)} %bitcast.29), kind=kOutput, calls=%fused_computation | convolution fusion | flops 4297031680 | bytes 14811136 | tf_op jit(solution)/shard_map/dot_general | solution.py:71
  50.7 0.1 multiply_reduce_fusion
  50.8 11.0 %all_to_all.12 = f32[32,1,16]{2,1,0:T(1,128)S(1)} all-to-all(f32[32,1,16]{2,1,0:T(1,128)S(1)} %broadcast_in_dim.5), channel_id=1, replica_groups=mesh['grp'=1,'tok_o'=4,'tok_m'=4,'tok_c'=2] {'tok_o','tok_m','tok_c'}, dimensions={0} | all-to-all | bytes 4096 | tf_op jit(solution)/shard_map/all_to_all | solution.py:76
  61.9 0.1 reduce_sum.29
  61.9 0.7 %broadcast_divide_fusion = f32[2048,16]{0,1:T(8,128)} fusion(f32[2048,16]{0,1:T(8,128)S(1)} %bitcast_reduce_fusion, f32[16]{0:T(128)S(1)} %add_sqrt_fusion), kind=kLoop, calls=%fused_computation.13 | loop fusion | flops 32768 | bytes 262208 | tf_op jit(solution)/shard_map/div | solution.py:119
  (5 shorter events, 0.1 us)
Async XLA Ops:
  0.0 42.6 %copy-start = (bf16[2048,512]{1,0:T(8,128)(2,1)S(1)}, bf16[2048,512]{1,0:T(8,128)(2,1)}, u32[]{:S(2)}) copy-start(bf16[2048,512]{1,0:T(8,128)(2,1)} %param.6) | copy-start | bytes 6291460
  4.7 8.3 %collective-permute-start.2 = (bf16[80,512]{1,0:T(8,128)(2,1)}, bf16[80,512]{1,0:T(8,128)(2,1)S(1)}, u32[]{:S(2)}, u32[]{:S(2)}) collective-permute-start(bf16[80,512]{1,0:T(8,128)(2,1)} %shard_map.55), channel_id=1, source_target_pairs={{0,8},{8,16},{16,24},{24,0},{1,9},{9,17},{17,25},{25,1},{2,10},{10... | collective-permute-start | bytes 245768 | tf_op jit(solution)/shard_map/ppermute | solution.py:90
  7.8 8.3 %collective-permute-start.1 = (bf16[80,512]{1,0:T(8,128)(2,1)}, bf16[80,512]{1,0:T(8,128)(2,1)S(1)}, u32[]{:S(2)}, u32[]{:S(2)}) collective-permute-start(bf16[80,512]{1,0:T(8,128)(2,1)} %shard_map.55), channel_id=1, source_target_pairs={{0,16},{8,24},{16,0},{24,8},{1,17},{9,25},{17,1},{25,9},{2,18},{10... | collective-permute-start | bytes 245768 | tf_op jit(solution)/shard_map/ppermute | solution.py:90
  10.4 5.9 %collective-permute-start = (bf16[80,512]{1,0:T(8,128)(2,1)}, bf16[80,512]{1,0:T(8,128)(2,1)S(1)}, u32[]{:S(2)}, u32[]{:S(2)}) collective-permute-start(bf16[80,512]{1,0:T(8,128)(2,1)} %shard_map.55), channel_id=1, source_target_pairs={{0,24},{8,0},{16,8},{24,16},{1,25},{9,1},{17,9},{25,17},{2,26},{10... | collective-permute-start | bytes 245768 | tf_op jit(solution)/shard_map/ppermute | solution.py:90
  18.0 11.8 %collective-permute-start.5 = (bf16[4,80,512]{2,1,0:T(8,128)(2,1)}, bf16[4,80,512]{2,1,0:T(8,128)(2,1)S(1)}, u32[]{:S(2)}, u32[]{:S(2)}) collective-permute-start(bf16[4,80,512]{2,1,0:T(8,128)(2,1)} %pad_maximum_fusion.1), channel_id=1, source_target_pairs={{0,2},{2,4},{4,6},{6,0},{1,3},{3,5},{5,7},{7,1},{8,10},{10,12},{12... | collective-permute-start | bytes 983048 | tf_op jit(solution)/shard_map/ppermute | solution.py:90
  19.5 16.0 %collective-permute-start.4 = (bf16[4,80,512]{2,1,0:T(8,128)(2,1)}, bf16[4,80,512]{2,1,0:T(8,128)(2,1)S(1)}, u32[]{:S(2)}, u32[]{:S(2)}) collective-permute-start(bf16[4,80,512]{2,1,0:T(8,128)(2,1)} %pad_maximum_fusion.1), channel_id=1, source_target_pairs={{0,4},{2,6},{4,0},{6,2},{1,5},{3,7},{5,1},{7,3},{8,12},{10,14},{12... | collective-permute-start | bytes 983048 | tf_op jit(solution)/shard_map/ppermute | solution.py:90
  21.0 14.5 %collective-permute-start.3 = (bf16[4,80,512]{2,1,0:T(8,128)(2,1)}, bf16[4,80,512]{2,1,0:T(8,128)(2,1)S(1)}, u32[]{:S(2)}, u32[]{:S(2)}) collective-permute-start(bf16[4,80,512]{2,1,0:T(8,128)(2,1)} %pad_maximum_fusion.1), channel_id=1, source_target_pairs={{0,6},{2,0},{4,2},{6,4},{1,7},{3,1},{5,3},{7,5},{8,14},{10,8},{12,... | collective-permute-start | bytes 983048 | tf_op jit(solution)/shard_map/ppermute | solution.py:90
  42.3 2.2 %slice-start = ((s8[8388608]{0:T(1024)(128)(4,1)}), s8[4194304]{0:T(1024)(128)(4,1)S(1)}, s32[]{:S(2)}) async-start(s8[8388608]{0:T(1024)(128)(4,1)} %bitcast.28), calls=%async_computation.2 | async-start | bytes 8388608
  42.6 3.2 %slice-start.1 = ((s8[8388608]{0:T(1024)(128)(4,1)}), s8[4194304]{0:T(1024)(128)(4,1)S(1)}, s32[]{:S(2)}) async-start(s8[8388608]{0:T(1024)(128)(4,1)} %bitcast.28), calls=%async_computation.3 | async-start | bytes 8388608

commit v10 on v9

--- a/solution.py
+++ b/solution.py
@@ -101,8 +101,16 @@
     cols = both.shape[1]
     held = shifted(both, OUTER, 0)
     held = shifted(held, MIDDLE, 1)
-    held = spread(held, CORE, 2)
-    return held[:, :, :, :rows_v].reshape(-1, cols), held[:, :, :, rows_v:].reshape(-1, cols)
+    mine = held
+    other = lax.ppermute(held, CORE, [(0, 1), (1, 0)])
+    first = lax.axis_index(CORE) == 0
+    low = jnp.where(first, mine, other)
+    high = jnp.where(first, other, mine)
+
+    def part(lo, hi):
+        return jnp.stack([low[:, :, lo:hi], high[:, :, lo:hi]], axis=2).reshape(-1, cols)
+
+    return part(0, rows_v), part(rows_v, both.shape[0])
 
 
 def on_device(activations, out_grads, v_bank, u_bank, query_ids):

time: 62.9 us -> 65.1 us (1.035)
  blocking collectives: 16.9 us -> 11 us
  other arithmetic: 3 us -> 7.49 us
  waiting for transfers between devices: 17.6 us -> 20.7 us
    all_to_all x1 -> x0, blocking collectives: 5.84 us -> none  [spread(): return lax.all_to_all(copies, axis, at, at, tiled=True)]
    ppermute x0 -> x1, waiting for transfers between devices: none -> 3.26 us  [gather_factors(): other = lax.ppermute(held, CORE, [(0, 1), (1, 0)])]
    another operation x5, other arithmetic: 2.07 us -> 4.75 us  [shifted(): return jnp.stack(slots, axis=at)]
    select_n x0 -> x1, other arithmetic: none -> 1.55 us  [gather_factors(): low = jnp.where(first, mine, other)]
    unnamed x8 -> x14, local copies, waits for them, and re-layouts: 2.16 us -> 2.53 us
  transfers between devices with their start and end apart: 6 -> 7, of which waited for: 5 -> 7; matrix products, arithmetic and copies ran while one was open for 0% -> 0% of each run, Pallas kernels for 0% -> 0%
where the time goes in v10:
time: 65.1 us; the launch traced here: 64.8 us
  waiting for transfers between devices  20.7 us (32%)
  starting transfers between devices  11.6 us (18%)
  blocking collectives  11 us (17%)
  other arithmetic  7.49 us (12%)
  matrix products  6.12 us (9%)
  Pallas kernels  4.73 us (7%)
  local copies, waits for them, and re-layouts  2.96 us (5%)
    ppermute x6, waiting for transfers between devices, shifted(): lax.ppermute(x, axis, [(j, (j + s) % k) for j in range(k)])  17.5 us
    ppermute x6, starting transfers between devices, shifted(): lax.ppermute(x, axis, [(j, (j + s) % k) for j in range(k)])  11.5 us
    all_to_all x1, blocking collectives, total_over(): return lax.all_to_all(copies, axis, 0, 0, tiled=False).sum(axis=0)  11 us
    dot_general x2, matrix products, folder(): return jnp.dot(left, piece, preferred_element_type=jnp.float32)  6.12 us
    another operation x5, other arithmetic, shifted(): return jnp.stack(slots, axis=at)  4.75 us
    pallas_call x1, Pallas kernels, pick_columns(): pl.pallas_call(pick_kernel, out_shape=jax.ShapeDtypeStruct((v_bank.shape[...  4.73 us
    ppermute x1, waiting for transfers between devices, gather_factors(): other = lax.ppermute(held, CORE, [(0, 1), (1, 0)])  3.26 us
    unnamed x14, local copies, waits for them, and re-layouts  2.53 us
  transfers between devices with their start and end apart: 7, of which 7 were waited for; matrix products, arithmetic and copies ran while one was open for 0% of the time, Pallas kernels for 0%

profile of v10, /device:TPU:0, one launch (start us, length us, event | category | flops | bytes accessed | tf_op | source)
XLA Modules:
  0.0 64.8 jit_solution(1608008216779106709)
XLA Ops:
  0.0 0.0 copy-start
  0.0 4.7 %shard_map.55 = bf16[80,512]{1,0:T(8,128)(2,1)} custom-call(s32[16]{0:T(128)} %ids_ref.1, bf16[64,65536]{1,0:T(8,128)(2,1)} %v_ref.1, bf16[16,65536]{1,0:T(8,128)(2,1)} %u_ref.1), custom_call_target="tpu_custom_call" | custom-call | tf_op jit(solution)/shard_map/pallas_call | solution.py:47
  4.7 3.1 %collective-permute-start.2 = (bf16[80,512]{1,0:T(8,128)(2,1)}, bf16[80,512]{1,0:T(8,128)(2,1)S(1)}, u32[]{:S(2)}, u32[]{:S(2)}) collective-permute-start(bf16[80,512]{1,0:T(8,128)(2,1)} %shard_map.55), channel_id=1, source_target_pairs={{0,8},{8,16},{16,24},{24,0},{1,9},{9,17},{17,25},{25,1},{2,10},{10... | collective-permute-start | bytes 245768 | tf_op jit(solution)/shard_map/ppermute | solution.py:90
  7.8 2.6 %collective-permute-start.1 = (bf16[80,512]{1,0:T(8,128)(2,1)}, bf16[80,512]{1,0:T(8,128)(2,1)S(1)}, u32[]{:S(2)}, u32[]{:S(2)}) collective-permute-start(bf16[80,512]{1,0:T(8,128)(2,1)} %shard_map.55), channel_id=1, source_target_pairs={{0,16},{8,24},{16,0},{24,8},{1,17},{9,25},{17,1},{25,9},{2,18},{10... | collective-permute-start | bytes 245768 | tf_op jit(solution)/shard_map/ppermute | solution.py:90
  10.4 1.3 %collective-permute-start = (bf16[80,512]{1,0:T(8,128)(2,1)}, bf16[80,512]{1,0:T(8,128)(2,1)S(1)}, u32[]{:S(2)}, u32[]{:S(2)}) collective-permute-start(bf16[80,512]{1,0:T(8,128)(2,1)} %shard_map.55), channel_id=1, source_target_pairs={{0,24},{8,0},{16,8},{24,16},{1,25},{9,1},{17,9},{25,17},{2,26},{10... | collective-permute-start | bytes 245768 | tf_op jit(solution)/shard_map/ppermute | solution.py:90
  11.8 1.3 %collective-permute-done.2 = bf16[80,512]{1,0:T(8,128)(2,1)S(1)} collective-permute-done((bf16[80,512]{1,0:T(8,128)(2,1)}, bf16[80,512]{1,0:T(8,128)(2,1)S(1)}, u32[]{:S(2)}, u32[]{:S(2)}) %collective-permute-start.2) | collective-permute-done | bytes 81952 | tf_op jit(solution)/shard_map/ppermute | solution.py:90
  13.1 3.0 %collective-permute-done.1 = bf16[80,512]{1,0:T(8,128)(2,1)S(1)} collective-permute-done((bf16[80,512]{1,0:T(8,128)(2,1)}, bf16[80,512]{1,0:T(8,128)(2,1)S(1)}, u32[]{:S(2)}, u32[]{:S(2)}) %collective-permute-start.1) | collective-permute-done | bytes 81952 | tf_op jit(solution)/shard_map/ppermute | solution.py:90
  16.1 0.2 collective-permute-done
  16.3 0.9 %select_bitcast_fusion.7 = (bf16[1,80,512]{2,1,0:T(8,128)(2,1)S(1)}, bf16[1,80,512]{2,1,0:T(8,128)(2,1)S(1)}, bf16[1,80,512]{2,1,0:T(8,128)(2,1)S(1)}, bf16[1,80,512]{2,1,0:T(8,128)(2,1)S(1)}) fusion(bf16[80,512]{1,0:T(8,128)(2,1)S(1)} %collective-permute-done, bf16[80,512]{1,0:T(8,128)(2,1)S(1)} %collective-permute-done.1, ...), kind=kLoop, calls=%fused_computation.20 | loop fusion | flops 491520 | bytes 655372 | tf_op jit(solution)/shard_map/stack | solution.py:97
  17.3 0.0 copy-start.1
  17.3 0.0 copy-start.2
  17.3 0.0 copy-start.3
  17.3 1.5 %collective-permute-start.5 = (bf16[4,80,512]{2,1,0:T(8,128)(2,1)S(1)}, bf16[4,80,512]{2,1,0:T(8,128)(2,1)}, u32[]{:S(2)}, u32[]{:S(2)}) collective-permute-start(bf16[4,80,512]{2,1,0:T(8,128)(2,1)S(1)} %pad_maximum_fusion.3), channel_id=1, source_target_pairs={{0,2},{2,4},{4,6},{6,0},{1,3},{3,5},{5,7},{7,1},{8,10},{10,12},{12... | collective-permute-start | bytes 983048 | tf_op jit(solution)/shard_map/ppermute | solution.py:90
  18.9 1.5 %collective-permute-start.4 = (bf16[4,80,512]{2,1,0:T(8,128)(2,1)S(1)}, bf16[4,80,512]{2,1,0:T(8,128)(2,1)S(1)}, u32[]{:S(2)}, u32[]{:S(2)}) collective-permute-start(bf16[4,80,512]{2,1,0:T(8,128)(2,1)S(1)} %pad_maximum_fusion.3), channel_id=1, source_target_pairs={{0,4},{2,6},{4,0},{6,2},{1,5},{3,7},{5,1},{7,3},{8,12},{10,14},{12... | collective-permute-start | bytes 983048 | tf_op jit(solution)/shard_map/ppermute | solution.py:90
  20.4 1.4 %collective-permute-start.3 = (bf16[4,80,512]{2,1,0:T(8,128)(2,1)S(1)}, bf16[4,80,512]{2,1,0:T(8,128)(2,1)}, u32[]{:S(2)}, u32[]{:S(2)}) collective-permute-start(bf16[4,80,512]{2,1,0:T(8,128)(2,1)S(1)} %pad_maximum_fusion.3), channel_id=1, source_target_pairs={{0,6},{2,0},{4,2},{6,4},{1,7},{3,1},{5,3},{7,5},{8,14},{10,8},{12,... | collective-permute-start | bytes 983048 | tf_op jit(solution)/shard_map/ppermute | solution.py:90
  21.8 7.2 %collective-permute-done.5 = bf16[4,80,512]{2,1,0:T(8,128)(2,1)} collective-permute-done((bf16[4,80,512]{2,1,0:T(8,128)(2,1)S(1)}, bf16[4,80,512]{2,1,0:T(8,128)(2,1)}, u32[]{:S(2)}, u32[]{:S(2)}) %collective-permute-start.5) | collective-permute-done | bytes 327712 | tf_op jit(solution)/shard_map/ppermute | solution.py:90
  29.1 5.6 %collective-permute-done.4 = bf16[4,80,512]{2,1,0:T(8,128)(2,1)S(1)} collective-permute-done((bf16[4,80,512]{2,1,0:T(8,128)(2,1)S(1)}, bf16[4,80,512]{2,1,0:T(8,128)(2,1)S(1)}, u32[]{:S(2)}, u32[]{:S(2)}) %collective-permute-start.4) | collective-permute-done | bytes 327712 | tf_op jit(solution)/shard_map/ppermute | solution.py:90
  34.6 0.0 copy-start.4
  34.6 0.1 collective-permute-done.3
  34.7 0.0 copy-done.1
  34.8 0.0 copy-done.2
  34.8 0.0 copy-done.3
  34.8 0.6 copy-done.4
  35.4 1.2 %select_bitcast_fusion.2 = (bf16[4,1,80,512]{3,2,0,1:T(8,128)(2,1)S(1)}, bf16[4,1,80,512]{3,2,0,1:T(8,128)(2,1)S(1)}) fusion(bf16[4,80,512]{2,1,0:T(8,128)(2,1)} %collective-permute-done.3, bf16[4,80,512]{2,1,0:T(8,128)(2,1)S(1)} %collective-permute-done.4, bf16[4,80,512]{2,1,0:T(8,128)(2,1)} %collective-permute-done.5, pred[]{:T(512)S(6)} %eq.118, ...), kind=kLoop, calls=%fused_computation.12 | loop fusion | flops 1474560 | bytes 1966086 | tf_op jit(solution)/shard_map/stack | solution.py:97
  36.5 1.4 %select_bitcast_fusion.3 = (bf16[4,1,80,512]{3,2,0,1:T(8,128)(2,1)S(1)}, bf16[4,1,80,512]{3,2,0,1:T(8,128)(2,1)S(1)}) fusion(bf16[4,80,512]{2,1,0:T(8,128)(2,1)} %collective-permute-done.3, bf16[4,80,512]{2,1,0:T(8,128)(2,1)} %copy-done.4, bf16[4,80,512]{2,1,0:T(8,128)(2,1)} %collective-permute-done.5, pred[]{:T(512)S(6)} %eq.115, pred[]{:T(512)S(6)} %eq.114, ...), kind=kLoop, calls=%fused_computation.13 | loop fusion | flops 1474560 | bytes 1966086 | tf_op jit(solution)/shard_map/stack | solution.py:97
  37.9 1.2 %pad_maximum_fusion.1 = bf16[4,4,80,512]{3,2,0,1:T(8,128)(2,1)} fusion(bf16[4,1,80,512]{3,2,0,1:T(8,128)(2,1)S(1)} %get-tuple-element.8, bf16[4,1,80,512]{3,2,0,1:T(8,128)(2,1)S(1)} %get-tuple-element.10, bf16[4,1,80,512]{3,2,0,1:T(8,128)(2,1)S(1)} %get-tuple-element.9, bf16[4,1,80,512]{3,2,0,1:T(8,128)(2,1)S(1)} %get-tuple-element.7), kind=kLoop, calls=%fused_computation.3 | loop fusion | flops 1966080 | bytes 2621440 | tf_op jit(solution)/shard_map/stack | solution.py:97
  39.1 0.1 collective-permute-start.6
  39.3 3.3 %collective-permute-done.6 = bf16[4,4,80,512]{3,2,0,1:T(8,128)(2,1)} collective-permute-done((bf16[4,4,80,512]{3,2,0,1:T(8,128)(2,1)}, bf16[4,4,80,512]{3,2,0,1:T(8,128)(2,1)}, u32[]{:S(2)}, u32[]{:S(2)}) %collective-permute-start.6) | collective-permute-done | bytes 1310752 | tf_op jit(solution)/shard_map/ppermute | solution.py:105
  42.5 1.6 %broadcast_select_fusion.1 = (bf16[4,4,80,512]{3,2,0,1:T(8,128)(2,1)S(1)}, bf16[4,4,80,512]{3,2,0,1:T(8,128)(2,1)S(1)}) fusion(bf16[4,4,80,512]{3,2,0,1:T(8,128)(2,1)} %collective-permute-done.6, pred[]{:T(512)S(6)} %eq.100, bf16[4,1,80,512]{3,2,0,1:T(8,128)(2,1)S(1)} %get-tuple-element.8, bf16[4,1,80,512]{3,2,0,1:T(8,128)(2,1)S(1)} %get-tuple-element.10, ...), kind=kLoop, calls=%fused_computation.5 | loop fusion | flops 3276800 | bytes 5242881 | tf_op jit(solution)/shard_map/jit(_where)/select_n | solution.py:107
  44.1 0.1 slice_bitcast_fusion
  44.3 0.2 pad_maximum_fusion
  44.5 0.0 slice-start
  44.5 0.2 copy.10
  44.7 0.1 pad_maximum_fusion.2
  44.8 0.0 copy-done
  44.8 0.0 slice-start.1
  44.8 1.3 %fusion = f32[512,2048]{1,0:T(8,128)S(1)} fusion(bf16[512,512]{1,0:T(8,128)(2,1)S(1)} %bitcast.34, bf16[2048,512]{1,0:T(8,128)(2,1)S(1)} %copy-done), kind=kOutput, calls=%fused_computation.23 | convolution fusion | flops 1073741824 | bytes 6815744 | tf_op jit(solution)/shard_map/dot_general | solution.py:71
  46.1 0.5 slice-done
  46.7 1.4 %slice-done.1 = s8[4194304]{0:T(1024)(128)(4,1)S(1)} async-done(((s8[8388608]{0:T(1024)(128)(4,1)}), s8[4194304]{0:T(1024)(128)(4,1)S(1)}, s32[]{:S(2)}) %slice-start.1) | async-done | bytes 4194328
  48.0 4.8 %bitcast_reduce_fusion = f32[2048,16]{0,1:T(8,128)S(1)} fusion(f32[512,2048]{1,0:T(8,128)S(1)} %fusion, bf16[2048,512]{1,0:T(8,128)(2,1)S(1)} %bitcast.35, bf16[2048,2048]{1,0:T(8,128)(2,1)S(1)} %bitcast.37), kind=kOutput, calls=%fused_computation | convolution fusion | flops 4297031680 | bytes 14811136 | tf_op jit(solution)/shard_map/dot_general | solution.py:71
  52.8 0.1 multiply_reduce_fusion
  53.0 11.0 %all_to_all.6 = f32[32,1,16]{2,1,0:T(1,128)S(1)} all-to-all(f32[32,1,16]{2,1,0:T(1,128)S(1)} %broadcast_in_dim.2), channel_id=1, replica_groups=mesh['grp'=1,'tok_o'=4,'tok_m'=4,'tok_c'=2] {'tok_o','tok_m','tok_c'}, dimensions={0} | all-to-all | bytes 4096 | tf_op jit(solution)/shard_map/all_to_all | solution.py:76
  64.0 0.1 reduce_sum.29
  64.1 0.7 %broadcast_divide_fusion = f32[2048,16]{0,1:T(8,128)} fusion(f32[2048,16]{0,1:T(8,128)S(1)} %bitcast_reduce_fusion, f32[16]{0:T(128)S(1)} %add_sqrt_fusion), kind=kLoop, calls=%fused_computation.21 | loop fusion | flops 32768 | bytes 262208 | tf_op jit(solution)/shard_map/div | solution.py:127
  (6 shorter events, 0.1 us)
Async XLA Ops:
  0.0 44.8 %copy-start = (bf16[2048,512]{1,0:T(8,128)(2,1)S(1)}, bf16[2048,512]{1,0:T(8,128)(2,1)}, u32[]{:S(2)}) copy-start(bf16[2048,512]{1,0:T(8,128)(2,1)} %param.6) | copy-start | bytes 6291460
  4.7 8.3 %collective-permute-start.2 = (bf16[80,512]{1,0:T(8,128)(2,1)}, bf16[80,512]{1,0:T(8,128)(2,1)S(1)}, u32[]{:S(2)}, u32[]{:S(2)}) collective-permute-start(bf16[80,512]{1,0:T(8,128)(2,1)} %shard_map.55), channel_id=1, source_target_pairs={{0,8},{8,16},{16,24},{24,0},{1,9},{9,17},{17,25},{25,1},{2,10},{10... | collective-permute-start | bytes 245768 | tf_op jit(solution)/shard_map/ppermute | solution.py:90
  7.8 8.3 %collective-permute-start.1 = (bf16[80,512]{1,0:T(8,128)(2,1)}, bf16[80,512]{1,0:T(8,128)(2,1)S(1)}, u32[]{:S(2)}, u32[]{:S(2)}) collective-permute-start(bf16[80,512]{1,0:T(8,128)(2,1)} %shard_map.55), channel_id=1, source_target_pairs={{0,16},{8,24},{16,0},{24,8},{1,17},{9,25},{17,1},{25,9},{2,18},{10... | collective-permute-start | bytes 245768 | tf_op jit(solution)/shard_map/ppermute | solution.py:90
  10.4 5.9 %collective-permute-start = (bf16[80,512]{1,0:T(8,128)(2,1)}, bf16[80,512]{1,0:T(8,128)(2,1)S(1)}, u32[]{:S(2)}, u32[]{:S(2)}) collective-permute-start(bf16[80,512]{1,0:T(8,128)(2,1)} %shard_map.55), channel_id=1, source_target_pairs={{0,24},{8,0},{16,8},{24,16},{1,25},{9,1},{17,9},{25,17},{2,26},{10... | collective-permute-start | bytes 245768 | tf_op jit(solution)/shard_map/ppermute | solution.py:90
  17.3 17.5 %copy-start.1 = (bf16[1,80,512]{2,1,0:T(8,128)(2,1)}, bf16[1,80,512]{2,1,0:T(8,128)(2,1)S(1)}, u32[]{:S(2)}) copy-start(bf16[1,80,512]{2,1,0:T(8,128)(2,1)S(1)} %get-tuple-element.12) | copy-start | bytes 245764
  17.3 17.5 %copy-start.2 = (bf16[1,80,512]{2,1,0:T(8,128)(2,1)}, bf16[1,80,512]{2,1,0:T(8,128)(2,1)S(1)}, u32[]{:S(2)}) copy-start(bf16[1,80,512]{2,1,0:T(8,128)(2,1)S(1)} %get-tuple-element.13) | copy-start | bytes 245764
  17.3 17.5 %copy-start.3 = (bf16[1,80,512]{2,1,0:T(8,128)(2,1)}, bf16[1,80,512]{2,1,0:T(8,128)(2,1)S(1)}, u32[]{:S(2)}) copy-start(bf16[1,80,512]{2,1,0:T(8,128)(2,1)S(1)} %get-tuple-element.14) | copy-start | bytes 245764
  17.3 11.7 %collective-permute-start.5 = (bf16[4,80,512]{2,1,0:T(8,128)(2,1)S(1)}, bf16[4,80,512]{2,1,0:T(8,128)(2,1)}, u32[]{:S(2)}, u32[]{:S(2)}) collective-permute-start(bf16[4,80,512]{2,1,0:T(8,128)(2,1)S(1)} %pad_maximum_fusion.3), channel_id=1, source_target_pairs={{0,2},{2,4},{4,6},{6,0},{1,3},{3,5},{5,7},{7,1},{8,10},{10,12},{12... | collective-permute-start | bytes 983048 | tf_op jit(solution)/shard_map/ppermute | solution.py:90
  18.9 15.8 %collective-permute-start.4 = (bf16[4,80,512]{2,1,0:T(8,128)(2,1)S(1)}, bf16[4,80,512]{2,1,0:T(8,128)(2,1)S(1)}, u32[]{:S(2)}, u32[]{:S(2)}) collective-permute-start(bf16[4,80,512]{2,1,0:T(8,128)(2,1)S(1)} %pad_maximum_fusion.3), channel_id=1, source_target_pairs={{0,4},{2,6},{4,0},{6,2},{1,5},{3,7},{5,1},{7,3},{8,12},{10,14},{12... | collective-permute-start | bytes 983048 | tf_op jit(solution)/shard_map/ppermute | solution.py:90
  20.4 14.3 %collective-permute-start.3 = (bf16[4,80,512]{2,1,0:T(8,128)(2,1)S(1)}, bf16[4,80,512]{2,1,0:T(8,128)(2,1)}, u32[]{:S(2)}, u32[]{:S(2)}) collective-permute-start(bf16[4,80,512]{2,1,0:T(8,128)(2,1)S(1)} %pad_maximum_fusion.3), channel_id=1, source_target_pairs={{0,6},{2,0},{4,2},{6,4},{1,7},{3,1},{5,3},{7,5},{8,14},{10,8},{12,... | collective-permute-start | bytes 983048 | tf_op jit(solution)/shard_map/ppermute | solution.py:90
  34.6 0.7 %copy-start.4 = (bf16[4,80,512]{2,1,0:T(8,128)(2,1)}, bf16[4,80,512]{2,1,0:T(8,128)(2,1)S(1)}, u32[]{:S(2)}) copy-start(bf16[4,80,512]{2,1,0:T(8,128)(2,1)S(1)} %collective-permute-done.4) | copy-start | bytes 983044
  39.1 3.4 %collective-permute-start.6 = (bf16[4,4,80,512]{3,2,0,1:T(8,128)(2,1)}, bf16[4,4,80,512]{3,2,0,1:T(8,128)(2,1)}, u32[]{:S(2)}, u32[]{:S(2)}) collective-permute-start(bf16[4,4,80,512]{3,2,0,1:T(8,128)(2,1)} %pad_maximum_fusion.1), channel_id=1, source_target_pairs={{0,1},{1,0},{2,3},{3,2},{4,5},{5,4},{6,7},{7,6},{8,9},{9,8},{10,11... | collective-permute-start | bytes 3932168 | tf_op jit(solution)/shard_map/ppermute | solution.py:105
  44.5 2.2 %slice-start = ((s8[8388608]{0:T(1024)(128)(4,1)}), s8[4194304]{0:T(1024)(128)(4,1)S(1)}, s32[]{:S(2)}) async-start(s8[8388608]{0:T(1024)(128)(4,1)} %bitcast.36), calls=%async_computation.1 | async-start | bytes 8388608
  44.8 3.2 %slice-start.1 = ((s8[8388608]{0:T(1024)(128)(4,1)}), s8[4194304]{0:T(1024)(128)(4,1)S(1)}, s32[]{:S(2)}) async-start(s8[8388608]{0:T(1024)(128)(4,1)} %bitcast.36), calls=%async_computation.2 | async-start | bytes 8388608

commit v11 on v9

--- a/solution.py
+++ b/solution.py
@@ -101,8 +101,9 @@
     cols = both.shape[1]
     held = shifted(both, OUTER, 0)
     held = shifted(held, MIDDLE, 1)
-    held = spread(held, CORE, 2)
-    return held[:, :, :, :rows_v].reshape(-1, cols), held[:, :, :, rows_v:].reshape(-1, cols)
+    v_full = spread(held[:, :, :rows_v], CORE, 2)
+    u_full = spread(held[:, :, rows_v:], CORE, 2)
+    return v_full.reshape(-1, cols), u_full.reshape(-1, cols)
 
 
 def on_device(activations, out_grads, v_bank, u_bank, query_ids):

time: 62.9 us -> 73.8 us (1.17)
  matrix products: 6.12 us -> 11.8 us
  starting transfers between devices: 11.5 us -> 16.3 us
  local copies, waits for them, and re-layouts: 2.79 us -> 4.68 us
  blocking collectives: 16.9 us -> 15.3 us
    dot_general x2, matrix products: 6.12 us -> 11.8 us  [folder(): return jnp.dot(left, piece, preferred_element_type=jnp.float32)]
    all_to_all x0 -> x1, starting transfers between devices: none -> 4.81 us  [spread(): return lax.all_to_all(copies, axis, at, at, tiled=True)]
    all_to_all x0 -> x2, local copies, waits for them, and re-layouts: none -> 2 us  [spread(): return lax.all_to_all(copies, axis, at, at, tiled=True)]
    all_to_all x1, blocking collectives: 5.84 us -> 4.15 us  [spread(): return lax.all_to_all(copies, axis, at, at, tiled=True)]
    broadcast_in_dim x1 -> x2, local copies, waits for them, and re-layouts: 0.31 us -> 1.64 us  [spread(): jnp.broadcast_to(jnp.expand_dims(x, at), x.shape[:at] + (k,) + x.shape[at:])]
    unnamed x8 -> x4, local copies, waits for them, and re-layouts: 2.16 us -> 0.86 us
  transfers between devices with their start and end apart: 6 -> 7, of which waited for: 5 -> 5; matrix products, arithmetic and copies ran while one was open for 0% -> 4% of each run, Pallas kernels for 0% -> 0%
where the time goes in v11:
time: 73.8 us; the launch traced here: 73.5 us
  waiting for transfers between devices  17.6 us (24%)
  starting transfers between devices  16.3 us (22%)
  blocking collectives  15.3 us (21%)
  matrix products  11.8 us (16%)
  Pallas kernels  4.73 us (6%)
  local copies, waits for them, and re-layouts  4.68 us (6%)
  other arithmetic  3.01 us (4%)
    ppermute x6, waiting for transfers between devices, shifted(): lax.ppermute(x, axis, [(j, (j + s) % k) for j in range(k)])  17.6 us
    dot_general x2, matrix products, folder(): return jnp.dot(left, piece, preferred_element_type=jnp.float32)  11.8 us
    ppermute x6, starting transfers between devices, shifted(): lax.ppermute(x, axis, [(j, (j + s) % k) for j in range(k)])  11.5 us
    all_to_all x1, blocking collectives, total_over(): return lax.all_to_all(copies, axis, 0, 0, tiled=False).sum(axis=0)  11.1 us
    all_to_all x1, starting transfers between devices, spread(): return lax.all_to_all(copies, axis, at, at, tiled=True)  4.81 us
    pallas_call x1, Pallas kernels, pick_columns(): pl.pallas_call(pick_kernel, out_shape=jax.ShapeDtypeStruct((v_bank.shape[...  4.73 us
    all_to_all x1, blocking collectives, spread(): return lax.all_to_all(copies, axis, at, at, tiled=True)  4.15 us
    another operation x5, other arithmetic, shifted(): return jnp.stack(slots, axis=at)  2.06 us
  transfers between devices with their start and end apart: 7, of which 5 were waited for; matrix products, arithmetic and copies ran while one was open for 4% of the time, Pallas kernels for 0%

profile of v11, /device:TPU:0, one launch (start us, length us, event | category | flops | bytes accessed | tf_op | source)
XLA Modules:
  0.0 73.5 jit_solution(16018355755049668292)
XLA Ops:
  0.0 0.0 copy-start
  0.0 4.7 %shard_map.55 = bf16[80,512]{1,0:T(8,128)(2,1)} custom-call(s32[16]{0:T(128)} %ids_ref.1, bf16[64,65536]{1,0:T(8,128)(2,1)} %v_ref.1, bf16[16,65536]{1,0:T(8,128)(2,1)} %u_ref.1), custom_call_target="tpu_custom_call" | custom-call | tf_op jit(solution)/shard_map/pallas_call | solution.py:47
  4.7 3.1 %collective-permute-start.2 = (bf16[80,512]{1,0:T(8,128)(2,1)}, bf16[80,512]{1,0:T(8,128)(2,1)S(1)}, u32[]{:S(2)}, u32[]{:S(2)}) collective-permute-start(bf16[80,512]{1,0:T(8,128)(2,1)} %shard_map.55), channel_id=1, source_target_pairs={{0,8},{8,16},{16,24},{24,0},{1,9},{9,17},{17,25},{25,1},{2,10},{10... | collective-permute-start | bytes 245768 | tf_op jit(solution)/shard_map/ppermute | solution.py:90
  7.8 2.6 %collective-permute-start.1 = (bf16[80,512]{1,0:T(8,128)(2,1)}, bf16[80,512]{1,0:T(8,128)(2,1)S(1)}, u32[]{:S(2)}, u32[]{:S(2)}) collective-permute-start(bf16[80,512]{1,0:T(8,128)(2,1)} %shard_map.55), channel_id=1, source_target_pairs={{0,16},{8,24},{16,0},{24,8},{1,17},{9,25},{17,1},{25,9},{2,18},{10... | collective-permute-start | bytes 245768 | tf_op jit(solution)/shard_map/ppermute | solution.py:90
  10.4 1.3 %collective-permute-start = (bf16[80,512]{1,0:T(8,128)(2,1)}, bf16[80,512]{1,0:T(8,128)(2,1)S(1)}, u32[]{:S(2)}, u32[]{:S(2)}) collective-permute-start(bf16[80,512]{1,0:T(8,128)(2,1)} %shard_map.55), channel_id=1, source_target_pairs={{0,24},{8,0},{16,8},{24,16},{1,25},{9,1},{17,9},{25,17},{2,26},{10... | collective-permute-start | bytes 245768 | tf_op jit(solution)/shard_map/ppermute | solution.py:90
  11.8 1.3 %collective-permute-done.2 = bf16[80,512]{1,0:T(8,128)(2,1)S(1)} collective-permute-done((bf16[80,512]{1,0:T(8,128)(2,1)}, bf16[80,512]{1,0:T(8,128)(2,1)S(1)}, u32[]{:S(2)}, u32[]{:S(2)}) %collective-permute-start.2) | collective-permute-done | bytes 81952 | tf_op jit(solution)/shard_map/ppermute | solution.py:90
  13.1 3.0 %collective-permute-done.1 = bf16[80,512]{1,0:T(8,128)(2,1)S(1)} collective-permute-done((bf16[80,512]{1,0:T(8,128)(2,1)}, bf16[80,512]{1,0:T(8,128)(2,1)S(1)}, u32[]{:S(2)}, u32[]{:S(2)}) %collective-permute-start.1) | collective-permute-done | bytes 81952 | tf_op jit(solution)/shard_map/ppermute | solution.py:90
  16.1 0.2 collective-permute-done
  16.3 0.9 %select_bitcast_fusion.7 = (bf16[1,80,512]{2,1,0:T(8,128)(2,1)S(1)}, bf16[1,80,512]{2,1,0:T(8,128)(2,1)S(1)}, bf16[1,80,512]{2,1,0:T(8,128)(2,1)S(1)}, bf16[1,80,512]{2,1,0:T(8,128)(2,1)S(1)}) fusion(bf16[80,512]{1,0:T(8,128)(2,1)S(1)} %collective-permute-done, bf16[80,512]{1,0:T(8,128)(2,1)S(1)} %collective-permute-done.1, ...), kind=kLoop, calls=%fused_computation.13 | loop fusion | flops 491520 | bytes 655372 | tf_op jit(solution)/shard_map/stack | solution.py:97
  17.3 0.8 %pad_maximum_fusion.1 = bf16[4,80,512]{2,1,0:T(8,128)(2,1)} fusion(bf16[1,80,512]{2,1,0:T(8,128)(2,1)S(1)} %get-tuple-element.10, bf16[1,80,512]{2,1,0:T(8,128)(2,1)S(1)} %get-tuple-element.11, bf16[1,80,512]{2,1,0:T(8,128)(2,1)S(1)} %get-tuple-element.12, bf16[1,80,512]{2,1,0:T(8,128)(2,1)S(1)} %get-tuple-element.9), kind=kLoop, calls=%fused_computation.3 | loop fusion | flops 491520 | bytes 655360 | tf_op jit(solution)/shard_map/stack | solution.py:97
  18.0 1.5 %collective-permute-start.5 = (bf16[4,80,512]{2,1,0:T(8,128)(2,1)}, bf16[4,80,512]{2,1,0:T(8,128)(2,1)S(1)}, u32[]{:S(2)}, u32[]{:S(2)}) collective-permute-start(bf16[4,80,512]{2,1,0:T(8,128)(2,1)} %pad_maximum_fusion.1), channel_id=1, source_target_pairs={{0,2},{2,4},{4,6},{6,0},{1,3},{3,5},{5,7},{7,1},{8,10},{10,12},{12... | collective-permute-start | bytes 983048 | tf_op jit(solution)/shard_map/ppermute | solution.py:90
  19.5 1.5 %collective-permute-start.4 = (bf16[4,80,512]{2,1,0:T(8,128)(2,1)}, bf16[4,80,512]{2,1,0:T(8,128)(2,1)S(1)}, u32[]{:S(2)}, u32[]{:S(2)}) collective-permute-start(bf16[4,80,512]{2,1,0:T(8,128)(2,1)} %pad_maximum_fusion.1), channel_id=1, source_target_pairs={{0,4},{2,6},{4,0},{6,2},{1,5},{3,7},{5,1},{7,3},{8,12},{10,14},{12... | collective-permute-start | bytes 983048 | tf_op jit(solution)/shard_map/ppermute | solution.py:90
  21.0 1.4 %collective-permute-start.3 = (bf16[4,80,512]{2,1,0:T(8,128)(2,1)}, bf16[4,80,512]{2,1,0:T(8,128)(2,1)S(1)}, u32[]{:S(2)}, u32[]{:S(2)}) collective-permute-start(bf16[4,80,512]{2,1,0:T(8,128)(2,1)} %pad_maximum_fusion.1), channel_id=1, source_target_pairs={{0,6},{2,0},{4,2},{6,4},{1,7},{3,1},{5,3},{7,5},{8,14},{10,8},{12,... | collective-permute-start | bytes 983048 | tf_op jit(solution)/shard_map/ppermute | solution.py:90
  22.5 7.3 %collective-permute-done.5 = bf16[4,80,512]{2,1,0:T(8,128)(2,1)S(1)} collective-permute-done((bf16[4,80,512]{2,1,0:T(8,128)(2,1)}, bf16[4,80,512]{2,1,0:T(8,128)(2,1)S(1)}, u32[]{:S(2)}, u32[]{:S(2)}) %collective-permute-start.5) | collective-permute-done | bytes 327712 | tf_op jit(solution)/shard_map/ppermute | solution.py:90
  29.8 5.7 %collective-permute-done.4 = bf16[4,80,512]{2,1,0:T(8,128)(2,1)S(1)} collective-permute-done((bf16[4,80,512]{2,1,0:T(8,128)(2,1)}, bf16[4,80,512]{2,1,0:T(8,128)(2,1)S(1)}, u32[]{:S(2)}, u32[]{:S(2)}) %collective-permute-start.4) | collective-permute-done | bytes 327712 | tf_op jit(solution)/shard_map/ppermute | solution.py:90
  35.5 0.0 collective-permute-done.3
  35.5 0.1 select_bitcast_fusion.2
  35.6 0.1 select_bitcast_fusion.3
  35.7 0.2 pad_maximum_fusion
  35.9 0.1 slice.8
  36.0 0.1 copy.18
  36.1 0.1 broadcast_in_dim.7
  36.1 4.2 %all_to_all.16 = bf16[4,4,2,16,512]{4,3,1,0,2:T(8,128)(2,1)S(1)} all-to-all(bf16[4,4,2,16,512]{4,3,1,0,2:T(8,128)(2,1)S(1)} %broadcast_in_dim.7), channel_id=1, replica_groups=mesh['grp'=1,'tok_o'=4,'tok_m'=4,'tok_c'=2] {'tok_c'}, dimensions={2} | all-to-all | bytes 1048576 | tf_op jit(solution)/shard_map/all_to_all | solution.py:82
  40.3 1.6 %broadcast_in_dim.6 = bf16[4,4,2,64,512]{4,3,1,0,2:T(8,128)(2,1)} broadcast(bf16[4,4,64,512]{3,2,1,0:T(8,128)(2,1)S(1)} %copy.18), dimensions={0,1,3,4} | broadcast | bytes 3145728 | tf_op jit(solution)/shard_map/broadcast_in_dim | solution.py:81
  41.9 4.8 %all-to-all-start = ((bf16[4,4,2,64,512]{4,3,1,0,2:T(8,128)(2,1)}), bf16[4,4,2,64,512]{4,3,1,0,2:T(8,128)(2,1)}, u32[]{:S(2)}, u32[]{:S(2)}) async-start(bf16[4,4,2,64,512]{4,3,1,0,2:T(8,128)(2,1)} %broadcast_in_dim.6), calls=%async_computation | async-start | bytes 4194304 | tf_op jit(solution)/shard_map/all_to_all | solution.py:82
  46.8 0.0 copy-done
  46.8 3.2 %fusion = f32[512,2048]{1,0:T(8,128)} fusion(bf16[512,512]{1,0:T(8,128)(2,1)S(1)} %bitcast.26, bf16[2048,512]{1,0:T(8,128)(2,1)S(1)} %copy-done), kind=kOutput, calls=%fused_computation.16 | convolution fusion | flops 1073741824 | bytes 6815744 | tf_op jit(solution)/shard_map/dot_general | solution.py:71
  50.0 0.0 all-to-all-done
  50.0 0.0 copy-start.1
  50.0 2.0 %copy.19 = bf16[4,4,2,64,512]{4,3,2,1,0:T(8,128)(2,1)S(1)} copy(bf16[4,4,2,64,512]{4,3,1,0,2:T(8,128)(2,1)} %all-to-all-done) | data formatting | bytes 4194304 | tf_op jit(solution)/shard_map/all_to_all | solution.py:82
  52.0 0.9 %copy-done.1 = f32[512,2048]{1,0:T(8,128)S(1)} copy-done((f32[512,2048]{1,0:T(8,128)S(1)}, f32[512,2048]{1,0:T(8,128)}, u32[]{:S(2)}) %copy-start.1) | copy-done | bytes 4194328
  52.8 8.5 %bitcast_reduce_fusion = f32[2048,16]{0,1:T(8,128)S(1)} fusion(f32[512,2048]{1,0:T(8,128)S(1)} %copy-done.1, bf16[2048,512]{1,0:T(8,128)(2,1)S(1)} %bitcast.27, bf16[2048,2048]{1,0:T(8,128)(2,1)} %param.5), kind=kOutput, calls=%fused_computation | convolution fusion | flops 4297031680 | bytes 14811136 | tf_op jit(solution)/shard_map/dot_general | solution.py:71
  61.4 0.1 multiply_reduce_fusion
  61.5 11.1 %all_to_all.17 = f32[32,1,16]{2,1,0:T(1,128)S(1)} all-to-all(f32[32,1,16]{2,1,0:T(1,128)S(1)} %broadcast_in_dim.8), channel_id=1, replica_groups=mesh['grp'=1,'tok_o'=4,'tok_m'=4,'tok_c'=2] {'tok_o','tok_m','tok_c'}, dimensions={0} | all-to-all | bytes 4096 | tf_op jit(solution)/shard_map/all_to_all | solution.py:76
  72.6 0.1 reduce_sum.29
  72.7 0.7 %broadcast_divide_fusion = f32[2048,16]{0,1:T(8,128)} fusion(f32[2048,16]{0,1:T(8,128)S(1)} %bitcast_reduce_fusion, f32[16]{0:T(128)S(1)} %add_sqrt_fusion), kind=kLoop, calls=%fused_computation.14 | loop fusion | flops 32768 | bytes 262208 | tf_op jit(solution)/shard_map/div | solution.py:120
  (5 shorter events, 0.1 us)
Async XLA Ops:
  0.0 46.8 %copy-start = (bf16[2048,512]{1,0:T(8,128)(2,1)S(1)}, bf16[2048,512]{1,0:T(8,128)(2,1)}, u32[]{:S(2)}) copy-start(bf16[2048,512]{1,0:T(8,128)(2,1)} %param.6) | copy-start | bytes 6291460
  4.7 8.3 %collective-permute-start.2 = (bf16[80,512]{1,0:T(8,128)(2,1)}, bf16[80,512]{1,0:T(8,128)(2,1)S(1)}, u32[]{:S(2)}, u32[]{:S(2)}) collective-permute-start(bf16[80,512]{1,0:T(8,128)(2,1)} %shard_map.55), channel_id=1, source_target_pairs={{0,8},{8,16},{16,24},{24,0},{1,9},{9,17},{17,25},{25,1},{2,10},{10... | collective-permute-start | bytes 245768 | tf_op jit(solution)/shard_map/ppermute | solution.py:90
  7.8 8.3 %collective-permute-start.1 = (bf16[80,512]{1,0:T(8,128)(2,1)}, bf16[80,512]{1,0:T(8,128)(2,1)S(1)}, u32[]{:S(2)}, u32[]{:S(2)}) collective-permute-start(bf16[80,512]{1,0:T(8,128)(2,1)} %shard_map.55), channel_id=1, source_target_pairs={{0,16},{8,24},{16,0},{24,8},{1,17},{9,25},{17,1},{25,9},{2,18},{10... | collective-permute-start | bytes 245768 | tf_op jit(solution)/shard_map/ppermute | solution.py:90
  10.4 5.9 %collective-permute-start = (bf16[80,512]{1,0:T(8,128)(2,1)}, bf16[80,512]{1,0:T(8,128)(2,1)S(1)}, u32[]{:S(2)}, u32[]{:S(2)}) collective-permute-start(bf16[80,512]{1,0:T(8,128)(2,1)} %shard_map.55), channel_id=1, source_target_pairs={{0,24},{8,0},{16,8},{24,16},{1,25},{9,1},{17,9},{25,17},{2,26},{10... | collective-permute-start | bytes 245768 | tf_op jit(solution)/shard_map/ppermute | solution.py:90
  18.0 11.8 %collective-permute-start.5 = (bf16[4,80,512]{2,1,0:T(8,128)(2,1)}, bf16[4,80,512]{2,1,0:T(8,128)(2,1)S(1)}, u32[]{:S(2)}, u32[]{:S(2)}) collective-permute-start(bf16[4,80,512]{2,1,0:T(8,128)(2,1)} %pad_maximum_fusion.1), channel_id=1, source_target_pairs={{0,2},{2,4},{4,6},{6,0},{1,3},{3,5},{5,7},{7,1},{8,10},{10,12},{12... | collective-permute-start | bytes 983048 | tf_op jit(solution)/shard_map/ppermute | solution.py:90
  19.5 16.0 %collective-permute-start.4 = (bf16[4,80,512]{2,1,0:T(8,128)(2,1)}, bf16[4,80,512]{2,1,0:T(8,128)(2,1)S(1)}, u32[]{:S(2)}, u32[]{:S(2)}) collective-permute-start(bf16[4,80,512]{2,1,0:T(8,128)(2,1)} %pad_maximum_fusion.1), channel_id=1, source_target_pairs={{0,4},{2,6},{4,0},{6,2},{1,5},{3,7},{5,1},{7,3},{8,12},{10,14},{12... | collective-permute-start | bytes 983048 | tf_op jit(solution)/shard_map/ppermute | solution.py:90
  21.0 14.5 %collective-permute-start.3 = (bf16[4,80,512]{2,1,0:T(8,128)(2,1)}, bf16[4,80,512]{2,1,0:T(8,128)(2,1)S(1)}, u32[]{:S(2)}, u32[]{:S(2)}) collective-permute-start(bf16[4,80,512]{2,1,0:T(8,128)(2,1)} %pad_maximum_fusion.1), channel_id=1, source_target_pairs={{0,6},{2,0},{4,2},{6,4},{1,7},{3,1},{5,3},{7,5},{8,14},{10,8},{12,... | collective-permute-start | bytes 983048 | tf_op jit(solution)/shard_map/ppermute | solution.py:90
  41.9 8.1 %all-to-all-start = ((bf16[4,4,2,64,512]{4,3,1,0,2:T(8,128)(2,1)}), bf16[4,4,2,64,512]{4,3,1,0,2:T(8,128)(2,1)}, u32[]{:S(2)}, u32[]{:S(2)}) async-start(bf16[4,4,2,64,512]{4,3,1,0,2:T(8,128)(2,1)} %broadcast_in_dim.6), calls=%async_computation | async-start | bytes 4194304 | tf_op jit(solution)/shard_map/all_to_all | solution.py:82
  50.0 2.8 %copy-start.1 = (f32[512,2048]{1,0:T(8,128)S(1)}, f32[512,2048]{1,0:T(8,128)}, u32[]{:S(2)}) copy-start(f32[512,2048]{1,0:T(8,128)} %fusion) | copy-start | bytes 12582916

commit v12 on v9

--- a/solution.py
+++ b/solution.py
@@ -114,7 +114,9 @@
     proj_in = folder(activations, v_full)
     proj_out = folder(out_grads, u_full)
     scores = (proj_in * proj_out).reshape(tok_rows, queries, RANK).sum(axis=2)
-    total = total_over(jnp.sum(scores * scores, axis=0), TOK, n)
+    part = jnp.sum(scores * scores, axis=0)
+    part = part + lax.ppermute(part, CORE, [(0, 1), (1, 0)])
+    total = total_over(part, (OUTER, MIDDLE), n // lax.axis_size(CORE))
     scale = jnp.sqrt(total / (tok_rows * n) + 1e-06)
     return scores / scale[None, :]
 

time: 62.9 us -> 65.2 us (1.037)
  blocking collectives: 16.9 us -> 18 us
  waiting for transfers between devices: 17.6 us -> 18.6 us
    all_to_all x1, blocking collectives: 11 us -> 12.2 us  [total_over(): return lax.all_to_all(copies, axis, 0, 0, tiled=False).sum(axis=0)]
    ppermute x0 -> x1, waiting for transfers between devices: none -> 0.98 us  [on_device(): part = part + lax.ppermute(part, CORE, [(0, 1), (1, 0)])]
  transfers between devices with their start and end apart: 6 -> 7, of which waited for: 5 -> 6; matrix products, arithmetic and copies ran while one was open for 0% -> 0% of each run, Pallas kernels for 0% -> 0%
where the time goes in v12:
time: 65.2 us; the launch traced here: 65 us
  waiting for transfers between devices  18.6 us (29%)
  blocking collectives  18 us (28%)
  starting transfers between devices  11.7 us (18%)
  matrix products  6.12 us (9%)
  Pallas kernels  4.73 us (7%)
  other arithmetic  2.99 us (5%)
  local copies, waits for them, and re-layouts  2.79 us (4%)
    ppermute x6, waiting for transfers between devices, shifted(): lax.ppermute(x, axis, [(j, (j + s) % k) for j in range(k)])  17.6 us
    all_to_all x1, blocking collectives, total_over(): return lax.all_to_all(copies, axis, 0, 0, tiled=False).sum(axis=0)  12.2 us
    ppermute x6, starting transfers between devices, shifted(): lax.ppermute(x, axis, [(j, (j + s) % k) for j in range(k)])  11.5 us
    dot_general x2, matrix products, folder(): return jnp.dot(left, piece, preferred_element_type=jnp.float32)  6.12 us
    all_to_all x1, blocking collectives, spread(): return lax.all_to_all(copies, axis, at, at, tiled=True)  5.84 us
    pallas_call x1, Pallas kernels, pick_columns(): pl.pallas_call(pick_kernel, out_shape=jax.ShapeDtypeStruct((v_bank.shape[...  4.73 us
    unnamed x8, local copies, waits for them, and re-layouts  2.16 us
    another operation x5, other arithmetic, shifted(): return jnp.stack(slots, axis=at)  2.08 us
  transfers between devices with their start and end apart: 7, of which 6 were waited for; matrix products, arithmetic and copies ran while one was open for 0% of the time, Pallas kernels for 0%

profile of v12, /device:TPU:0, one launch (start us, length us, event | category | flops | bytes accessed | tf_op | source)
XLA Modules:
  0.0 65.0 jit_solution(3090308493496779587)
XLA Ops:
  0.0 0.0 copy-start
  0.0 4.7 %shard_map.55 = bf16[80,512]{1,0:T(8,128)(2,1)} custom-call(s32[16]{0:T(128)} %ids_ref.1, bf16[64,65536]{1,0:T(8,128)(2,1)} %v_ref.1, bf16[16,65536]{1,0:T(8,128)(2,1)} %u_ref.1), custom_call_target="tpu_custom_call" | custom-call | tf_op jit(solution)/shard_map/pallas_call | solution.py:47
  4.7 3.1 %collective-permute-start.2 = (bf16[80,512]{1,0:T(8,128)(2,1)}, bf16[80,512]{1,0:T(8,128)(2,1)S(1)}, u32[]{:S(2)}, u32[]{:S(2)}) collective-permute-start(bf16[80,512]{1,0:T(8,128)(2,1)} %shard_map.55), channel_id=1, source_target_pairs={{0,8},{8,16},{16,24},{24,0},{1,9},{9,17},{17,25},{25,1},{2,10},{10... | collective-permute-start | bytes 245768 | tf_op jit(solution)/shard_map/ppermute | solution.py:90
  7.8 2.6 %collective-permute-start.1 = (bf16[80,512]{1,0:T(8,128)(2,1)}, bf16[80,512]{1,0:T(8,128)(2,1)S(1)}, u32[]{:S(2)}, u32[]{:S(2)}) collective-permute-start(bf16[80,512]{1,0:T(8,128)(2,1)} %shard_map.55), channel_id=1, source_target_pairs={{0,16},{8,24},{16,0},{24,8},{1,17},{9,25},{17,1},{25,9},{2,18},{10... | collective-permute-start | bytes 245768 | tf_op jit(solution)/shard_map/ppermute | solution.py:90
  10.4 1.3 %collective-permute-start = (bf16[80,512]{1,0:T(8,128)(2,1)}, bf16[80,512]{1,0:T(8,128)(2,1)S(1)}, u32[]{:S(2)}, u32[]{:S(2)}) collective-permute-start(bf16[80,512]{1,0:T(8,128)(2,1)} %shard_map.55), channel_id=1, source_target_pairs={{0,24},{8,0},{16,8},{24,16},{1,25},{9,1},{17,9},{25,17},{2,26},{10... | collective-permute-start | bytes 245768 | tf_op jit(solution)/shard_map/ppermute | solution.py:90
  11.8 1.3 %collective-permute-done.2 = bf16[80,512]{1,0:T(8,128)(2,1)S(1)} collective-permute-done((bf16[80,512]{1,0:T(8,128)(2,1)}, bf16[80,512]{1,0:T(8,128)(2,1)S(1)}, u32[]{:S(2)}, u32[]{:S(2)}) %collective-permute-start.2) | collective-permute-done | bytes 81952 | tf_op jit(solution)/shard_map/ppermute | solution.py:90
  13.1 3.0 %collective-permute-done.1 = bf16[80,512]{1,0:T(8,128)(2,1)S(1)} collective-permute-done((bf16[80,512]{1,0:T(8,128)(2,1)}, bf16[80,512]{1,0:T(8,128)(2,1)S(1)}, u32[]{:S(2)}, u32[]{:S(2)}) %collective-permute-start.1) | collective-permute-done | bytes 81952 | tf_op jit(solution)/shard_map/ppermute | solution.py:90
  16.1 0.2 collective-permute-done
  16.3 0.9 %select_bitcast_fusion.7 = (bf16[1,80,512]{2,1,0:T(8,128)(2,1)S(1)}, bf16[1,80,512]{2,1,0:T(8,128)(2,1)S(1)}, bf16[1,80,512]{2,1,0:T(8,128)(2,1)S(1)}, bf16[1,80,512]{2,1,0:T(8,128)(2,1)S(1)}) fusion(bf16[80,512]{1,0:T(8,128)(2,1)S(1)} %collective-permute-done, bf16[80,512]{1,0:T(8,128)(2,1)S(1)} %collective-permute-done.1, ...), kind=kLoop, calls=%fused_computation.12 | loop fusion | flops 491520 | bytes 655372 | tf_op jit(solution)/shard_map/stack | solution.py:97
  17.3 0.8 %pad_maximum_fusion.1 = bf16[4,80,512]{2,1,0:T(8,128)(2,1)} fusion(bf16[1,80,512]{2,1,0:T(8,128)(2,1)S(1)} %get-tuple-element.10, bf16[1,80,512]{2,1,0:T(8,128)(2,1)S(1)} %get-tuple-element.11, bf16[1,80,512]{2,1,0:T(8,128)(2,1)S(1)} %get-tuple-element.12, bf16[1,80,512]{2,1,0:T(8,128)(2,1)S(1)} %get-tuple-element.9), kind=kLoop, calls=%fused_computation.3 | loop fusion | flops 491520 | bytes 655360 | tf_op jit(solution)/shard_map/stack | solution.py:97
  18.0 1.5 %collective-permute-start.5 = (bf16[4,80,512]{2,1,0:T(8,128)(2,1)}, bf16[4,80,512]{2,1,0:T(8,128)(2,1)S(1)}, u32[]{:S(2)}, u32[]{:S(2)}) collective-permute-start(bf16[4,80,512]{2,1,0:T(8,128)(2,1)} %pad_maximum_fusion.1), channel_id=1, source_target_pairs={{0,2},{2,4},{4,6},{6,0},{1,3},{3,5},{5,7},{7,1},{8,10},{10,12},{12... | collective-permute-start | bytes 983048 | tf_op jit(solution)/shard_map/ppermute | solution.py:90
  19.5 1.5 %collective-permute-start.4 = (bf16[4,80,512]{2,1,0:T(8,128)(2,1)}, bf16[4,80,512]{2,1,0:T(8,128)(2,1)S(1)}, u32[]{:S(2)}, u32[]{:S(2)}) collective-permute-start(bf16[4,80,512]{2,1,0:T(8,128)(2,1)} %pad_maximum_fusion.1), channel_id=1, source_target_pairs={{0,4},{2,6},{4,0},{6,2},{1,5},{3,7},{5,1},{7,3},{8,12},{10,14},{12... | collective-permute-start | bytes 983048 | tf_op jit(solution)/shard_map/ppermute | solution.py:90
  21.0 1.4 %collective-permute-start.3 = (bf16[4,80,512]{2,1,0:T(8,128)(2,1)}, bf16[4,80,512]{2,1,0:T(8,128)(2,1)S(1)}, u32[]{:S(2)}, u32[]{:S(2)}) collective-permute-start(bf16[4,80,512]{2,1,0:T(8,128)(2,1)} %pad_maximum_fusion.1), channel_id=1, source_target_pairs={{0,6},{2,0},{4,2},{6,4},{1,7},{3,1},{5,3},{7,5},{8,14},{10,8},{12,... | collective-permute-start | bytes 983048 | tf_op jit(solution)/shard_map/ppermute | solution.py:90
  22.5 7.3 %collective-permute-done.5 = bf16[4,80,512]{2,1,0:T(8,128)(2,1)S(1)} collective-permute-done((bf16[4,80,512]{2,1,0:T(8,128)(2,1)}, bf16[4,80,512]{2,1,0:T(8,128)(2,1)S(1)}, u32[]{:S(2)}, u32[]{:S(2)}) %collective-permute-start.5) | collective-permute-done | bytes 327712 | tf_op jit(solution)/shard_map/ppermute | solution.py:90
  29.8 5.7 %collective-permute-done.4 = bf16[4,80,512]{2,1,0:T(8,128)(2,1)S(1)} collective-permute-done((bf16[4,80,512]{2,1,0:T(8,128)(2,1)}, bf16[4,80,512]{2,1,0:T(8,128)(2,1)S(1)}, u32[]{:S(2)}, u32[]{:S(2)}) %collective-permute-start.4) | collective-permute-done | bytes 327712 | tf_op jit(solution)/shard_map/ppermute | solution.py:90
  35.5 0.0 collective-permute-done.3
  35.5 0.1 select_bitcast_fusion.2
  35.6 0.1 select_bitcast_fusion.3
  35.7 0.2 pad_maximum_fusion
  35.9 0.1 copy.14
  36.0 0.3 broadcast_in_dim.4
  36.3 5.8 %all_to_all.11 = bf16[4,4,2,80,512]{4,3,1,0,2:T(8,128)(2,1)S(1)} all-to-all(bf16[4,4,2,80,512]{4,3,1,0,2:T(8,128)(2,1)S(1)} %broadcast_in_dim.4), channel_id=1, replica_groups=mesh['grp'=1,'tok_o'=4,'tok_m'=4,'tok_c'=2] {'tok_c'}, dimensions={2} | all-to-all | bytes 5242880 | tf_op jit(solution)/shard_map/all_to_all | solution.py:82
  42.2 0.2 slice.8
  42.3 0.0 slice-start
  42.3 0.2 copy.18
  42.7 0.0 copy-done
  42.7 0.0 slice-start.1
  42.7 1.3 %fusion = f32[512,2048]{1,0:T(8,128)S(1)} fusion(bf16[512,512]{1,0:T(8,128)(2,1)S(1)} %bitcast.27, bf16[2048,512]{1,0:T(8,128)(2,1)S(1)} %copy-done), kind=kOutput, calls=%fused_computation.15 | convolution fusion | flops 1073741824 | bytes 6815744 | tf_op jit(solution)/shard_map/dot_general | solution.py:71
  44.0 0.5 slice-done
  44.5 1.4 %slice-done.1 = s8[4194304]{0:T(1024)(128)(4,1)S(1)} async-done(((s8[8388608]{0:T(1024)(128)(4,1)}), s8[4194304]{0:T(1024)(128)(4,1)S(1)}, s32[]{:S(2)}) %slice-start.1) | async-done | bytes 4194328
  45.9 4.8 %bitcast_reduce_fusion = f32[2048,16]{0,1:T(8,128)S(1)} fusion(f32[512,2048]{1,0:T(8,128)S(1)} %fusion, bf16[2048,512]{1,0:T(8,128)(2,1)S(1)} %bitcast.28, bf16[2048,2048]{1,0:T(8,128)(2,1)S(1)} %bitcast.31), kind=kOutput, calls=%fused_computation | convolution fusion | flops 4297031680 | bytes 14811136 | tf_op jit(solution)/shard_map/dot_general | solution.py:71
  50.7 0.1 multiply_reduce_fusion
  50.8 0.2 collective-permute-start.6
  51.0 1.0 %collective-permute-done.6 = f32[16]{0:T(128)S(1)} collective-permute-done((f32[16]{0:T(128)S(1)}, f32[16]{0:T(128)S(1)}, u32[]{:S(2)}, u32[]{:S(2)}) %collective-permute-start.6) | collective-permute-done | bytes 96 | tf_op jit(solution)/shard_map/ppermute | solution.py:118
  52.0 12.2 %all_to_all.12 = f32[16,1,16]{2,1,0:T(1,128)S(1)} all-to-all(f32[16,1,16]{2,1,0:T(1,128)S(1)} %broadcast_in_dim.5), channel_id=1, replica_groups=mesh['grp'=1,'tok_o'=4,'tok_m'=4,'tok_c'=2] {'tok_o','tok_m'}, dimensions={0} | all-to-all | bytes 2048 | tf_op jit(solution)/shard_map/all_to_all | solution.py:76
  64.2 0.7 %broadcast_divide_fusion = f32[2048,16]{0,1:T(8,128)} fusion(f32[2048,16]{0,1:T(8,128)S(1)} %bitcast_reduce_fusion, f32[16]{0:T(128)S(1)} %add_sqrt_fusion), kind=kLoop, calls=%fused_computation.13 | loop fusion | flops 32768 | bytes 262208 | tf_op jit(solution)/shard_map/div | solution.py:121
  (7 shorter events, 0.1 us)
Async XLA Ops:
  0.0 42.7 %copy-start = (bf16[2048,512]{1,0:T(8,128)(2,1)S(1)}, bf16[2048,512]{1,0:T(8,128)(2,1)}, u32[]{:S(2)}) copy-start(bf16[2048,512]{1,0:T(8,128)(2,1)} %param.6) | copy-start | bytes 6291460
  4.7 8.3 %collective-permute-start.2 = (bf16[80,512]{1,0:T(8,128)(2,1)}, bf16[80,512]{1,0:T(8,128)(2,1)S(1)}, u32[]{:S(2)}, u32[]{:S(2)}) collective-permute-start(bf16[80,512]{1,0:T(8,128)(2,1)} %shard_map.55), channel_id=1, source_target_pairs={{0,8},{8,16},{16,24},{24,0},{1,9},{9,17},{17,25},{25,1},{2,10},{10... | collective-permute-start | bytes 245768 | tf_op jit(solution)/shard_map/ppermute | solution.py:90
  7.8 8.3 %collective-permute-start.1 = (bf16[80,512]{1,0:T(8,128)(2,1)}, bf16[80,512]{1,0:T(8,128)(2,1)S(1)}, u32[]{:S(2)}, u32[]{:S(2)}) collective-permute-start(bf16[80,512]{1,0:T(8,128)(2,1)} %shard_map.55), channel_id=1, source_target_pairs={{0,16},{8,24},{16,0},{24,8},{1,17},{9,25},{17,1},{25,9},{2,18},{10... | collective-permute-start | bytes 245768 | tf_op jit(solution)/shard_map/ppermute | solution.py:90
  10.4 5.9 %collective-permute-start = (bf16[80,512]{1,0:T(8,128)(2,1)}, bf16[80,512]{1,0:T(8,128)(2,1)S(1)}, u32[]{:S(2)}, u32[]{:S(2)}) collective-permute-start(bf16[80,512]{1,0:T(8,128)(2,1)} %shard_map.55), channel_id=1, source_target_pairs={{0,24},{8,0},{16,8},{24,16},{1,25},{9,1},{17,9},{25,17},{2,26},{10... | collective-permute-start | bytes 245768 | tf_op jit(solution)/shard_map/ppermute | solution.py:90
  18.0 11.8 %collective-permute-start.5 = (bf16[4,80,512]{2,1,0:T(8,128)(2,1)}, bf16[4,80,512]{2,1,0:T(8,128)(2,1)S(1)}, u32[]{:S(2)}, u32[]{:S(2)}) collective-permute-start(bf16[4,80,512]{2,1,0:T(8,128)(2,1)} %pad_maximum_fusion.1), channel_id=1, source_target_pairs={{0,2},{2,4},{4,6},{6,0},{1,3},{3,5},{5,7},{7,1},{8,10},{10,12},{12... | collective-permute-start | bytes 983048 | tf_op jit(solution)/shard_map/ppermute | solution.py:90
  19.5 16.0 %collective-permute-start.4 = (bf16[4,80,512]{2,1,0:T(8,128)(2,1)}, bf16[4,80,512]{2,1,0:T(8,128)(2,1)S(1)}, u32[]{:S(2)}, u32[]{:S(2)}) collective-permute-start(bf16[4,80,512]{2,1,0:T(8,128)(2,1)} %pad_maximum_fusion.1), channel_id=1, source_target_pairs={{0,4},{2,6},{4,0},{6,2},{1,5},{3,7},{5,1},{7,3},{8,12},{10,14},{12... | collective-permute-start | bytes 983048 | tf_op jit(solution)/shard_map/ppermute | solution.py:90
  21.0 14.5 %collective-permute-start.3 = (bf16[4,80,512]{2,1,0:T(8,128)(2,1)}, bf16[4,80,512]{2,1,0:T(8,128)(2,1)S(1)}, u32[]{:S(2)}, u32[]{:S(2)}) collective-permute-start(bf16[4,80,512]{2,1,0:T(8,128)(2,1)} %pad_maximum_fusion.1), channel_id=1, source_target_pairs={{0,6},{2,0},{4,2},{6,4},{1,7},{3,1},{5,3},{7,5},{8,14},{10,8},{12,... | collective-permute-start | bytes 983048 | tf_op jit(solution)/shard_map/ppermute | solution.py:90
  42.3 2.2 %slice-start = ((s8[8388608]{0:T(1024)(128)(4,1)}), s8[4194304]{0:T(1024)(128)(4,1)S(1)}, s32[]{:S(2)}) async-start(s8[8388608]{0:T(1024)(128)(4,1)} %bitcast.30), calls=%async_computation.2 | async-start | bytes 8388608
  42.7 3.2 %slice-start.1 = ((s8[8388608]{0:T(1024)(128)(4,1)}), s8[4194304]{0:T(1024)(128)(4,1)S(1)}, s32[]{:S(2)}) async-start(s8[8388608]{0:T(1024)(128)(4,1)} %bitcast.30), calls=%async_computation.3 | async-start | bytes 8388608
  50.8 1.2 %collective-permute-start.6 = (f32[16]{0:T(128)S(1)}, f32[16]{0:T(128)S(1)}, u32[]{:S(2)}, u32[]{:S(2)}) collective-permute-start(f32[16]{0:T(128)S(1)} %multiply_reduce_fusion), channel_id=1, source_target_pairs={{0,1},{1,0},{2,3},{3,2},{4,5},{5,4},{6,7},{7,6},{8,9},{9,8},{10,11... | collective-permute-start | bytes 200 | tf_op jit(solution)/shard_map/ppermute | solution.py:118

commit v13 on v9

--- a/solution.py
+++ b/solution.py
@@ -97,22 +97,31 @@
     return jnp.stack(slots, axis=at)
 
 
-def gather_factors(both, rows_v):
-    cols = both.shape[1]
-    held = shifted(both, OUTER, 0)
-    held = shifted(held, MIDDLE, 1)
-    held = spread(held, CORE, 2)
-    return held[:, :, :, :rows_v].reshape(-1, cols), held[:, :, :, rows_v:].reshape(-1, cols)
+def halves(x, rows, first):
+    tok_rows = x.shape[0]
+    grouped = x.reshape(tok_rows, -1, 2, rows)
+    own = jnp.where(first, grouped[:, :, 0], grouped[:, :, 1])
+    other = jnp.where(first, grouped[:, :, 1], grouped[:, :, 0])
+    return own.reshape(tok_rows, -1), other.reshape(tok_rows, -1)
 
 
 def on_device(activations, out_grads, v_bank, u_bank, query_ids):
     tok_rows = activations.shape[0]
     queries = query_ids.shape[0]
+    rows_v, rows_u = v_bank.shape[0], u_bank.shape[0]
     n = lax.axis_size(OUTER) * lax.axis_size(MIDDLE) * lax.axis_size(CORE)
+    first = lax.axis_index(CORE) == 0
     both = pick_columns(v_bank, u_bank, query_ids)
-    v_full, u_full = gather_factors(both, v_bank.shape[0])
-    proj_in = folder(activations, v_full)
-    proj_out = folder(out_grads, u_full)
+    cols = both.shape[1]
+    held = shifted(both, OUTER, 0)
+    held = shifted(held, MIDDLE, 1)
+    sent = lax.ppermute(held, CORE, [(0, 1), (1, 0)])
+    act_own, act_other = halves(activations, rows_v, first)
+    grad_own, grad_other = halves(out_grads, rows_u, first)
+    proj_in = folder(act_own, held[:, :, :rows_v].reshape(-1, cols))
+    proj_out = folder(grad_own, held[:, :, rows_v:].reshape(-1, cols))
+    proj_in = proj_in + folder(act_other, sent[:, :, :rows_v].reshape(-1, cols))
+    proj_out = proj_out + folder(grad_other, sent[:, :, rows_v:].reshape(-1, cols))
     scores = (proj_in * proj_out).reshape(tok_rows, queries, RANK).sum(axis=2)
     total = total_over(jnp.sum(scores * scores, axis=0), TOK, n)
     scale = jnp.sqrt(total / (tok_rows * n) + 1e-06)

time: 62.9 us -> 65.9 us (1.048)
  local copies, waits for them, and re-layouts: 2.79 us -> 19.1 us
  waiting for transfers between devices: 17.6 us -> 5.84 us
  blocking collectives: 16.9 us -> 10.5 us
  other arithmetic: 3 us -> 7.98 us
  starting transfers between devices: 11.5 us -> 9.73 us
  matrix products: 6.12 us -> 7.25 us
    unnamed x8, local copies, waits for them, and re-layouts: 2.16 us -> 18.7 us
    ppermute x6, waiting for transfers between devices: 17.6 us -> 5.84 us  [shifted(): lax.ppermute(x, axis, [(j, (j + s) % k) for j in range(k)])]
    all_to_all x1 -> x0, blocking collectives: 5.84 us -> none  [spread(): return lax.all_to_all(copies, axis, at, at, tiled=True)]
    select_n x0 -> x2, other arithmetic: none -> 5.84 us  [halves(): other = jnp.where(first, grouped[:, :, 1], grouped[:, :, 0])]
    ppermute x6, starting transfers between devices: 11.5 us -> 9.66 us  [shifted(): lax.ppermute(x, axis, [(j, (j + s) % k) for j in range(k)])]
    dot_general x2 -> x4, matrix products: 6.12 us -> 7.25 us  [folder(): return jnp.dot(left, piece, preferred_element_type=jnp.float32)]
    another operation x5, other arithmetic: 2.07 us -> 1.21 us  [shifted(): return jnp.stack(slots, axis=at)]
  transfers between devices with their start and end apart: 6 -> 7, of which waited for: 5 -> 1; matrix products, arithmetic and copies ran while one was open for 0% -> 38% of each run, Pallas kernels for 0% -> 0%
where the time goes in v13:
time: 65.9 us; the launch traced here: 65.2 us
  local copies, waits for them, and re-layouts  19.1 us (29%)
  blocking collectives  10.5 us (16%)
  starting transfers between devices  9.73 us (15%)
  other arithmetic  7.98 us (12%)
  matrix products  7.25 us (11%)
  waiting for transfers between devices  5.84 us (9%)
  Pallas kernels  4.6 us (7%)
    unnamed x8, local copies, waits for them, and re-layouts  18.7 us
    all_to_all x1, blocking collectives, total_over(): return lax.all_to_all(copies, axis, 0, 0, tiled=False).sum(axis=0)  10.5 us
    ppermute x6, starting transfers between devices, shifted(): lax.ppermute(x, axis, [(j, (j + s) % k) for j in range(k)])  9.66 us
    dot_general x4, matrix products, folder(): return jnp.dot(left, piece, preferred_element_type=jnp.float32)  7.25 us
    ppermute x6, waiting for transfers between devices, shifted(): lax.ppermute(x, axis, [(j, (j + s) % k) for j in range(k)])  5.84 us
    select_n x2, other arithmetic, halves(): other = jnp.where(first, grouped[:, :, 1], grouped[:, :, 0])  5.84 us
    pallas_call x1, Pallas kernels, pick_columns(): pl.pallas_call(pick_kernel, out_shape=jax.ShapeDtypeStruct((v_bank.shape[...  4.6 us
  transfers between devices with their start and end apart: 7, of which 1 were waited for; matrix products, arithmetic and copies ran while one was open for 38% of the time, Pallas kernels for 0%

profile of v13, /device:TPU:0, one launch (start us, length us, event | category | flops | bytes accessed | tf_op | source)
XLA Modules:
  0.0 65.2 jit_solution(3369079609179864069)
XLA Ops:
  0.0 4.6 %shard_map.55 = bf16[80,512]{1,0:T(8,128)(2,1)} custom-call(s32[16]{0:T(128)} %ids_ref.1, bf16[64,65536]{1,0:T(8,128)(2,1)} %v_ref.1, bf16[16,65536]{1,0:T(8,128)(2,1)} %u_ref.1), custom_call_target="tpu_custom_call" | custom-call | tf_op jit(solution)/shard_map/pallas_call | solution.py:47
  4.6 5.1 %collective-permute-start = (bf16[80,512]{1,0:T(8,128)(2,1)}, bf16[80,512]{1,0:T(8,128)(2,1)S(1)}, u32[]{:S(2)}, u32[]{:S(2)}) collective-permute-start(bf16[80,512]{1,0:T(8,128)(2,1)} %shard_map.55), channel_id=1, source_target_pairs={{0,24},{8,0},{16,8},{24,16},{1,25},{9,1},{17,9},{25,17},{2,26},{10... | collective-permute-start | bytes 245768 | tf_op jit(solution)/shard_map/ppermute | solution.py:90
  9.7 0.0 collective-permute-start.1
  9.7 1.0 %collective-permute-start.2 = (bf16[80,512]{1,0:T(8,128)(2,1)}, bf16[80,512]{1,0:T(8,128)(2,1)S(1)}, u32[]{:S(2)}, u32[]{:S(2)}) collective-permute-start(bf16[80,512]{1,0:T(8,128)(2,1)} %shard_map.55), channel_id=1, source_target_pairs={{0,8},{8,16},{16,24},{24,0},{1,9},{9,17},{17,25},{25,1},{2,10},{10... | collective-permute-start | bytes 245768 | tf_op jit(solution)/shard_map/ppermute | solution.py:90
  10.7 0.0 copy-start.2
  10.7 12.4 %copy.18 = bf16[2048,2048]{0,1:T(8,128)(2,1)} copy(bf16[2048,2048]{1,0:T(8,128)(2,1)} %param.5) | data formatting | bytes 16777216 | tf_op args[0]
  23.1 0.0 collective-permute-done
  23.1 0.0 collective-permute-done.1
  23.2 0.0 collective-permute-done.2
  23.2 0.0 copy-done.2
  23.2 0.1 select_bitcast_fusion.7
  23.2 0.8 %pad_maximum_fusion.1 = bf16[4,80,512]{2,1,0:T(8,128)(2,1)} fusion(bf16[1,80,512]{2,1,0:T(8,128)(2,1)S(1)} %get-tuple-element.14, bf16[1,80,512]{2,1,0:T(8,128)(2,1)S(1)} %get-tuple-element.15, bf16[1,80,512]{2,1,0:T(8,128)(2,1)S(1)} %get-tuple-element.16, bf16[1,80,512]{2,1,0:T(8,128)(2,1)S(1)} %get-tuple-element.13), kind=kLoop, calls=%fused_computation.7 | loop fusion | flops 491520 | bytes 655360 | tf_op jit(solution)/shard_map/stack | solution.py:97
  24.0 2.4 %collective-permute-start.3 = (bf16[4,80,512]{2,1,0:T(8,128)(2,1)}, bf16[4,80,512]{2,1,0:T(8,128)(2,1)S(1)}, u32[]{:S(2)}, u32[]{:S(2)}) collective-permute-start(bf16[4,80,512]{2,1,0:T(8,128)(2,1)} %pad_maximum_fusion.1), channel_id=1, source_target_pairs={{0,6},{2,0},{4,2},{6,4},{1,7},{3,1},{5,3},{7,5},{8,14},{10,8},{12,... | collective-permute-start | bytes 983048 | tf_op jit(solution)/shard_map/ppermute | solution.py:90
  26.5 0.5 collective-permute-start.4
  27.0 0.6 collective-permute-start.5
  27.6 5.7 %broadcast_select_fusion = (bf16[2048,16,1,64]{0,3,2,1:T(8,128)(2,1)}, bf16[2048,16,1,64]{0,3,2,1:T(8,128)(2,1)}) fusion(pred[]{:T(512)S(6)} %eq.100, bf16[2048,16,2,64]{0,3,2,1:T(8,128)(2,1)} %bitcast.36), kind=kLoop, calls=%fused_computation.2 | loop fusion | flops 4194304 | bytes 16777216 | tf_op jit(solution)/shard_map/jit(_where)/select_n | solution.py:104
  33.3 2.9 %copy.21 = bf16[2048,512]{0,1:T(8,128)(2,1)S(1)} copy(bf16[2048,512]{1,0:T(8,128)(2,1)} %param.6) | data formatting | bytes 4194304 | tf_op args[1]
  36.2 0.0 collective-permute-done.3
  36.2 5.8 %collective-permute-done.4 = bf16[4,80,512]{2,1,0:T(8,128)(2,1)S(1)} collective-permute-done((bf16[4,80,512]{2,1,0:T(8,128)(2,1)}, bf16[4,80,512]{2,1,0:T(8,128)(2,1)S(1)}, u32[]{:S(2)}, u32[]{:S(2)}) %collective-permute-start.4) | collective-permute-done | bytes 327712 | tf_op jit(solution)/shard_map/ppermute | solution.py:90
  42.0 0.0 collective-permute-done.5
  42.0 0.1 select_bitcast_fusion.2
  42.1 0.1 select_bitcast_fusion.3
  42.2 0.2 pad_maximum_fusion
  42.4 0.1 collective-permute-start.6
  42.5 0.1 broadcast_select_fusion.2
  42.6 0.1 slice.38
  42.8 0.1 copy.19
  42.9 0.0 copy-start.1
  42.9 0.8 %fusion.2 = f32[2048,512]{0,1:T(8,128)S(1)} fusion(bf16[2048,256]{0,1:T(8,128)(2,1)S(1)} %bitcast.38, bf16[256,512]{1,0:T(8,128)(2,1)S(1)} %bitcast.43), kind=kOutput, calls=%fused_computation.21 | convolution fusion | flops 536870912 | bytes 5505024 | tf_op jit(solution)/shard_map/dot_general | solution.py:71
  43.7 1.4 %copy-done.1 = bf16[2048,16,1,64]{0,3,2,1:T(8,128)(2,1)S(1)} copy-done((bf16[2048,16,1,64]{0,3,2,1:T(8,128)(2,1)S(1)}, bf16[2048,16,1,64]{0,3,2,1:T(8,128)(2,1)}, u32[]{:S(2)}) %copy-start.1) | copy-done | bytes 4194328
  45.1 2.6 %fusion = f32[2048,512]{0,1:T(8,128)S(1)} fusion(bf16[2048,1024]{0,1:T(8,128)(2,1)S(1)} %bitcast.40, bf16[1024,512]{1,0:T(8,128)(2,1)S(1)} %bitcast.44), kind=kOutput, calls=%fused_computation.19 | convolution fusion | flops 2147483648 | bytes 9437184 | tf_op jit(solution)/shard_map/dot_general | solution.py:71
  47.6 0.0 copy-start
  47.6 0.0 collective-permute-done.6
  47.7 0.1 slice.39
  47.7 0.1 copy.20
  47.9 1.9 %copy-done = bf16[2048,16,1,64]{0,3,2,1:T(8,128)(2,1)S(1)} copy-done((bf16[2048,16,1,64]{0,3,2,1:T(8,128)(2,1)S(1)}, bf16[2048,16,1,64]{0,3,2,1:T(8,128)(2,1)}, u32[]{:S(2)}) %copy-start) | copy-done | bytes 4194328
  49.8 2.6 %fusion.1 = f32[2048,512]{0,1:T(8,128)S(1)} fusion(bf16[2048,1024]{0,1:T(8,128)(2,1)S(1)} %bitcast.39, bf16[1024,512]{1,0:T(8,128)(2,1)S(1)} %bitcast.45), kind=kOutput, calls=%fused_computation.20 | convolution fusion | flops 2147483648 | bytes 9437184 | tf_op jit(solution)/shard_map/dot_general | solution.py:71
  52.4 1.4 %bitcast_reduce_fusion = f32[2048,16]{0,1:T(8,128)S(1)} fusion(f32[2048,512]{0,1:T(8,128)S(1)} %fusion.2, f32[2048,512]{0,1:T(8,128)S(1)} %fusion, f32[2048,512]{0,1:T(8,128)S(1)} %fusion.1, bf16[2048,256]{0,1:T(8,128)(2,1)S(1)} %bitcast.41, bf16[256,512]{1,0:T(8,128)(2,1)S(1)} %bitcast.42), kind=kOutput, calls=%fused_computation | convolution fusion | flops 541032448 | bytes 14024704 | tf_op jit(solution)/shard_map/dot_general | solution.py:71
  53.8 0.1 multiply_reduce_fusion
  53.9 10.5 %all_to_all.6 = f32[32,1,16]{2,1,0:T(1,128)S(1)} all-to-all(f32[32,1,16]{2,1,0:T(1,128)S(1)} %broadcast_in_dim.2), channel_id=1, replica_groups=mesh['grp'=1,'tok_o'=4,'tok_m'=4,'tok_c'=2] {'tok_o','tok_m','tok_c'}, dimensions={0} | all-to-all | bytes 4096 | tf_op jit(solution)/shard_map/all_to_all | solution.py:76
  64.4 0.1 reduce_sum.29
  64.5 0.7 %broadcast_divide_fusion = f32[2048,16]{0,1:T(8,128)} fusion(f32[2048,16]{0,1:T(8,128)S(1)} %bitcast_reduce_fusion, f32[16]{0:T(128)S(1)} %add_sqrt_fusion), kind=kLoop, calls=%fused_computation.17 | loop fusion | flops 32768 | bytes 262208 | tf_op jit(solution)/shard_map/div | solution.py:128
  (6 shorter events, 0.1 us)
Async XLA Ops:
  4.6 18.5 %collective-permute-start = (bf16[80,512]{1,0:T(8,128)(2,1)}, bf16[80,512]{1,0:T(8,128)(2,1)S(1)}, u32[]{:S(2)}, u32[]{:S(2)}) collective-permute-start(bf16[80,512]{1,0:T(8,128)(2,1)} %shard_map.55), channel_id=1, source_target_pairs={{0,24},{8,0},{16,8},{24,16},{1,25},{9,1},{17,9},{25,17},{2,26},{10... | collective-permute-start | bytes 245768 | tf_op jit(solution)/shard_map/ppermute | solution.py:90
  9.7 13.4 %collective-permute-start.1 = (bf16[80,512]{1,0:T(8,128)(2,1)}, bf16[80,512]{1,0:T(8,128)(2,1)S(1)}, u32[]{:S(2)}, u32[]{:S(2)}) collective-permute-start(bf16[80,512]{1,0:T(8,128)(2,1)} %shard_map.55), channel_id=1, source_target_pairs={{0,16},{8,24},{16,0},{24,8},{1,17},{9,25},{17,1},{25,9},{2,18},{10... | collective-permute-start | bytes 245768 | tf_op jit(solution)/shard_map/ppermute | solution.py:90
  9.7 13.4 %collective-permute-start.2 = (bf16[80,512]{1,0:T(8,128)(2,1)}, bf16[80,512]{1,0:T(8,128)(2,1)S(1)}, u32[]{:S(2)}, u32[]{:S(2)}) collective-permute-start(bf16[80,512]{1,0:T(8,128)(2,1)} %shard_map.55), channel_id=1, source_target_pairs={{0,8},{8,16},{16,24},{24,0},{1,9},{9,17},{17,25},{25,1},{2,10},{10... | collective-permute-start | bytes 245768 | tf_op jit(solution)/shard_map/ppermute | solution.py:90
  10.7 12.4 %copy-start.2 = (bf16[80,512]{1,0:T(8,128)(2,1)S(1)}, bf16[80,512]{1,0:T(8,128)(2,1)}, u32[]{:S(2)}) copy-start(bf16[80,512]{1,0:T(8,128)(2,1)} %shard_map.55) | copy-start | bytes 245764
  24.0 12.2 %collective-permute-start.3 = (bf16[4,80,512]{2,1,0:T(8,128)(2,1)}, bf16[4,80,512]{2,1,0:T(8,128)(2,1)S(1)}, u32[]{:S(2)}, u32[]{:S(2)}) collective-permute-start(bf16[4,80,512]{2,1,0:T(8,128)(2,1)} %pad_maximum_fusion.1), channel_id=1, source_target_pairs={{0,6},{2,0},{4,2},{6,4},{1,7},{3,1},{5,3},{7,5},{8,14},{10,8},{12,... | collective-permute-start | bytes 983048 | tf_op jit(solution)/shard_map/ppermute | solution.py:90
  26.5 15.6 %collective-permute-start.4 = (bf16[4,80,512]{2,1,0:T(8,128)(2,1)}, bf16[4,80,512]{2,1,0:T(8,128)(2,1)S(1)}, u32[]{:S(2)}, u32[]{:S(2)}) collective-permute-start(bf16[4,80,512]{2,1,0:T(8,128)(2,1)} %pad_maximum_fusion.1), channel_id=1, source_target_pairs={{0,4},{2,6},{4,0},{6,2},{1,5},{3,7},{5,1},{7,3},{8,12},{10,14},{12... | collective-permute-start | bytes 983048 | tf_op jit(solution)/shard_map/ppermute | solution.py:90
  27.0 15.1 %collective-permute-start.5 = (bf16[4,80,512]{2,1,0:T(8,128)(2,1)}, bf16[4,80,512]{2,1,0:T(8,128)(2,1)S(1)}, u32[]{:S(2)}, u32[]{:S(2)}) collective-permute-start(bf16[4,80,512]{2,1,0:T(8,128)(2,1)} %pad_maximum_fusion.1), channel_id=1, source_target_pairs={{0,2},{2,4},{4,6},{6,0},{1,3},{3,5},{5,7},{7,1},{8,10},{10,12},{12... | collective-permute-start | bytes 983048 | tf_op jit(solution)/shard_map/ppermute | solution.py:90
  42.4 5.2 %collective-permute-start.6 = (bf16[4,4,80,512]{3,2,0,1:T(8,128)(2,1)S(1)}, bf16[4,4,80,512]{3,2,0,1:T(8,128)(2,1)S(1)}, u32[]{:S(2)}, u32[]{:S(2)}) collective-permute-start(bf16[4,4,80,512]{3,2,0,1:T(8,128)(2,1)S(1)} %pad_maximum_fusion), channel_id=1, source_target_pairs={{0,1},{1,0},{2,3},{3,2},{4,5},{5,4},{6,7},{7,6},{8,9},{9,8},{10,11... | collective-permute-start | bytes 3932168 | tf_op jit(solution)/shard_map/ppermute | solution.py:118
  42.9 2.2 %copy-start.1 = (bf16[2048,16,1,64]{0,3,2,1:T(8,128)(2,1)S(1)}, bf16[2048,16,1,64]{0,3,2,1:T(8,128)(2,1)}, u32[]{:S(2)}) copy-start(bf16[2048,16,1,64]{0,3,2,1:T(8,128)(2,1)} %get-tuple-element.6) | copy-start | bytes 12582916
  47.6 2.2 %copy-start = (bf16[2048,16,1,64]{0,3,2,1:T(8,128)(2,1)S(1)}, bf16[2048,16,1,64]{0,3,2,1:T(8,128)(2,1)}, u32[]{:S(2)}) copy-start(bf16[2048,16,1,64]{0,3,2,1:T(8,128)(2,1)} %get-tuple-element.5) | copy-start | bytes 12582916

commit v14 on v13

--- a/solution.py
+++ b/solution.py
@@ -97,12 +97,13 @@
     return jnp.stack(slots, axis=at)
 
 
-def halves(x, rows, first):
-    tok_rows = x.shape[0]
-    grouped = x.reshape(tok_rows, -1, 2, rows)
-    own = jnp.where(first, grouped[:, :, 0], grouped[:, :, 1])
-    other = jnp.where(first, grouped[:, :, 1], grouped[:, :, 0])
-    return own.reshape(tok_rows, -1), other.reshape(tok_rows, -1)
+def spread_rows(part, first, mine):
+    zero = jnp.zeros_like(part)
+    if mine:
+        pair = [jnp.where(first, part, zero), jnp.where(first, zero, part)]
+    else:
+        pair = [jnp.where(first, zero, part), jnp.where(first, part, zero)]
+    return jnp.stack(pair, axis=2).reshape(-1, part.shape[-1])
 
 
 def on_device(activations, out_grads, v_bank, u_bank, query_ids):
@@ -116,12 +117,10 @@
     held = shifted(both, OUTER, 0)
     held = shifted(held, MIDDLE, 1)
     sent = lax.ppermute(held, CORE, [(0, 1), (1, 0)])
-    act_own, act_other = halves(activations, rows_v, first)
-    grad_own, grad_other = halves(out_grads, rows_u, first)
-    proj_in = folder(act_own, held[:, :, :rows_v].reshape(-1, cols))
-    proj_out = folder(grad_own, held[:, :, rows_v:].reshape(-1, cols))
-    proj_in = proj_in + folder(act_other, sent[:, :, :rows_v].reshape(-1, cols))
-    proj_out = proj_out + folder(grad_other, sent[:, :, rows_v:].reshape(-1, cols))
+    proj_in = folder(activations, spread_rows(held[:, :, :rows_v], first, True))
+    proj_out = folder(out_grads, spread_rows(held[:, :, rows_v:], first, True))
+    proj_in = proj_in + folder(activations, spread_rows(sent[:, :, :rows_v], first, False))
+    proj_out = proj_out + folder(out_grads, spread_rows(sent[:, :, rows_v:], first, False))
     scores = (proj_in * proj_out).reshape(tok_rows, queries, RANK).sum(axis=2)
     total = total_over(jnp.sum(scores * scores, axis=0), TOK, n)
     scale = jnp.sqrt(total / (tok_rows * n) + 1e-06)

time: 65.9 us -> 70 us (1.062)
  local copies, waits for them, and re-layouts: 19.1 us -> 3.21 us
  waiting for transfers between devices: 5.84 us -> 20.7 us
  matrix products: 7.25 us -> 12.3 us
  other arithmetic: 7.98 us -> 6.03 us
  starting transfers between devices: 9.73 us -> 11.5 us
    unnamed x8 -> x6, local copies, waits for them, and re-layouts: 18.7 us -> 2.78 us
    ppermute x6, waiting for transfers between devices: 5.84 us -> 17.6 us  [shifted(): lax.ppermute(x, axis, [(j, (j + s) % k) for j in range(k)])]
    select_n x2 -> x0, other arithmetic: 5.84 us -> none  [halves(): other = jnp.where(first, grouped[:, :, 1], grouped[:, :, 0])]
    dot_general x4, matrix products: 7.25 us -> 12.3 us  [folder(): return jnp.dot(left, piece, preferred_element_type=jnp.float32)]
    ppermute x1, waiting for transfers between devices: 0.01 us -> 3.15 us  [on_device(): sent = lax.ppermute(held, CORE, [(0, 1), (1, 0)])]
    another operation x0 -> x6, other arithmetic: none -> 3.02 us  [spread_rows(): return jnp.stack(pair, axis=2).reshape(-1, part.shape[-1])]
    ppermute x6, starting transfers between devices: 9.66 us -> 11.5 us  [shifted(): lax.ppermute(x, axis, [(j, (j + s) % k) for j in range(k)])]
    another operation x5, other arithmetic: 1.21 us -> 2.07 us  [shifted(): return jnp.stack(slots, axis=at)]
  transfers between devices with their start and end apart: 7 -> 7, of which waited for: 1 -> 6; matrix products, arithmetic and copies ran while one was open for 38% -> 0% of each run, Pallas kernels for 0% -> 0%
where the time goes in v14:
time: 70 us; the launch traced here: 69.7 us
  waiting for transfers between devices  20.7 us (30%)
  matrix products  12.3 us (18%)
  starting transfers between devices  11.5 us (16%)
  blocking collectives  11 us (16%)
  other arithmetic  6.03 us (9%)
  Pallas kernels  4.73 us (7%)
  local copies, waits for them, and re-layouts  3.21 us (5%)
    ppermute x6, waiting for transfers between devices, shifted(): lax.ppermute(x, axis, [(j, (j + s) % k) for j in range(k)])  17.6 us
    dot_general x4, matrix products, folder(): return jnp.dot(left, piece, preferred_element_type=jnp.float32)  12.3 us
    ppermute x6, starting transfers between devices, shifted(): lax.ppermute(x, axis, [(j, (j + s) % k) for j in range(k)])  11.5 us
    all_to_all x1, blocking collectives, total_over(): return lax.all_to_all(copies, axis, 0, 0, tiled=False).sum(axis=0)  11 us
    pallas_call x1, Pallas kernels, pick_columns(): pl.pallas_call(pick_kernel, out_shape=jax.ShapeDtypeStruct((v_bank.shape[...  4.73 us
    ppermute x1, waiting for transfers between devices, on_device(): sent = lax.ppermute(held, CORE, [(0, 1), (1, 0)])  3.15 us
    another operation x6, other arithmetic, spread_rows(): return jnp.stack(pair, axis=2).reshape(-1, part.shape[-1])  3.02 us
    unnamed x6, local copies, waits for them, and re-layouts  2.78 us
  transfers between devices with their start and end apart: 7, of which 6 were waited for; matrix products, arithmetic and copies ran while one was open for 0% of the time, Pallas kernels for 0%

profile of v14, /device:TPU:0, one launch (start us, length us, event | category | flops | bytes accessed | tf_op | source)
XLA Modules:
  0.0 69.7 jit_solution(10704427478869708220)
XLA Ops:
  0.0 0.0 copy-start
  0.0 4.7 %shard_map.55 = bf16[80,512]{1,0:T(8,128)(2,1)} custom-call(s32[16]{0:T(128)} %ids_ref.1, bf16[64,65536]{1,0:T(8,128)(2,1)} %v_ref.1, bf16[16,65536]{1,0:T(8,128)(2,1)} %u_ref.1), custom_call_target="tpu_custom_call" | custom-call | tf_op jit(solution)/shard_map/pallas_call | solution.py:47
  4.7 3.1 %collective-permute-start.2 = (bf16[80,512]{1,0:T(8,128)(2,1)}, bf16[80,512]{1,0:T(8,128)(2,1)S(1)}, u32[]{:S(2)}, u32[]{:S(2)}) collective-permute-start(bf16[80,512]{1,0:T(8,128)(2,1)} %shard_map.55), channel_id=1, source_target_pairs={{0,8},{8,16},{16,24},{24,0},{1,9},{9,17},{17,25},{25,1},{2,10},{10... | collective-permute-start | bytes 245768 | tf_op jit(solution)/shard_map/ppermute | solution.py:90
  7.8 2.6 %collective-permute-start.1 = (bf16[80,512]{1,0:T(8,128)(2,1)}, bf16[80,512]{1,0:T(8,128)(2,1)S(1)}, u32[]{:S(2)}, u32[]{:S(2)}) collective-permute-start(bf16[80,512]{1,0:T(8,128)(2,1)} %shard_map.55), channel_id=1, source_target_pairs={{0,16},{8,24},{16,0},{24,8},{1,17},{9,25},{17,1},{25,9},{2,18},{10... | collective-permute-start | bytes 245768 | tf_op jit(solution)/shard_map/ppermute | solution.py:90
  10.4 1.3 %collective-permute-start = (bf16[80,512]{1,0:T(8,128)(2,1)}, bf16[80,512]{1,0:T(8,128)(2,1)S(1)}, u32[]{:S(2)}, u32[]{:S(2)}) collective-permute-start(bf16[80,512]{1,0:T(8,128)(2,1)} %shard_map.55), channel_id=1, source_target_pairs={{0,24},{8,0},{16,8},{24,16},{1,25},{9,1},{17,9},{25,17},{2,26},{10... | collective-permute-start | bytes 245768 | tf_op jit(solution)/shard_map/ppermute | solution.py:90
  11.8 1.3 %collective-permute-done.2 = bf16[80,512]{1,0:T(8,128)(2,1)S(1)} collective-permute-done((bf16[80,512]{1,0:T(8,128)(2,1)}, bf16[80,512]{1,0:T(8,128)(2,1)S(1)}, u32[]{:S(2)}, u32[]{:S(2)}) %collective-permute-start.2) | collective-permute-done | bytes 81952 | tf_op jit(solution)/shard_map/ppermute | solution.py:90
  13.1 3.0 %collective-permute-done.1 = bf16[80,512]{1,0:T(8,128)(2,1)S(1)} collective-permute-done((bf16[80,512]{1,0:T(8,128)(2,1)}, bf16[80,512]{1,0:T(8,128)(2,1)S(1)}, u32[]{:S(2)}, u32[]{:S(2)}) %collective-permute-start.1) | collective-permute-done | bytes 81952 | tf_op jit(solution)/shard_map/ppermute | solution.py:90
  16.1 0.2 collective-permute-done
  16.3 0.9 %select_bitcast_fusion.15 = (bf16[1,80,512]{2,1,0:T(8,128)(2,1)S(1)}, bf16[1,80,512]{2,1,0:T(8,128)(2,1)S(1)}, bf16[1,80,512]{2,1,0:T(8,128)(2,1)S(1)}, bf16[1,80,512]{2,1,0:T(8,128)(2,1)S(1)}) fusion(bf16[80,512]{1,0:T(8,128)(2,1)S(1)} %collective-permute-done, bf16[80,512]{1,0:T(8,128)(2,1)S(1)} %collective-permute-done.1, ...), kind=kLoop, calls=%fused_computation.24 | loop fusion | flops 491520 | bytes 655372 | tf_op jit(solution)/shard_map/stack | solution.py:97
  17.3 0.8 %pad_maximum_fusion.5 = bf16[4,80,512]{2,1,0:T(8,128)(2,1)} fusion(bf16[1,80,512]{2,1,0:T(8,128)(2,1)S(1)} %get-tuple-element.18, bf16[1,80,512]{2,1,0:T(8,128)(2,1)S(1)} %get-tuple-element.19, bf16[1,80,512]{2,1,0:T(8,128)(2,1)S(1)} %get-tuple-element.20, bf16[1,80,512]{2,1,0:T(8,128)(2,1)S(1)} %get-tuple-element.17), kind=kLoop, calls=%fused_computation.11 | loop fusion | flops 491520 | bytes 655360 | tf_op jit(solution)/shard_map/stack | solution.py:97
  18.0 1.5 %collective-permute-start.5 = (bf16[4,80,512]{2,1,0:T(8,128)(2,1)}, bf16[4,80,512]{2,1,0:T(8,128)(2,1)S(1)}, u32[]{:S(2)}, u32[]{:S(2)}) collective-permute-start(bf16[4,80,512]{2,1,0:T(8,128)(2,1)} %pad_maximum_fusion.5), channel_id=1, source_target_pairs={{0,2},{2,4},{4,6},{6,0},{1,3},{3,5},{5,7},{7,1},{8,10},{10,12},{12... | collective-permute-start | bytes 983048 | tf_op jit(solution)/shard_map/ppermute | solution.py:90
  19.5 1.5 %collective-permute-start.4 = (bf16[4,80,512]{2,1,0:T(8,128)(2,1)}, bf16[4,80,512]{2,1,0:T(8,128)(2,1)S(1)}, u32[]{:S(2)}, u32[]{:S(2)}) collective-permute-start(bf16[4,80,512]{2,1,0:T(8,128)(2,1)} %pad_maximum_fusion.5), channel_id=1, source_target_pairs={{0,4},{2,6},{4,0},{6,2},{1,5},{3,7},{5,1},{7,3},{8,12},{10,14},{12... | collective-permute-start | bytes 983048 | tf_op jit(solution)/shard_map/ppermute | solution.py:90
  21.0 1.4 %collective-permute-start.3 = (bf16[4,80,512]{2,1,0:T(8,128)(2,1)}, bf16[4,80,512]{2,1,0:T(8,128)(2,1)S(1)}, u32[]{:S(2)}, u32[]{:S(2)}) collective-permute-start(bf16[4,80,512]{2,1,0:T(8,128)(2,1)} %pad_maximum_fusion.5), channel_id=1, source_target_pairs={{0,6},{2,0},{4,2},{6,4},{1,7},{3,1},{5,3},{7,5},{8,14},{10,8},{12,... | collective-permute-start | bytes 983048 | tf_op jit(solution)/shard_map/ppermute | solution.py:90
  22.5 7.3 %collective-permute-done.5 = bf16[4,80,512]{2,1,0:T(8,128)(2,1)S(1)} collective-permute-done((bf16[4,80,512]{2,1,0:T(8,128)(2,1)}, bf16[4,80,512]{2,1,0:T(8,128)(2,1)S(1)}, u32[]{:S(2)}, u32[]{:S(2)}) %collective-permute-start.5) | collective-permute-done | bytes 327712 | tf_op jit(solution)/shard_map/ppermute | solution.py:90
  29.8 5.7 %collective-permute-done.4 = bf16[4,80,512]{2,1,0:T(8,128)(2,1)S(1)} collective-permute-done((bf16[4,80,512]{2,1,0:T(8,128)(2,1)}, bf16[4,80,512]{2,1,0:T(8,128)(2,1)S(1)}, u32[]{:S(2)}, u32[]{:S(2)}) %collective-permute-start.4) | collective-permute-done | bytes 327712 | tf_op jit(solution)/shard_map/ppermute | solution.py:90
  35.5 0.0 collective-permute-done.3
  35.5 0.1 select_bitcast_fusion.6
  35.6 0.1 select_bitcast_fusion.7
  35.7 0.2 pad_maximum_fusion.2
  35.9 0.1 collective-permute-start.6
  36.0 3.1 %collective-permute-done.6 = bf16[4,4,80,512]{3,2,0,1:T(8,128)(2,1)} collective-permute-done((bf16[4,4,80,512]{3,2,0,1:T(8,128)(2,1)S(1)}, bf16[4,4,80,512]{3,2,0,1:T(8,128)(2,1)}, u32[]{:S(2)}, u32[]{:S(2)}) %collective-permute-start.6) | collective-permute-done | bytes 1310752 | tf_op jit(solution)/shard_map/ppermute | solution.py:119
  39.1 1.0 %select_bitcast_fusion.9 = (bf16[4,4,1,16,512]{4,3,0,1,2:T(8,128)(2,1)S(1)}, bf16[4,4,1,16,512]{4,3,0,1,2:T(8,128)(2,1)S(1)}, bf16[4,4,1,16,512]{4,3,0,1,2:T(8,128)(2,1)S(1)}, bf16[4,4,1,16,512]{4,3,0,1,2:T(8,128)(2,1)S(1)}) fusion(pred[]{:T(512)S(6)} %eq.100, bf16[4,4,80,512]{3,2,0,1:T(8,128)(2,1)} %collective-permute-done.6, ...), kind=kLoop, calls=%fused_computation.17 | loop fusion | flops 524288 | bytes 1572865 | tf_op jit(solution)/shard_map/stack | solution.py:106
  40.1 0.1 pad_maximum_fusion.4
  40.2 0.1 pad_maximum_fusion.3
  40.3 1.5 %select_bitcast_fusion.1 = (bf16[4,4,1,64,512]{4,3,0,1,2:T(8,128)(2,1)S(1)}, bf16[4,4,1,64,512]{4,3,0,1,2:T(8,128)(2,1)S(1)}, bf16[4,4,1,64,512]{4,3,0,1,2:T(8,128)(2,1)S(1)}, bf16[4,4,1,64,512]{4,3,0,1,2:T(8,128)(2,1)S(1)}) fusion(pred[]{:T(512)S(6)} %eq.100, bf16[4,4,80,512]{3,2,0,1:T(8,128)(2,1)} %collective-permute-done.6, ...), kind=kLoop, calls=%fused_computation.6 | loop fusion | flops 2097152 | bytes 6291457 | tf_op jit(solution)/shard_map/stack | solution.py:106
  41.8 0.0 slice-start
  41.9 0.2 pad_maximum_fusion.1
  42.1 0.1 copy.15
  42.2 0.0 slice-start.1
  42.2 0.2 pad_maximum_fusion
  42.4 0.2 copy.14
  42.6 1.4 %slice-done = s8[4194304]{0:T(1024)(128)(4,1)S(1)} async-done(((s8[8388608]{0:T(1024)(128)(4,1)}), s8[4194304]{0:T(1024)(128)(4,1)S(1)}, s32[]{:S(2)}) %slice-start) | async-done | bytes 4194328
  44.0 1.4 %slice-done.1 = s8[4194304]{0:T(1024)(128)(4,1)S(1)} async-done(((s8[8388608]{0:T(1024)(128)(4,1)}), s8[4194304]{0:T(1024)(128)(4,1)S(1)}, s32[]{:S(2)}) %slice-start.1) | async-done | bytes 4194328
  45.4 4.5 %fusion.1 = f32[512,2048]{1,0:T(8,128)S(1)} fusion(bf16[2048,512]{1,0:T(8,128)(2,1)S(1)} %bitcast.49, bf16[2048,2048]{1,0:T(8,128)(2,1)S(1)} %bitcast.53), kind=kOutput, calls=%fused_computation.28 | convolution fusion | flops 4294967296 | bytes 14680064 | tf_op jit(solution)/shard_map/dot_general | solution.py:71
  50.0 4.5 %fusion = f32[512,2048]{1,0:T(8,128)S(1)} fusion(bf16[2048,512]{1,0:T(8,128)(2,1)S(1)} %bitcast.50, bf16[2048,2048]{1,0:T(8,128)(2,1)S(1)} %bitcast.53), kind=kOutput, calls=%fused_computation.27 | convolution fusion | flops 4294967296 | bytes 14680064 | tf_op jit(solution)/shard_map/dot_general | solution.py:71
  54.5 0.0 copy-done
  54.5 1.3 %fusion.2 = f32[512,2048]{1,0:T(8,128)S(1)} fusion(bf16[512,512]{1,0:T(8,128)(2,1)S(1)} %bitcast.48, bf16[2048,512]{1,0:T(8,128)(2,1)S(1)} %copy-done), kind=kOutput, calls=%fused_computation.29 | convolution fusion | flops 1073741824 | bytes 6815744 | tf_op jit(solution)/shard_map/dot_general | solution.py:71
  55.8 1.9 %bitcast_reduce_fusion = f32[2048,16]{0,1:T(8,128)S(1)} fusion(f32[512,2048]{1,0:T(8,128)S(1)} %fusion.2, f32[512,2048]{1,0:T(8,128)S(1)} %fusion, f32[512,2048]{1,0:T(8,128)S(1)} %fusion.1, bf16[512,512]{1,0:T(8,128)(2,1)S(1)} %bitcast.51, bf16[2048,512]{1,0:T(8,128)(2,1)S(1)} %copy-done), kind=kOutput, calls=%fused_computation | convolution fusion | flops 1077903360 | bytes 15335424 | tf_op jit(solution)/shard_map/dot_general | solution.py:71
  57.7 0.1 multiply_reduce_fusion
  57.9 11.0 %all_to_all.6 = f32[32,1,16]{2,1,0:T(1,128)S(1)} all-to-all(f32[32,1,16]{2,1,0:T(1,128)S(1)} %broadcast_in_dim.2), channel_id=1, replica_groups=mesh['grp'=1,'tok_o'=4,'tok_m'=4,'tok_c'=2] {'tok_o','tok_m','tok_c'}, dimensions={0} | all-to-all | bytes 4096 | tf_op jit(solution)/shard_map/all_to_all | solution.py:76
  68.9 0.1 reduce_sum.29
  69.0 0.7 %broadcast_divide_fusion = f32[2048,16]{0,1:T(8,128)} fusion(f32[2048,16]{0,1:T(8,128)S(1)} %bitcast_reduce_fusion, f32[16]{0:T(128)S(1)} %add_sqrt_fusion), kind=kLoop, calls=%fused_computation.25 | loop fusion | flops 32768 | bytes 262208 | tf_op jit(solution)/shard_map/div | solution.py:127
  (5 shorter events, 0.1 us)
Async XLA Ops:
  0.0 54.5 %copy-start = (bf16[2048,512]{1,0:T(8,128)(2,1)S(1)}, bf16[2048,512]{1,0:T(8,128)(2,1)}, u32[]{:S(2)}) copy-start(bf16[2048,512]{1,0:T(8,128)(2,1)} %param.6) | copy-start | bytes 6291460
  4.7 8.3 %collective-permute-start.2 = (bf16[80,512]{1,0:T(8,128)(2,1)}, bf16[80,512]{1,0:T(8,128)(2,1)S(1)}, u32[]{:S(2)}, u32[]{:S(2)}) collective-permute-start(bf16[80,512]{1,0:T(8,128)(2,1)} %shard_map.55), channel_id=1, source_target_pairs={{0,8},{8,16},{16,24},{24,0},{1,9},{9,17},{17,25},{25,1},{2,10},{10... | collective-permute-start | bytes 245768 | tf_op jit(solution)/shard_map/ppermute | solution.py:90
  7.8 8.3 %collective-permute-start.1 = (bf16[80,512]{1,0:T(8,128)(2,1)}, bf16[80,512]{1,0:T(8,128)(2,1)S(1)}, u32[]{:S(2)}, u32[]{:S(2)}) collective-permute-start(bf16[80,512]{1,0:T(8,128)(2,1)} %shard_map.55), channel_id=1, source_target_pairs={{0,16},{8,24},{16,0},{24,8},{1,17},{9,25},{17,1},{25,9},{2,18},{10... | collective-permute-start | bytes 245768 | tf_op jit(solution)/shard_map/ppermute | solution.py:90
  10.4 5.9 %collective-permute-start = (bf16[80,512]{1,0:T(8,128)(2,1)}, bf16[80,512]{1,0:T(8,128)(2,1)S(1)}, u32[]{:S(2)}, u32[]{:S(2)}) collective-permute-start(bf16[80,512]{1,0:T(8,128)(2,1)} %shard_map.55), channel_id=1, source_target_pairs={{0,24},{8,0},{16,8},{24,16},{1,25},{9,1},{17,9},{25,17},{2,26},{10... | collective-permute-start | bytes 245768 | tf_op jit(solution)/shard_map/ppermute | solution.py:90
  18.0 11.8 %collective-permute-start.5 = (bf16[4,80,512]{2,1,0:T(8,128)(2,1)}, bf16[4,80,512]{2,1,0:T(8,128)(2,1)S(1)}, u32[]{:S(2)}, u32[]{:S(2)}) collective-permute-start(bf16[4,80,512]{2,1,0:T(8,128)(2,1)} %pad_maximum_fusion.5), channel_id=1, source_target_pairs={{0,2},{2,4},{4,6},{6,0},{1,3},{3,5},{5,7},{7,1},{8,10},{10,12},{12... | collective-permute-start | bytes 983048 | tf_op jit(solution)/shard_map/ppermute | solution.py:90
  19.5 16.0 %collective-permute-start.4 = (bf16[4,80,512]{2,1,0:T(8,128)(2,1)}, bf16[4,80,512]{2,1,0:T(8,128)(2,1)S(1)}, u32[]{:S(2)}, u32[]{:S(2)}) collective-permute-start(bf16[4,80,512]{2,1,0:T(8,128)(2,1)} %pad_maximum_fusion.5), channel_id=1, source_target_pairs={{0,4},{2,6},{4,0},{6,2},{1,5},{3,7},{5,1},{7,3},{8,12},{10,14},{12... | collective-permute-start | bytes 983048 | tf_op jit(solution)/shard_map/ppermute | solution.py:90
  21.0 14.5 %collective-permute-start.3 = (bf16[4,80,512]{2,1,0:T(8,128)(2,1)}, bf16[4,80,512]{2,1,0:T(8,128)(2,1)S(1)}, u32[]{:S(2)}, u32[]{:S(2)}) collective-permute-start(bf16[4,80,512]{2,1,0:T(8,128)(2,1)} %pad_maximum_fusion.5), channel_id=1, source_target_pairs={{0,6},{2,0},{4,2},{6,4},{1,7},{3,1},{5,3},{7,5},{8,14},{10,8},{12,... | collective-permute-start | bytes 983048 | tf_op jit(solution)/shard_map/ppermute | solution.py:90
  35.9 3.2 %collective-permute-start.6 = (bf16[4,4,80,512]{3,2,0,1:T(8,128)(2,1)S(1)}, bf16[4,4,80,512]{3,2,0,1:T(8,128)(2,1)}, u32[]{:S(2)}, u32[]{:S(2)}) collective-permute-start(bf16[4,4,80,512]{3,2,0,1:T(8,128)(2,1)S(1)} %pad_maximum_fusion.2), channel_id=1, source_target_pairs={{0,1},{1,0},{2,3},{3,2},{4,5},{5,4},{6,7},{7,6},{8,9},{9,8},{10,11... | collective-permute-start | bytes 3932168 | tf_op jit(solution)/shard_map/ppermute | solution.py:119
  41.8 2.2 %slice-start = ((s8[8388608]{0:T(1024)(128)(4,1)}), s8[4194304]{0:T(1024)(128)(4,1)S(1)}, s32[]{:S(2)}) async-start(s8[8388608]{0:T(1024)(128)(4,1)} %bitcast.52), calls=%async_computation.1 | async-start | bytes 8388608
  42.2 3.2 %slice-start.1 = ((s8[8388608]{0:T(1024)(128)(4,1)}), s8[4194304]{0:T(1024)(128)(4,1)S(1)}, s32[]{:S(2)}) async-start(s8[8388608]{0:T(1024)(128)(4,1)} %bitcast.52), calls=%async_computation.2 | async-start | bytes 8388608

commit v15 on v9

--- a/solution.py
+++ b/solution.py
@@ -10,7 +10,7 @@
 PER_TILE = LANES // RANK
 
 
-def pick_kernel(ids_ref, v_ref, u_ref, out, v_buf, u_buf, sems):
+def pick_kernel(ids_ref, v_ref, u_ref, out_hbm, v_buf, u_buf, sems, out, out_sem):
     queries = ids_ref.shape[0]
     copies = []
     for k, (bank, buf) in enumerate(((v_ref, v_buf), (u_ref, u_buf))):
@@ -38,6 +38,9 @@
                 keep = (lane >= RANK * j) & (lane < RANK * (j + 1))
                 acc = jnp.where(keep, moved, acc)
             out[base:base + rows, g * LANES:(g + 1) * LANES] = acc
+    done = pltpu.make_async_copy(out, out_hbm, out_sem)
+    done.start()
+    done.wait()
 
 
 def pick_columns(v_bank, u_bank, query_ids):
@@ -52,11 +55,13 @@
             pl.BlockSpec(memory_space=pl.ANY),
             pl.BlockSpec(memory_space=pl.ANY),
         ],
-        out_specs=vmem,
+        out_specs=pl.BlockSpec(memory_space=pl.ANY),
         scratch_shapes=[
             pltpu.VMEM((queries, v_bank.shape[0], LANES), v_bank.dtype),
             pltpu.VMEM((queries, u_bank.shape[0], LANES), u_bank.dtype),
             pltpu.SemaphoreType.DMA((2, queries)),
+            pltpu.VMEM((v_bank.shape[0] + u_bank.shape[0], queries * RANK), v_bank.dtype),
+            pltpu.SemaphoreType.DMA(()),
         ],
     )(query_ids, v_bank, u_bank)
 

time: 62.9 us -> 62.9 us (level)
  no operation moved by 1% of the time
where the time goes in v15:
time: 62.9 us; the launch traced here: 62.7 us
  waiting for transfers between devices  17.6 us (28%)
  blocking collectives  16.9 us (27%)
  starting transfers between devices  11.5 us (18%)
  matrix products  6.12 us (10%)
  Pallas kernels  4.74 us (8%)
  other arithmetic  3 us (5%)
  local copies, waits for them, and re-layouts  2.79 us (4%)
    ppermute x6, waiting for transfers between devices, shifted(): lax.ppermute(x, axis, [(j, (j + s) % k) for j in range(k)])  17.6 us
    ppermute x6, starting transfers between devices, shifted(): lax.ppermute(x, axis, [(j, (j + s) % k) for j in range(k)])  11.5 us
    all_to_all x1, blocking collectives, total_over(): return lax.all_to_all(copies, axis, 0, 0, tiled=False).sum(axis=0)  11 us
    dot_general x2, matrix products, folder(): return jnp.dot(left, piece, preferred_element_type=jnp.float32)  6.12 us
    all_to_all x1, blocking collectives, spread(): return lax.all_to_all(copies, axis, at, at, tiled=True)  5.84 us
    pallas_call x1, Pallas kernels, pick_columns(): pl.pallas_call(pick_kernel, out_shape=jax.ShapeDtypeStruct((v_bank.shape[...  4.74 us
    unnamed x8, local copies, waits for them, and re-layouts  2.16 us
    another operation x5, other arithmetic, shifted(): return jnp.stack(slots, axis=at)  2.07 us
  transfers between devices with their start and end apart: 6, of which 5 were waited for; matrix products, arithmetic and copies ran while one was open for 0% of the time, Pallas kernels for 0%

profile of v15, /device:TPU:0, one launch (start us, length us, event | category | flops | bytes accessed | tf_op | source)
XLA Modules:
  0.0 62.7 jit_solution(18145329068052105792)
XLA Ops:
  0.0 0.0 copy-start
  0.0 4.7 %shard_map.55 = bf16[80,512]{1,0:T(8,128)(2,1)} custom-call(s32[16]{0:T(128)} %ids_ref.1, bf16[64,65536]{1,0:T(8,128)(2,1)} %v_ref.1, bf16[16,65536]{1,0:T(8,128)(2,1)} %u_ref.1), custom_call_target="tpu_custom_call" | custom-call | tf_op jit(solution)/shard_map/pallas_call | solution.py:50
  4.8 3.1 %collective-permute-start.2 = (bf16[80,512]{1,0:T(8,128)(2,1)}, bf16[80,512]{1,0:T(8,128)(2,1)S(1)}, u32[]{:S(2)}, u32[]{:S(2)}) collective-permute-start(bf16[80,512]{1,0:T(8,128)(2,1)} %shard_map.55), channel_id=1, source_target_pairs={{0,8},{8,16},{16,24},{24,0},{1,9},{9,17},{17,25},{25,1},{2,10},{10... | collective-permute-start | bytes 245768 | tf_op jit(solution)/shard_map/ppermute | solution.py:95
  7.8 2.6 %collective-permute-start.1 = (bf16[80,512]{1,0:T(8,128)(2,1)}, bf16[80,512]{1,0:T(8,128)(2,1)S(1)}, u32[]{:S(2)}, u32[]{:S(2)}) collective-permute-start(bf16[80,512]{1,0:T(8,128)(2,1)} %shard_map.55), channel_id=1, source_target_pairs={{0,16},{8,24},{16,0},{24,8},{1,17},{9,25},{17,1},{25,9},{2,18},{10... | collective-permute-start | bytes 245768 | tf_op jit(solution)/shard_map/ppermute | solution.py:95
  10.4 1.3 %collective-permute-start = (bf16[80,512]{1,0:T(8,128)(2,1)}, bf16[80,512]{1,0:T(8,128)(2,1)S(1)}, u32[]{:S(2)}, u32[]{:S(2)}) collective-permute-start(bf16[80,512]{1,0:T(8,128)(2,1)} %shard_map.55), channel_id=1, source_target_pairs={{0,24},{8,0},{16,8},{24,16},{1,25},{9,1},{17,9},{25,17},{2,26},{10... | collective-permute-start | bytes 245768 | tf_op jit(solution)/shard_map/ppermute | solution.py:95
  11.8 1.3 %collective-permute-done.2 = bf16[80,512]{1,0:T(8,128)(2,1)S(1)} collective-permute-done((bf16[80,512]{1,0:T(8,128)(2,1)}, bf16[80,512]{1,0:T(8,128)(2,1)S(1)}, u32[]{:S(2)}, u32[]{:S(2)}) %collective-permute-start.2) | collective-permute-done | bytes 81952 | tf_op jit(solution)/shard_map/ppermute | solution.py:95
  13.1 3.0 %collective-permute-done.1 = bf16[80,512]{1,0:T(8,128)(2,1)S(1)} collective-permute-done((bf16[80,512]{1,0:T(8,128)(2,1)}, bf16[80,512]{1,0:T(8,128)(2,1)S(1)}, u32[]{:S(2)}, u32[]{:S(2)}) %collective-permute-start.1) | collective-permute-done | bytes 81952 | tf_op jit(solution)/shard_map/ppermute | solution.py:95
  16.1 0.2 collective-permute-done
  16.3 0.9 %select_bitcast_fusion.7 = (bf16[1,80,512]{2,1,0:T(8,128)(2,1)S(1)}, bf16[1,80,512]{2,1,0:T(8,128)(2,1)S(1)}, bf16[1,80,512]{2,1,0:T(8,128)(2,1)S(1)}, bf16[1,80,512]{2,1,0:T(8,128)(2,1)S(1)}) fusion(bf16[80,512]{1,0:T(8,128)(2,1)S(1)} %collective-permute-done, bf16[80,512]{1,0:T(8,128)(2,1)S(1)} %collective-permute-done.1, ...), kind=kLoop, calls=%fused_computation.12 | loop fusion | flops 491520 | bytes 655372 | tf_op jit(solution)/shard_map/stack | solution.py:102
  17.3 0.8 %pad_maximum_fusion.1 = bf16[4,80,512]{2,1,0:T(8,128)(2,1)} fusion(bf16[1,80,512]{2,1,0:T(8,128)(2,1)S(1)} %get-tuple-element.10, bf16[1,80,512]{2,1,0:T(8,128)(2,1)S(1)} %get-tuple-element.11, bf16[1,80,512]{2,1,0:T(8,128)(2,1)S(1)} %get-tuple-element.12, bf16[1,80,512]{2,1,0:T(8,128)(2,1)S(1)} %get-tuple-element.9), kind=kLoop, calls=%fused_computation.3 | loop fusion | flops 491520 | bytes 655360 | tf_op jit(solution)/shard_map/stack | solution.py:102
  18.0 1.5 %collective-permute-start.5 = (bf16[4,80,512]{2,1,0:T(8,128)(2,1)}, bf16[4,80,512]{2,1,0:T(8,128)(2,1)S(1)}, u32[]{:S(2)}, u32[]{:S(2)}) collective-permute-start(bf16[4,80,512]{2,1,0:T(8,128)(2,1)} %pad_maximum_fusion.1), channel_id=1, source_target_pairs={{0,2},{2,4},{4,6},{6,0},{1,3},{3,5},{5,7},{7,1},{8,10},{10,12},{12... | collective-permute-start | bytes 983048 | tf_op jit(solution)/shard_map/ppermute | solution.py:95
  19.5 1.5 %collective-permute-start.4 = (bf16[4,80,512]{2,1,0:T(8,128)(2,1)}, bf16[4,80,512]{2,1,0:T(8,128)(2,1)S(1)}, u32[]{:S(2)}, u32[]{:S(2)}) collective-permute-start(bf16[4,80,512]{2,1,0:T(8,128)(2,1)} %pad_maximum_fusion.1), channel_id=1, source_target_pairs={{0,4},{2,6},{4,0},{6,2},{1,5},{3,7},{5,1},{7,3},{8,12},{10,14},{12... | collective-permute-start | bytes 983048 | tf_op jit(solution)/shard_map/ppermute | solution.py:95
  21.0 1.4 %collective-permute-start.3 = (bf16[4,80,512]{2,1,0:T(8,128)(2,1)}, bf16[4,80,512]{2,1,0:T(8,128)(2,1)S(1)}, u32[]{:S(2)}, u32[]{:S(2)}) collective-permute-start(bf16[4,80,512]{2,1,0:T(8,128)(2,1)} %pad_maximum_fusion.1), channel_id=1, source_target_pairs={{0,6},{2,0},{4,2},{6,4},{1,7},{3,1},{5,3},{7,5},{8,14},{10,8},{12,... | collective-permute-start | bytes 983048 | tf_op jit(solution)/shard_map/ppermute | solution.py:95
  22.5 7.3 %collective-permute-done.5 = bf16[4,80,512]{2,1,0:T(8,128)(2,1)S(1)} collective-permute-done((bf16[4,80,512]{2,1,0:T(8,128)(2,1)}, bf16[4,80,512]{2,1,0:T(8,128)(2,1)S(1)}, u32[]{:S(2)}, u32[]{:S(2)}) %collective-permute-start.5) | collective-permute-done | bytes 327712 | tf_op jit(solution)/shard_map/ppermute | solution.py:95
  29.8 5.7 %collective-permute-done.4 = bf16[4,80,512]{2,1,0:T(8,128)(2,1)S(1)} collective-permute-done((bf16[4,80,512]{2,1,0:T(8,128)(2,1)}, bf16[4,80,512]{2,1,0:T(8,128)(2,1)S(1)}, u32[]{:S(2)}, u32[]{:S(2)}) %collective-permute-start.4) | collective-permute-done | bytes 327712 | tf_op jit(solution)/shard_map/ppermute | solution.py:95
  35.5 0.0 collective-permute-done.3
  35.5 0.1 select_bitcast_fusion.2
  35.6 0.1 select_bitcast_fusion.3
  35.7 0.2 pad_maximum_fusion
  35.9 0.1 copy.14
  36.0 0.3 broadcast_in_dim.4
  36.3 5.8 %all_to_all.11 = bf16[4,4,2,80,512]{4,3,1,0,2:T(8,128)(2,1)S(1)} all-to-all(bf16[4,4,2,80,512]{4,3,1,0,2:T(8,128)(2,1)S(1)} %broadcast_in_dim.4), channel_id=1, replica_groups=mesh['grp'=1,'tok_o'=4,'tok_m'=4,'tok_c'=2] {'tok_c'}, dimensions={2} | all-to-all | bytes 5242880 | tf_op jit(solution)/shard_map/all_to_all | solution.py:87
  42.2 0.2 slice.8
  42.3 0.0 slice-start
  42.3 0.2 copy.19
  42.6 0.0 copy-done
  42.7 0.0 slice-start.1
  42.7 1.3 %fusion = f32[512,2048]{1,0:T(8,128)S(1)} fusion(bf16[512,512]{1,0:T(8,128)(2,1)S(1)} %bitcast.26, bf16[2048,512]{1,0:T(8,128)(2,1)S(1)} %copy-done), kind=kOutput, calls=%fused_computation.15 | convolution fusion | flops 1073741824 | bytes 6815744 | tf_op jit(solution)/shard_map/dot_general | solution.py:76
  44.0 0.5 slice-done
  44.5 1.4 %slice-done.1 = s8[4194304]{0:T(1024)(128)(4,1)S(1)} async-done(((s8[8388608]{0:T(1024)(128)(4,1)}), s8[4194304]{0:T(1024)(128)(4,1)S(1)}, s32[]{:S(2)}) %slice-start.1) | async-done | bytes 4194328
  45.9 4.8 %bitcast_reduce_fusion = f32[2048,16]{0,1:T(8,128)S(1)} fusion(f32[512,2048]{1,0:T(8,128)S(1)} %fusion, bf16[2048,512]{1,0:T(8,128)(2,1)S(1)} %bitcast.27, bf16[2048,2048]{1,0:T(8,128)(2,1)S(1)} %bitcast.29), kind=kOutput, calls=%fused_computation | convolution fusion | flops 4297031680 | bytes 14811136 | tf_op jit(solution)/shard_map/dot_general | solution.py:76
  50.7 0.1 multiply_reduce_fusion
  50.8 11.0 %all_to_all.12 = f32[32,1,16]{2,1,0:T(1,128)S(1)} all-to-all(f32[32,1,16]{2,1,0:T(1,128)S(1)} %broadcast_in_dim.5), channel_id=1, replica_groups=mesh['grp'=1,'tok_o'=4,'tok_m'=4,'tok_c'=2] {'tok_o','tok_m','tok_c'}, dimensions={0} | all-to-all | bytes 4096 | tf_op jit(solution)/shard_map/all_to_all | solution.py:81
  61.9 0.1 reduce_sum.29
  61.9 0.7 %broadcast_divide_fusion = f32[2048,16]{0,1:T(8,128)} fusion(f32[2048,16]{0,1:T(8,128)S(1)} %bitcast_reduce_fusion, f32[16]{0:T(128)S(1)} %add_sqrt_fusion), kind=kLoop, calls=%fused_computation.13 | loop fusion | flops 32768 | bytes 262208 | tf_op jit(solution)/shard_map/div | solution.py:124
  (5 shorter events, 0.1 us)
Async XLA Ops:
  0.0 42.6 %copy-start = (bf16[2048,512]{1,0:T(8,128)(2,1)S(1)}, bf16[2048,512]{1,0:T(8,128)(2,1)}, u32[]{:S(2)}) copy-start(bf16[2048,512]{1,0:T(8,128)(2,1)} %param.6) | copy-start | bytes 6291460
  4.8 8.3 %collective-permute-start.2 = (bf16[80,512]{1,0:T(8,128)(2,1)}, bf16[80,512]{1,0:T(8,128)(2,1)S(1)}, u32[]{:S(2)}, u32[]{:S(2)}) collective-permute-start(bf16[80,512]{1,0:T(8,128)(2,1)} %shard_map.55), channel_id=1, source_target_pairs={{0,8},{8,16},{16,24},{24,0},{1,9},{9,17},{17,25},{25,1},{2,10},{10... | collective-permute-start | bytes 245768 | tf_op jit(solution)/shard_map/ppermute | solution.py:95
  7.8 8.3 %collective-permute-start.1 = (bf16[80,512]{1,0:T(8,128)(2,1)}, bf16[80,512]{1,0:T(8,128)(2,1)S(1)}, u32[]{:S(2)}, u32[]{:S(2)}) collective-permute-start(bf16[80,512]{1,0:T(8,128)(2,1)} %shard_map.55), channel_id=1, source_target_pairs={{0,16},{8,24},{16,0},{24,8},{1,17},{9,25},{17,1},{25,9},{2,18},{10... | collective-permute-start | bytes 245768 | tf_op jit(solution)/shard_map/ppermute | solution.py:95
  10.4 5.9 %collective-permute-start = (bf16[80,512]{1,0:T(8,128)(2,1)}, bf16[80,512]{1,0:T(8,128)(2,1)S(1)}, u32[]{:S(2)}, u32[]{:S(2)}) collective-permute-start(bf16[80,512]{1,0:T(8,128)(2,1)} %shard_map.55), channel_id=1, source_target_pairs={{0,24},{8,0},{16,8},{24,16},{1,25},{9,1},{17,9},{25,17},{2,26},{10... | collective-permute-start | bytes 245768 | tf_op jit(solution)/shard_map/ppermute | solution.py:95
  18.0 11.8 %collective-permute-start.5 = (bf16[4,80,512]{2,1,0:T(8,128)(2,1)}, bf16[4,80,512]{2,1,0:T(8,128)(2,1)S(1)}, u32[]{:S(2)}, u32[]{:S(2)}) collective-permute-start(bf16[4,80,512]{2,1,0:T(8,128)(2,1)} %pad_maximum_fusion.1), channel_id=1, source_target_pairs={{0,2},{2,4},{4,6},{6,0},{1,3},{3,5},{5,7},{7,1},{8,10},{10,12},{12... | collective-permute-start | bytes 983048 | tf_op jit(solution)/shard_map/ppermute | solution.py:95
  19.5 16.0 %collective-permute-start.4 = (bf16[4,80,512]{2,1,0:T(8,128)(2,1)}, bf16[4,80,512]{2,1,0:T(8,128)(2,1)S(1)}, u32[]{:S(2)}, u32[]{:S(2)}) collective-permute-start(bf16[4,80,512]{2,1,0:T(8,128)(2,1)} %pad_maximum_fusion.1), channel_id=1, source_target_pairs={{0,4},{2,6},{4,0},{6,2},{1,5},{3,7},{5,1},{7,3},{8,12},{10,14},{12... | collective-permute-start | bytes 983048 | tf_op jit(solution)/shard_map/ppermute | solution.py:95
  21.0 14.5 %collective-permute-start.3 = (bf16[4,80,512]{2,1,0:T(8,128)(2,1)}, bf16[4,80,512]{2,1,0:T(8,128)(2,1)S(1)}, u32[]{:S(2)}, u32[]{:S(2)}) collective-permute-start(bf16[4,80,512]{2,1,0:T(8,128)(2,1)} %pad_maximum_fusion.1), channel_id=1, source_target_pairs={{0,6},{2,0},{4,2},{6,4},{1,7},{3,1},{5,3},{7,5},{8,14},{10,8},{12,... | collective-permute-start | bytes 983048 | tf_op jit(solution)/shard_map/ppermute | solution.py:95
  42.3 2.2 %slice-start = ((s8[8388608]{0:T(1024)(128)(4,1)}), s8[4194304]{0:T(1024)(128)(4,1)S(1)}, s32[]{:S(2)}) async-start(s8[8388608]{0:T(1024)(128)(4,1)} %bitcast.28), calls=%async_computation.2 | async-start | bytes 8388608
  42.7 3.2 %slice-start.1 = ((s8[8388608]{0:T(1024)(128)(4,1)}), s8[4194304]{0:T(1024)(128)(4,1)S(1)}, s32[]{:S(2)}) async-start(s8[8388608]{0:T(1024)(128)(4,1)} %bitcast.28), calls=%async_computation.3 | async-start | bytes 8388608

commit v16 on v9

--- a/solution.py
+++ b/solution.py
@@ -84,15 +84,15 @@
 
 def shifted(x, axis, at):
     k = lax.axis_size(axis)
-    if k > 4:
+    if k > 4 or k & (k - 1):
         return spread(x, axis, at)
     me = lax.axis_index(axis)
-    got = [x] + [lax.ppermute(x, axis, [(j, (j + s) % k) for j in range(k)]) for s in range(1, k)]
+    got = [x] + [lax.ppermute(x, axis, [(j, j ^ s) for j in range(k)]) for s in range(1, k)]
     slots = []
     for o in range(k):
         value = got[0]
         for s in range(1, k):
-            value = jnp.where((me - s + k) % k == o, got[s], value)
+            value = jnp.where(jnp.bitwise_xor(me, s) == o, got[s], value)
         slots.append(value)
     return jnp.stack(slots, axis=at)
 

time: 62.9 us -> 62.8 us (level)
  starting transfers between devices: 11.5 us -> 9.17 us
  waiting for transfers between devices: 17.6 us -> 19.3 us
    ppermute x6, starting transfers between devices: 11.5 us -> 9.17 us  [shifted(): lax.ppermute(x, axis, [(j, j ^ s) for j in range(k)])]
    ppermute x6, waiting for transfers between devices: 17.6 us -> 19.3 us  [shifted(): lax.ppermute(x, axis, [(j, j ^ s) for j in range(k)])]
  transfers between devices with their start and end apart: 6 -> 6, of which waited for: 5 -> 4; matrix products, arithmetic and copies ran while one was open for 0% -> 0% of each run, Pallas kernels for 0% -> 0%
where the time goes in v16:
time: 62.8 us; the launch traced here: 62.6 us
  waiting for transfers between devices  19.3 us (31%)
  blocking collectives  17.3 us (28%)
  starting transfers between devices  9.17 us (15%)
  matrix products  6.12 us (10%)
  Pallas kernels  4.73 us (8%)
  other arithmetic  3.01 us (5%)
  local copies, waits for them, and re-layouts  2.79 us (4%)
    ppermute x6, waiting for transfers between devices, shifted(): lax.ppermute(x, axis, [(j, j ^ s) for j in range(k)])  19.3 us
    all_to_all x1, blocking collectives, total_over(): return lax.all_to_all(copies, axis, 0, 0, tiled=False).sum(axis=0)  11.5 us
    ppermute x6, starting transfers between devices, shifted(): lax.ppermute(x, axis, [(j, j ^ s) for j in range(k)])  9.17 us
    dot_general x2, matrix products, folder(): return jnp.dot(left, piece, preferred_element_type=jnp.float32)  6.12 us
    all_to_all x1, blocking collectives, spread(): return lax.all_to_all(copies, axis, at, at, tiled=True)  5.84 us
    pallas_call x1, Pallas kernels, pick_columns(): pl.pallas_call(pick_kernel, out_shape=jax.ShapeDtypeStruct((v_bank.shape[...  4.73 us
    unnamed x8, local copies, waits for them, and re-layouts  2.16 us
    another operation x5, other arithmetic, shifted(): return jnp.stack(slots, axis=at)  2.07 us
  transfers between devices with their start and end apart: 6, of which 4 were waited for; matrix products, arithmetic and copies ran while one was open for 0% of the time, Pallas kernels for 0%

profile of v16, /device:TPU:0, one launch (start us, length us, event | category | flops | bytes accessed | tf_op | source)
XLA Modules:
  0.0 62.6 jit_solution(518414576764886972)
XLA Ops:
  0.0 0.0 copy-start
  0.0 4.7 %shard_map.55 = bf16[80,512]{1,0:T(8,128)(2,1)} custom-call(s32[16]{0:T(128)} %ids_ref.1, bf16[64,65536]{1,0:T(8,128)(2,1)} %v_ref.1, bf16[16,65536]{1,0:T(8,128)(2,1)} %u_ref.1), custom_call_target="tpu_custom_call" | custom-call | tf_op jit(solution)/shard_map/pallas_call | solution.py:47
  4.7 3.1 %collective-permute-start.2 = (bf16[80,512]{1,0:T(8,128)(2,1)}, bf16[80,512]{1,0:T(8,128)(2,1)S(1)}, u32[]{:S(2)}, u32[]{:S(2)}) collective-permute-start(bf16[80,512]{1,0:T(8,128)(2,1)} %shard_map.55), channel_id=1, source_target_pairs={{0,8},{8,0},{16,24},{24,16},{1,9},{9,1},{17,25},{25,17},{2,10},{10... | collective-permute-start | bytes 245768 | tf_op jit(solution)/shard_map/ppermute | solution.py:90
  7.8 2.6 %collective-permute-start.1 = (bf16[80,512]{1,0:T(8,128)(2,1)}, bf16[80,512]{1,0:T(8,128)(2,1)S(1)}, u32[]{:S(2)}, u32[]{:S(2)}) collective-permute-start(bf16[80,512]{1,0:T(8,128)(2,1)} %shard_map.55), channel_id=1, source_target_pairs={{0,16},{8,24},{16,0},{24,8},{1,17},{9,25},{17,1},{25,9},{2,18},{10... | collective-permute-start | bytes 245768 | tf_op jit(solution)/shard_map/ppermute | solution.py:90
  10.4 0.0 collective-permute-start
  10.4 0.1 collective-permute-done.2
  10.5 6.8 %collective-permute-done.1 = bf16[80,512]{1,0:T(8,128)(2,1)S(1)} collective-permute-done((bf16[80,512]{1,0:T(8,128)(2,1)}, bf16[80,512]{1,0:T(8,128)(2,1)S(1)}, u32[]{:S(2)}, u32[]{:S(2)}) %collective-permute-start.1) | collective-permute-done | bytes 81952 | tf_op jit(solution)/shard_map/ppermute | solution.py:90
  17.3 0.0 collective-permute-done
  17.3 0.9 %select_bitcast_fusion.7 = (bf16[1,80,512]{2,1,0:T(8,128)(2,1)S(1)}, bf16[1,80,512]{2,1,0:T(8,128)(2,1)S(1)}, bf16[1,80,512]{2,1,0:T(8,128)(2,1)S(1)}, bf16[1,80,512]{2,1,0:T(8,128)(2,1)S(1)}) fusion(bf16[80,512]{1,0:T(8,128)(2,1)S(1)} %collective-permute-done, bf16[80,512]{1,0:T(8,128)(2,1)S(1)} %collective-permute-done.1, ...), kind=kLoop, calls=%fused_computation.12 | loop fusion | flops 491520 | bytes 655372 | tf_op jit(solution)/shard_map/stack | solution.py:97
  18.2 0.8 %pad_maximum_fusion.1 = bf16[4,80,512]{2,1,0:T(8,128)(2,1)} fusion(bf16[1,80,512]{2,1,0:T(8,128)(2,1)S(1)} %get-tuple-element.10, bf16[1,80,512]{2,1,0:T(8,128)(2,1)S(1)} %get-tuple-element.11, bf16[1,80,512]{2,1,0:T(8,128)(2,1)S(1)} %get-tuple-element.12, bf16[1,80,512]{2,1,0:T(8,128)(2,1)S(1)} %get-tuple-element.9), kind=kLoop, calls=%fused_computation.3 | loop fusion | flops 491520 | bytes 655360 | tf_op jit(solution)/shard_map/stack | solution.py:97
  19.0 1.5 %collective-permute-start.5 = (bf16[4,80,512]{2,1,0:T(8,128)(2,1)}, bf16[4,80,512]{2,1,0:T(8,128)(2,1)S(1)}, u32[]{:S(2)}, u32[]{:S(2)}) collective-permute-start(bf16[4,80,512]{2,1,0:T(8,128)(2,1)} %pad_maximum_fusion.1), channel_id=1, source_target_pairs={{0,2},{2,0},{4,6},{6,4},{1,3},{3,1},{5,7},{7,5},{8,10},{10,8},{12,... | collective-permute-start | bytes 983048 | tf_op jit(solution)/shard_map/ppermute | solution.py:90
  20.5 1.5 %collective-permute-start.4 = (bf16[4,80,512]{2,1,0:T(8,128)(2,1)}, bf16[4,80,512]{2,1,0:T(8,128)(2,1)S(1)}, u32[]{:S(2)}, u32[]{:S(2)}) collective-permute-start(bf16[4,80,512]{2,1,0:T(8,128)(2,1)} %pad_maximum_fusion.1), channel_id=1, source_target_pairs={{0,4},{2,6},{4,0},{6,2},{1,5},{3,7},{5,1},{7,3},{8,12},{10,14},{12... | collective-permute-start | bytes 983048 | tf_op jit(solution)/shard_map/ppermute | solution.py:90
  22.0 0.5 collective-permute-start.3
  22.5 7.4 %collective-permute-done.5 = bf16[4,80,512]{2,1,0:T(8,128)(2,1)S(1)} collective-permute-done((bf16[4,80,512]{2,1,0:T(8,128)(2,1)}, bf16[4,80,512]{2,1,0:T(8,128)(2,1)S(1)}, u32[]{:S(2)}, u32[]{:S(2)}) %collective-permute-start.5) | collective-permute-done | bytes 327712 | tf_op jit(solution)/shard_map/ppermute | solution.py:90
  29.8 5.1 %collective-permute-done.4 = bf16[4,80,512]{2,1,0:T(8,128)(2,1)S(1)} collective-permute-done((bf16[4,80,512]{2,1,0:T(8,128)(2,1)}, bf16[4,80,512]{2,1,0:T(8,128)(2,1)S(1)}, u32[]{:S(2)}, u32[]{:S(2)}) %collective-permute-start.4) | collective-permute-done | bytes 327712 | tf_op jit(solution)/shard_map/ppermute | solution.py:90
  34.9 0.0 collective-permute-done.3
  34.9 0.1 select_bitcast_fusion.2
  35.0 0.1 select_bitcast_fusion.3
  35.1 0.2 pad_maximum_fusion
  35.3 0.1 copy.14
  35.4 0.3 broadcast_in_dim.4
  35.7 5.8 %all_to_all.11 = bf16[4,4,2,80,512]{4,3,1,0,2:T(8,128)(2,1)S(1)} all-to-all(bf16[4,4,2,80,512]{4,3,1,0,2:T(8,128)(2,1)S(1)} %broadcast_in_dim.4), channel_id=1, replica_groups=mesh['grp'=1,'tok_o'=4,'tok_m'=4,'tok_c'=2] {'tok_c'}, dimensions={2} | all-to-all | bytes 5242880 | tf_op jit(solution)/shard_map/all_to_all | solution.py:82
  41.6 0.2 slice.8
  41.7 0.0 slice-start
  41.7 0.2 copy.19
  42.1 0.0 copy-done
  42.1 0.0 slice-start.1
  42.1 1.3 %fusion = f32[512,2048]{1,0:T(8,128)S(1)} fusion(bf16[512,512]{1,0:T(8,128)(2,1)S(1)} %bitcast.26, bf16[2048,512]{1,0:T(8,128)(2,1)S(1)} %copy-done), kind=kOutput, calls=%fused_computation.15 | convolution fusion | flops 1073741824 | bytes 6815744 | tf_op jit(solution)/shard_map/dot_general | solution.py:71
  43.4 0.5 slice-done
  43.9 1.4 %slice-done.1 = s8[4194304]{0:T(1024)(128)(4,1)S(1)} async-done(((s8[8388608]{0:T(1024)(128)(4,1)}), s8[4194304]{0:T(1024)(128)(4,1)S(1)}, s32[]{:S(2)}) %slice-start.1) | async-done | bytes 4194328
  45.3 4.8 %bitcast_reduce_fusion = f32[2048,16]{0,1:T(8,128)S(1)} fusion(f32[512,2048]{1,0:T(8,128)S(1)} %fusion, bf16[2048,512]{1,0:T(8,128)(2,1)S(1)} %bitcast.27, bf16[2048,2048]{1,0:T(8,128)(2,1)S(1)} %bitcast.29), kind=kOutput, calls=%fused_computation | convolution fusion | flops 4297031680 | bytes 14811136 | tf_op jit(solution)/shard_map/dot_general | solution.py:71
  50.1 0.1 multiply_reduce_fusion
  50.3 11.5 %all_to_all.12 = f32[32,1,16]{2,1,0:T(1,128)S(1)} all-to-all(f32[32,1,16]{2,1,0:T(1,128)S(1)} %broadcast_in_dim.5), channel_id=1, replica_groups=mesh['grp'=1,'tok_o'=4,'tok_m'=4,'tok_c'=2] {'tok_o','tok_m','tok_c'}, dimensions={0} | all-to-all | bytes 4096 | tf_op jit(solution)/shard_map/all_to_all | solution.py:76
  61.7 0.1 reduce_sum.29
  61.8 0.7 %broadcast_divide_fusion = f32[2048,16]{0,1:T(8,128)} fusion(f32[2048,16]{0,1:T(8,128)S(1)} %bitcast_reduce_fusion, f32[16]{0:T(128)S(1)} %add_sqrt_fusion), kind=kLoop, calls=%fused_computation.13 | loop fusion | flops 32768 | bytes 262208 | tf_op jit(solution)/shard_map/div | solution.py:119
  (5 shorter events, 0.1 us)
Async XLA Ops:
  0.0 42.1 %copy-start = (bf16[2048,512]{1,0:T(8,128)(2,1)S(1)}, bf16[2048,512]{1,0:T(8,128)(2,1)}, u32[]{:S(2)}) copy-start(bf16[2048,512]{1,0:T(8,128)(2,1)} %param.6) | copy-start | bytes 6291460
  4.7 5.7 %collective-permute-start.2 = (bf16[80,512]{1,0:T(8,128)(2,1)}, bf16[80,512]{1,0:T(8,128)(2,1)S(1)}, u32[]{:S(2)}, u32[]{:S(2)}) collective-permute-start(bf16[80,512]{1,0:T(8,128)(2,1)} %shard_map.55), channel_id=1, source_target_pairs={{0,8},{8,0},{16,24},{24,16},{1,9},{9,1},{17,25},{25,17},{2,10},{10... | collective-permute-start | bytes 245768 | tf_op jit(solution)/shard_map/ppermute | solution.py:90
  7.8 9.4 %collective-permute-start.1 = (bf16[80,512]{1,0:T(8,128)(2,1)}, bf16[80,512]{1,0:T(8,128)(2,1)S(1)}, u32[]{:S(2)}, u32[]{:S(2)}) collective-permute-start(bf16[80,512]{1,0:T(8,128)(2,1)} %shard_map.55), channel_id=1, source_target_pairs={{0,16},{8,24},{16,0},{24,8},{1,17},{9,25},{17,1},{25,9},{2,18},{10... | collective-permute-start | bytes 245768 | tf_op jit(solution)/shard_map/ppermute | solution.py:90
  10.4 6.8 %collective-permute-start = (bf16[80,512]{1,0:T(8,128)(2,1)}, bf16[80,512]{1,0:T(8,128)(2,1)S(1)}, u32[]{:S(2)}, u32[]{:S(2)}) collective-permute-start(bf16[80,512]{1,0:T(8,128)(2,1)} %shard_map.55), channel_id=1, source_target_pairs={{0,24},{8,16},{16,8},{24,0},{1,25},{9,17},{17,9},{25,1},{2,26},{10... | collective-permute-start | bytes 245768 | tf_op jit(solution)/shard_map/ppermute | solution.py:90
  19.0 10.9 %collective-permute-start.5 = (bf16[4,80,512]{2,1,0:T(8,128)(2,1)}, bf16[4,80,512]{2,1,0:T(8,128)(2,1)S(1)}, u32[]{:S(2)}, u32[]{:S(2)}) collective-permute-start(bf16[4,80,512]{2,1,0:T(8,128)(2,1)} %pad_maximum_fusion.1), channel_id=1, source_target_pairs={{0,2},{2,0},{4,6},{6,4},{1,3},{3,1},{5,7},{7,5},{8,10},{10,8},{12,... | collective-permute-start | bytes 983048 | tf_op jit(solution)/shard_map/ppermute | solution.py:90
  20.5 14.4 %collective-permute-start.4 = (bf16[4,80,512]{2,1,0:T(8,128)(2,1)}, bf16[4,80,512]{2,1,0:T(8,128)(2,1)S(1)}, u32[]{:S(2)}, u32[]{:S(2)}) collective-permute-start(bf16[4,80,512]{2,1,0:T(8,128)(2,1)} %pad_maximum_fusion.1), channel_id=1, source_target_pairs={{0,4},{2,6},{4,0},{6,2},{1,5},{3,7},{5,1},{7,3},{8,12},{10,14},{12... | collective-permute-start | bytes 983048 | tf_op jit(solution)/shard_map/ppermute | solution.py:90
  22.0 12.9 %collective-permute-start.3 = (bf16[4,80,512]{2,1,0:T(8,128)(2,1)}, bf16[4,80,512]{2,1,0:T(8,128)(2,1)S(1)}, u32[]{:S(2)}, u32[]{:S(2)}) collective-permute-start(bf16[4,80,512]{2,1,0:T(8,128)(2,1)} %pad_maximum_fusion.1), channel_id=1, source_target_pairs={{0,6},{2,4},{4,2},{6,0},{1,7},{3,5},{5,3},{7,1},{8,14},{10,12},{12... | collective-permute-start | bytes 983048 | tf_op jit(solution)/shard_map/ppermute | solution.py:90
  41.7 2.2 %slice-start = ((s8[8388608]{0:T(1024)(128)(4,1)}), s8[4194304]{0:T(1024)(128)(4,1)S(1)}, s32[]{:S(2)}) async-start(s8[8388608]{0:T(1024)(128)(4,1)} %bitcast.28), calls=%async_computation.2 | async-start | bytes 8388608
  42.1 3.2 %slice-start.1 = ((s8[8388608]{0:T(1024)(128)(4,1)}), s8[4194304]{0:T(1024)(128)(4,1)S(1)}, s32[]{:S(2)}) async-start(s8[8388608]{0:T(1024)(128)(4,1)} %bitcast.28), calls=%async_computation.3 | async-start | bytes 8388608

commit v17 on v16

--- a/solution.py
+++ b/solution.py
@@ -21,6 +21,8 @@
             copy = pltpu.make_async_copy(bank.at[:, pl.ds(start, LANES)], buf.at[q], sems.at[k, q])
             copy.start()
             copies.append(copy)
+    for copy in copies:
+        copy.wait()
     bases = (0, v_buf.shape[1])
     for k, buf in enumerate((v_buf, u_buf)):
         rows = buf.shape[1]
@@ -30,7 +32,6 @@
             acc = jnp.zeros((rows, LANES), buf.dtype)
             for j in range(PER_TILE):
                 q = g * PER_TILE + j
-                copies[k * queries + q].wait()
                 x = buf[q]
                 off = (ids_ref[q] % PER_TILE) * RANK
                 shift = (RANK * j - off + LANES) % LANES

time: 62.8 us -> 61 us (0.971)
  Pallas kernels: 4.73 us -> 2.93 us
    pallas_call x1, Pallas kernels: 4.73 us -> 2.93 us  [pick_columns(): pl.pallas_call(pick_kernel, out_shape=jax.ShapeDtypeStruct((v_bank.shape[...]
where the time goes in v17:
time: 61 us; the launch traced here: 60.7 us
  waiting for transfers between devices  19.3 us (32%)
  blocking collectives  17.3 us (28%)
  starting transfers between devices  9.17 us (15%)
  matrix products  6.12 us (10%)
  other arithmetic  3.01 us (5%)
  Pallas kernels  2.93 us (5%)
  local copies, waits for them, and re-layouts  2.79 us (5%)
    ppermute x6, waiting for transfers between devices, shifted(): lax.ppermute(x, axis, [(j, j ^ s) for j in range(k)])  19.3 us
    all_to_all x1, blocking collectives, total_over(): return lax.all_to_all(copies, axis, 0, 0, tiled=False).sum(axis=0)  11.5 us
    ppermute x6, starting transfers between devices, shifted(): lax.ppermute(x, axis, [(j, j ^ s) for j in range(k)])  9.17 us
    dot_general x2, matrix products, folder(): return jnp.dot(left, piece, preferred_element_type=jnp.float32)  6.12 us
    all_to_all x1, blocking collectives, spread(): return lax.all_to_all(copies, axis, at, at, tiled=True)  5.84 us
    pallas_call x1, Pallas kernels, pick_columns(): pl.pallas_call(pick_kernel, out_shape=jax.ShapeDtypeStruct((v_bank.shape[...  2.93 us
    unnamed x8, local copies, waits for them, and re-layouts  2.16 us
    another operation x5, other arithmetic, shifted(): return jnp.stack(slots, axis=at)  2.07 us
  transfers between devices with their start and end apart: 6, of which 4 were waited for; matrix products, arithmetic and copies ran while one was open for 0% of the time, Pallas kernels for 0%

profile of v17, /device:TPU:0, one launch (start us, length us, event | category | flops | bytes accessed | tf_op | source)
XLA Modules:
  0.0 60.7 jit_solution(11381340864060272397)
XLA Ops:
  0.0 0.0 copy-start
  0.0 2.9 %shard_map.55 = bf16[80,512]{1,0:T(8,128)(2,1)} custom-call(s32[16]{0:T(128)} %ids_ref.1, bf16[64,65536]{1,0:T(8,128)(2,1)} %v_ref.1, bf16[16,65536]{1,0:T(8,128)(2,1)} %u_ref.1), custom_call_target="tpu_custom_call" | custom-call | tf_op jit(solution)/shard_map/pallas_call | solution.py:48
  2.9 3.1 %collective-permute-start.2 = (bf16[80,512]{1,0:T(8,128)(2,1)}, bf16[80,512]{1,0:T(8,128)(2,1)S(1)}, u32[]{:S(2)}, u32[]{:S(2)}) collective-permute-start(bf16[80,512]{1,0:T(8,128)(2,1)} %shard_map.55), channel_id=1, source_target_pairs={{0,8},{8,0},{16,24},{24,16},{1,9},{9,1},{17,25},{25,17},{2,10},{10... | collective-permute-start | bytes 245768 | tf_op jit(solution)/shard_map/ppermute | solution.py:91
  6.0 2.6 %collective-permute-start.1 = (bf16[80,512]{1,0:T(8,128)(2,1)}, bf16[80,512]{1,0:T(8,128)(2,1)S(1)}, u32[]{:S(2)}, u32[]{:S(2)}) collective-permute-start(bf16[80,512]{1,0:T(8,128)(2,1)} %shard_map.55), channel_id=1, source_target_pairs={{0,16},{8,24},{16,0},{24,8},{1,17},{9,25},{17,1},{25,9},{2,18},{10... | collective-permute-start | bytes 245768 | tf_op jit(solution)/shard_map/ppermute | solution.py:91
  8.6 0.0 collective-permute-start
  8.6 0.1 collective-permute-done.2
  8.7 6.8 %collective-permute-done.1 = bf16[80,512]{1,0:T(8,128)(2,1)S(1)} collective-permute-done((bf16[80,512]{1,0:T(8,128)(2,1)}, bf16[80,512]{1,0:T(8,128)(2,1)S(1)}, u32[]{:S(2)}, u32[]{:S(2)}) %collective-permute-start.1) | collective-permute-done | bytes 81952 | tf_op jit(solution)/shard_map/ppermute | solution.py:91
  15.5 0.0 collective-permute-done
  15.5 0.9 %select_bitcast_fusion.7 = (bf16[1,80,512]{2,1,0:T(8,128)(2,1)S(1)}, bf16[1,80,512]{2,1,0:T(8,128)(2,1)S(1)}, bf16[1,80,512]{2,1,0:T(8,128)(2,1)S(1)}, bf16[1,80,512]{2,1,0:T(8,128)(2,1)S(1)}) fusion(bf16[80,512]{1,0:T(8,128)(2,1)S(1)} %collective-permute-done, bf16[80,512]{1,0:T(8,128)(2,1)S(1)} %collective-permute-done.1, ...), kind=kLoop, calls=%fused_computation.12 | loop fusion | flops 491520 | bytes 655372 | tf_op jit(solution)/shard_map/stack | solution.py:98
  16.4 0.8 %pad_maximum_fusion.1 = bf16[4,80,512]{2,1,0:T(8,128)(2,1)} fusion(bf16[1,80,512]{2,1,0:T(8,128)(2,1)S(1)} %get-tuple-element.10, bf16[1,80,512]{2,1,0:T(8,128)(2,1)S(1)} %get-tuple-element.11, bf16[1,80,512]{2,1,0:T(8,128)(2,1)S(1)} %get-tuple-element.12, bf16[1,80,512]{2,1,0:T(8,128)(2,1)S(1)} %get-tuple-element.9), kind=kLoop, calls=%fused_computation.3 | loop fusion | flops 491520 | bytes 655360 | tf_op jit(solution)/shard_map/stack | solution.py:98
  17.2 1.5 %collective-permute-start.5 = (bf16[4,80,512]{2,1,0:T(8,128)(2,1)}, bf16[4,80,512]{2,1,0:T(8,128)(2,1)S(1)}, u32[]{:S(2)}, u32[]{:S(2)}) collective-permute-start(bf16[4,80,512]{2,1,0:T(8,128)(2,1)} %pad_maximum_fusion.1), channel_id=1, source_target_pairs={{0,2},{2,0},{4,6},{6,4},{1,3},{3,1},{5,7},{7,5},{8,10},{10,8},{12,... | collective-permute-start | bytes 983048 | tf_op jit(solution)/shard_map/ppermute | solution.py:91
  18.7 1.5 %collective-permute-start.4 = (bf16[4,80,512]{2,1,0:T(8,128)(2,1)}, bf16[4,80,512]{2,1,0:T(8,128)(2,1)S(1)}, u32[]{:S(2)}, u32[]{:S(2)}) collective-permute-start(bf16[4,80,512]{2,1,0:T(8,128)(2,1)} %pad_maximum_fusion.1), channel_id=1, source_target_pairs={{0,4},{2,6},{4,0},{6,2},{1,5},{3,7},{5,1},{7,3},{8,12},{10,14},{12... | collective-permute-start | bytes 983048 | tf_op jit(solution)/shard_map/ppermute | solution.py:91
  20.2 0.5 collective-permute-start.3
  20.6 7.4 %collective-permute-done.5 = bf16[4,80,512]{2,1,0:T(8,128)(2,1)S(1)} collective-permute-done((bf16[4,80,512]{2,1,0:T(8,128)(2,1)}, bf16[4,80,512]{2,1,0:T(8,128)(2,1)S(1)}, u32[]{:S(2)}, u32[]{:S(2)}) %collective-permute-start.5) | collective-permute-done | bytes 327712 | tf_op jit(solution)/shard_map/ppermute | solution.py:91
  28.0 5.1 %collective-permute-done.4 = bf16[4,80,512]{2,1,0:T(8,128)(2,1)S(1)} collective-permute-done((bf16[4,80,512]{2,1,0:T(8,128)(2,1)}, bf16[4,80,512]{2,1,0:T(8,128)(2,1)S(1)}, u32[]{:S(2)}, u32[]{:S(2)}) %collective-permute-start.4) | collective-permute-done | bytes 327712 | tf_op jit(solution)/shard_map/ppermute | solution.py:91
  33.1 0.0 collective-permute-done.3
  33.1 0.1 select_bitcast_fusion.2
  33.2 0.1 select_bitcast_fusion.3
  33.3 0.2 pad_maximum_fusion
  33.5 0.1 copy.14
  33.6 0.3 broadcast_in_dim.4
  33.9 5.8 %all_to_all.11 = bf16[4,4,2,80,512]{4,3,1,0,2:T(8,128)(2,1)S(1)} all-to-all(bf16[4,4,2,80,512]{4,3,1,0,2:T(8,128)(2,1)S(1)} %broadcast_in_dim.4), channel_id=1, replica_groups=mesh['grp'=1,'tok_o'=4,'tok_m'=4,'tok_c'=2] {'tok_c'}, dimensions={2} | all-to-all | bytes 5242880 | tf_op jit(solution)/shard_map/all_to_all | solution.py:83
  39.8 0.2 slice.8
  39.9 0.0 slice-start
  39.9 0.2 copy.19
  40.2 0.0 copy-done
  40.3 0.0 slice-start.1
  40.3 1.3 %fusion = f32[512,2048]{1,0:T(8,128)S(1)} fusion(bf16[512,512]{1,0:T(8,128)(2,1)S(1)} %bitcast.26, bf16[2048,512]{1,0:T(8,128)(2,1)S(1)} %copy-done), kind=kOutput, calls=%fused_computation.15 | convolution fusion | flops 1073741824 | bytes 6815744 | tf_op jit(solution)/shard_map/dot_general | solution.py:72
  41.6 0.5 slice-done
  42.1 1.4 %slice-done.1 = s8[4194304]{0:T(1024)(128)(4,1)S(1)} async-done(((s8[8388608]{0:T(1024)(128)(4,1)}), s8[4194304]{0:T(1024)(128)(4,1)S(1)}, s32[]{:S(2)}) %slice-start.1) | async-done | bytes 4194328
  43.5 4.8 %bitcast_reduce_fusion = f32[2048,16]{0,1:T(8,128)S(1)} fusion(f32[512,2048]{1,0:T(8,128)S(1)} %fusion, bf16[2048,512]{1,0:T(8,128)(2,1)S(1)} %bitcast.27, bf16[2048,2048]{1,0:T(8,128)(2,1)S(1)} %bitcast.29), kind=kOutput, calls=%fused_computation | convolution fusion | flops 4297031680 | bytes 14811136 | tf_op jit(solution)/shard_map/dot_general | solution.py:72
  48.3 0.1 multiply_reduce_fusion
  48.5 11.5 %all_to_all.12 = f32[32,1,16]{2,1,0:T(1,128)S(1)} all-to-all(f32[32,1,16]{2,1,0:T(1,128)S(1)} %broadcast_in_dim.5), channel_id=1, replica_groups=mesh['grp'=1,'tok_o'=4,'tok_m'=4,'tok_c'=2] {'tok_o','tok_m','tok_c'}, dimensions={0} | all-to-all | bytes 4096 | tf_op jit(solution)/shard_map/all_to_all | solution.py:77
  59.9 0.1 reduce_sum.29
  60.0 0.7 %broadcast_divide_fusion = f32[2048,16]{0,1:T(8,128)} fusion(f32[2048,16]{0,1:T(8,128)S(1)} %bitcast_reduce_fusion, f32[16]{0:T(128)S(1)} %add_sqrt_fusion), kind=kLoop, calls=%fused_computation.13 | loop fusion | flops 32768 | bytes 262208 | tf_op jit(solution)/shard_map/div | solution.py:120
  (5 shorter events, 0.1 us)
Async XLA Ops:
  0.0 40.3 %copy-start = (bf16[2048,512]{1,0:T(8,128)(2,1)S(1)}, bf16[2048,512]{1,0:T(8,128)(2,1)}, u32[]{:S(2)}) copy-start(bf16[2048,512]{1,0:T(8,128)(2,1)} %param.6) | copy-start | bytes 6291460
  2.9 5.7 %collective-permute-start.2 = (bf16[80,512]{1,0:T(8,128)(2,1)}, bf16[80,512]{1,0:T(8,128)(2,1)S(1)}, u32[]{:S(2)}, u32[]{:S(2)}) collective-permute-start(bf16[80,512]{1,0:T(8,128)(2,1)} %shard_map.55), channel_id=1, source_target_pairs={{0,8},{8,0},{16,24},{24,16},{1,9},{9,1},{17,25},{25,17},{2,10},{10... | collective-permute-start | bytes 245768 | tf_op jit(solution)/shard_map/ppermute | solution.py:91
  6.0 9.4 %collective-permute-start.1 = (bf16[80,512]{1,0:T(8,128)(2,1)}, bf16[80,512]{1,0:T(8,128)(2,1)S(1)}, u32[]{:S(2)}, u32[]{:S(2)}) collective-permute-start(bf16[80,512]{1,0:T(8,128)(2,1)} %shard_map.55), channel_id=1, source_target_pairs={{0,16},{8,24},{16,0},{24,8},{1,17},{9,25},{17,1},{25,9},{2,18},{10... | collective-permute-start | bytes 245768 | tf_op jit(solution)/shard_map/ppermute | solution.py:91
  8.6 6.8 %collective-permute-start = (bf16[80,512]{1,0:T(8,128)(2,1)}, bf16[80,512]{1,0:T(8,128)(2,1)S(1)}, u32[]{:S(2)}, u32[]{:S(2)}) collective-permute-start(bf16[80,512]{1,0:T(8,128)(2,1)} %shard_map.55), channel_id=1, source_target_pairs={{0,24},{8,16},{16,8},{24,0},{1,25},{9,17},{17,9},{25,1},{2,26},{10... | collective-permute-start | bytes 245768 | tf_op jit(solution)/shard_map/ppermute | solution.py:91
  17.2 10.9 %collective-permute-start.5 = (bf16[4,80,512]{2,1,0:T(8,128)(2,1)}, bf16[4,80,512]{2,1,0:T(8,128)(2,1)S(1)}, u32[]{:S(2)}, u32[]{:S(2)}) collective-permute-start(bf16[4,80,512]{2,1,0:T(8,128)(2,1)} %pad_maximum_fusion.1), channel_id=1, source_target_pairs={{0,2},{2,0},{4,6},{6,4},{1,3},{3,1},{5,7},{7,5},{8,10},{10,8},{12,... | collective-permute-start | bytes 983048 | tf_op jit(solution)/shard_map/ppermute | solution.py:91
  18.7 14.4 %collective-permute-start.4 = (bf16[4,80,512]{2,1,0:T(8,128)(2,1)}, bf16[4,80,512]{2,1,0:T(8,128)(2,1)S(1)}, u32[]{:S(2)}, u32[]{:S(2)}) collective-permute-start(bf16[4,80,512]{2,1,0:T(8,128)(2,1)} %pad_maximum_fusion.1), channel_id=1, source_target_pairs={{0,4},{2,6},{4,0},{6,2},{1,5},{3,7},{5,1},{7,3},{8,12},{10,14},{12... | collective-permute-start | bytes 983048 | tf_op jit(solution)/shard_map/ppermute | solution.py:91
  20.2 12.9 %collective-permute-start.3 = (bf16[4,80,512]{2,1,0:T(8,128)(2,1)}, bf16[4,80,512]{2,1,0:T(8,128)(2,1)S(1)}, u32[]{:S(2)}, u32[]{:S(2)}) collective-permute-start(bf16[4,80,512]{2,1,0:T(8,128)(2,1)} %pad_maximum_fusion.1), channel_id=1, source_target_pairs={{0,6},{2,4},{4,2},{6,0},{1,7},{3,5},{5,3},{7,1},{8,14},{10,12},{12... | collective-permute-start | bytes 983048 | tf_op jit(solution)/shard_map/ppermute | solution.py:91
  39.9 2.2 %slice-start = ((s8[8388608]{0:T(1024)(128)(4,1)}), s8[4194304]{0:T(1024)(128)(4,1)S(1)}, s32[]{:S(2)}) async-start(s8[8388608]{0:T(1024)(128)(4,1)} %bitcast.28), calls=%async_computation.2 | async-start | bytes 8388608
  40.3 3.2 %slice-start.1 = ((s8[8388608]{0:T(1024)(128)(4,1)}), s8[4194304]{0:T(1024)(128)(4,1)S(1)}, s32[]{:S(2)}) async-start(s8[8388608]{0:T(1024)(128)(4,1)} %bitcast.28), calls=%async_computation.3 | async-start | bytes 8388608

commit v18 on v17

--- a/solution.py
+++ b/solution.py
@@ -89,13 +89,9 @@
         return spread(x, axis, at)
     me = lax.axis_index(axis)
     got = [x] + [lax.ppermute(x, axis, [(j, j ^ s) for j in range(k)]) for s in range(1, k)]
-    slots = []
-    for o in range(k):
-        value = got[0]
-        for s in range(1, k):
-            value = jnp.where(jnp.bitwise_xor(me, s) == o, got[s], value)
-        slots.append(value)
-    return jnp.stack(slots, axis=at)
+    by_partner = jnp.stack(got, axis=at)
+    order = jnp.bitwise_xor(me, jnp.arange(k, dtype=me.dtype))
+    return jnp.take(by_partner, order, axis=at, mode="clip")
 
 
 def gather_factors(both, rows_v):

time: 61 us -> 66.3 us (1.087)
  local copies, waits for them, and re-layouts: 2.79 us -> 7.1 us
  waiting for transfers between devices: 19.3 us -> 20 us
    gather x0 -> x3, local copies, waits for them, and re-layouts: none -> 3.68 us  [shifted(): return jnp.take(by_partner, order, axis=at, mode='clip')]
    ppermute x6, waiting for transfers between devices: 19.3 us -> 20 us  [shifted(): lax.ppermute(x, axis, [(j, j ^ s) for j in range(k)])]
    unnamed x8 -> x16, local copies, waits for them, and re-layouts: 2.16 us -> 2.9 us
    another operation x5 -> x2, other arithmetic: 2.07 us -> 2.36 us  [shifted(): by_partner = jnp.stack(got, axis=at)]
  transfers between devices with their start and end apart: 6 -> 6, of which waited for: 4 -> 5; matrix products, arithmetic and copies ran while one was open for 0% -> 0% of each run, Pallas kernels for 0% -> 0%
where the time goes in v18:
time: 66.3 us; the launch traced here: 66 us
  waiting for transfers between devices  20 us (30%)
  blocking collectives  17.1 us (26%)
  starting transfers between devices  9.31 us (14%)
  local copies, waits for them, and re-layouts  7.1 us (11%)
  matrix products  6.12 us (9%)
  other arithmetic  3.33 us (5%)
  Pallas kernels  2.93 us (4%)
    ppermute x6, waiting for transfers between devices, shifted(): lax.ppermute(x, axis, [(j, j ^ s) for j in range(k)])  20 us
    all_to_all x1, blocking collectives, total_over(): return lax.all_to_all(copies, axis, 0, 0, tiled=False).sum(axis=0)  11.2 us
    ppermute x6, starting transfers between devices, shifted(): lax.ppermute(x, axis, [(j, j ^ s) for j in range(k)])  9.31 us
    dot_general x2, matrix products, folder(): return jnp.dot(left, piece, preferred_element_type=jnp.float32)  6.12 us
    all_to_all x1, blocking collectives, spread(): return lax.all_to_all(copies, axis, at, at, tiled=True)  5.84 us
    gather x3, local copies, waits for them, and re-layouts, shifted(): return jnp.take(by_partner, order, axis=at, mode='clip')  3.68 us
    pallas_call x1, Pallas kernels, pick_columns(): pl.pallas_call(pick_kernel, out_shape=jax.ShapeDtypeStruct((v_bank.shape[...  2.93 us
    unnamed x16, local copies, waits for them, and re-layouts  2.9 us
  transfers between devices with their start and end apart: 6, of which 5 were waited for; matrix products, arithmetic and copies ran while one was open for 0% of the time, Pallas kernels for 0%

profile of v18, /device:TPU:0, one launch (start us, length us, event | category | flops | bytes accessed | tf_op | source)
XLA Modules:
  0.0 66.0 jit_solution(18116701940160544091)
XLA Ops:
  0.0 0.0 copy-start
  0.0 2.9 %shard_map.55 = bf16[80,512]{1,0:T(8,128)(2,1)} custom-call(s32[16]{0:T(128)} %ids_ref.1, bf16[64,65536]{1,0:T(8,128)(2,1)} %v_ref.1, bf16[16,65536]{1,0:T(8,128)(2,1)} %u_ref.1), custom_call_target="tpu_custom_call" | custom-call | tf_op jit(solution)/shard_map/pallas_call | solution.py:48
  2.9 5.1 %collective-permute-start.2 = (bf16[80,512]{1,0:T(8,128)(2,1)}, bf16[80,512]{1,0:T(8,128)(2,1)S(1)}, u32[]{:S(2)}, u32[]{:S(2)}) collective-permute-start(bf16[80,512]{1,0:T(8,128)(2,1)} %shard_map.55), channel_id=1, source_target_pairs={{0,24},{8,16},{16,8},{24,0},{1,25},{9,17},{17,9},{25,1},{2,26},{10... | collective-permute-start | bytes 245768 | tf_op jit(solution)/shard_map/ppermute | solution.py:91
  8.1 0.0 collective-permute-start.1
  8.1 0.6 collective-permute-start
  8.7 2.6 %collective-permute-done.2 = bf16[80,512]{1,0:T(8,128)(2,1)S(1)} collective-permute-done((bf16[80,512]{1,0:T(8,128)(2,1)}, bf16[80,512]{1,0:T(8,128)(2,1)S(1)}, u32[]{:S(2)}, u32[]{:S(2)}) %collective-permute-start.2) | collective-permute-done | bytes 81952 | tf_op jit(solution)/shard_map/ppermute | solution.py:91
  11.3 3.8 %collective-permute-done.1 = bf16[80,512]{1,0:T(8,128)(2,1)S(1)} collective-permute-done((bf16[80,512]{1,0:T(8,128)(2,1)}, bf16[80,512]{1,0:T(8,128)(2,1)S(1)}, u32[]{:S(2)}, u32[]{:S(2)}) %collective-permute-start.1) | collective-permute-done | bytes 81952 | tf_op jit(solution)/shard_map/ppermute | solution.py:91
  15.1 0.0 collective-permute-done
  15.1 0.9 %pad_maximum_fusion.1 = bf16[4,80,512]{2,1,0:T(8,128)(2,1)S(1)} fusion(bf16[1,80,512]{2,1,0:T(8,128)(2,1)S(1)} %bitcast.31, bf16[1,80,512]{2,1,0:T(8,128)(2,1)S(1)} %bitcast.32, bf16[1,80,512]{2,1,0:T(8,128)(2,1)S(1)} %bitcast.33, bf16[1,80,512]{2,1,0:T(8,128)(2,1)} %bitcast.27), kind=kLoop, calls=%fused_computation.5 | loop fusion | flops 491520 | bytes 655360 | tf_op jit(solution)/shard_map/stack | solution.py:92
  16.1 0.6 gather_fusion
  16.6 0.0 copy-start.1
  16.7 1.6 %collective-permute-start.4 = (bf16[4,80,512]{2,1,0:T(8,128)(2,1)S(1)}, bf16[4,80,512]{2,1,0:T(8,128)(2,1)S(1)}, u32[]{:S(2)}, u32[]{:S(2)}) collective-permute-start(bf16[4,80,512]{2,1,0:T(8,128)(2,1)S(1)} %gather_fusion), channel_id=1, source_target_pairs={{0,4},{2,6},{4,0},{6,2},{1,5},{3,7},{5,1},{7,3},{8,12},{10,14},{12... | collective-permute-start | bytes 983048 | tf_op jit(solution)/shard_map/ppermute | solution.py:91
  18.2 1.5 %collective-permute-start.3 = (bf16[4,80,512]{2,1,0:T(8,128)(2,1)S(1)}, bf16[4,80,512]{2,1,0:T(8,128)(2,1)S(1)}, u32[]{:S(2)}, u32[]{:S(2)}) collective-permute-start(bf16[4,80,512]{2,1,0:T(8,128)(2,1)S(1)} %gather_fusion), channel_id=1, source_target_pairs={{0,2},{2,0},{4,6},{6,4},{1,3},{3,1},{5,7},{7,5},{8,10},{10,8},{12,... | collective-permute-start | bytes 983048 | tf_op jit(solution)/shard_map/ppermute | solution.py:91
  19.7 0.5 collective-permute-start.5
  20.2 6.2 %collective-permute-done.4 = bf16[4,80,512]{2,1,0:T(8,128)(2,1)S(1)} collective-permute-done((bf16[4,80,512]{2,1,0:T(8,128)(2,1)S(1)}, bf16[4,80,512]{2,1,0:T(8,128)(2,1)S(1)}, u32[]{:S(2)}, u32[]{:S(2)}) %collective-permute-start.4) | collective-permute-done | bytes 327712 | tf_op jit(solution)/shard_map/ppermute | solution.py:91
  26.5 0.0 copy-start.2
  26.5 2.4 %collective-permute-done.3 = bf16[4,80,512]{2,1,0:T(8,128)(2,1)S(1)} collective-permute-done((bf16[4,80,512]{2,1,0:T(8,128)(2,1)S(1)}, bf16[4,80,512]{2,1,0:T(8,128)(2,1)S(1)}, u32[]{:S(2)}, u32[]{:S(2)}) %collective-permute-start.3) | collective-permute-done | bytes 327712 | tf_op jit(solution)/shard_map/ppermute | solution.py:91
  28.9 0.0 copy-start.3
  28.9 5.0 %collective-permute-done.5 = bf16[4,80,512]{2,1,0:T(8,128)(2,1)S(1)} collective-permute-done((bf16[4,80,512]{2,1,0:T(8,128)(2,1)S(1)}, bf16[4,80,512]{2,1,0:T(8,128)(2,1)S(1)}, u32[]{:S(2)}, u32[]{:S(2)}) %collective-permute-start.5) | collective-permute-done | bytes 327712 | tf_op jit(solution)/shard_map/ppermute | solution.py:91
  33.8 0.0 copy-start.4
  33.8 0.0 copy-done.1
  33.8 0.0 copy-done.2
  33.8 0.0 copy-done.3
  33.9 0.7 %copy-done.4 = bf16[4,80,512]{2,1,0:T(8,128)(2,1)} copy-done((bf16[4,80,512]{2,1,0:T(8,128)(2,1)}, bf16[4,80,512]{2,1,0:T(8,128)(2,1)S(1)}, u32[]{:S(2)}) %copy-start.4) | copy-done | bytes 327704
  34.6 1.4 %pad_maximum_fusion = bf16[4,4,80,512]{3,2,0,1:T(8,128)(2,1)S(1)} fusion(bf16[4,1,80,512]{3,2,0,1:T(8,128)(2,1)} %bitcast.30, bf16[4,1,80,512]{3,2,0,1:T(8,128)(2,1)} %bitcast.28, bf16[4,1,80,512]{3,2,0,1:T(8,128)(2,1)} %bitcast.29, bf16[4,1,80,512]{3,2,0,1:T(8,128)(2,1)} %bitcast.26), kind=kLoop, calls=%fused_computation.4 | loop fusion | flops 1966080 | bytes 2621440 | tf_op jit(solution)/shard_map/stack | solution.py:92
  36.0 1.7 %gather_fusion.1 = bf16[4,4,80,512]{3,2,1,0:T(8,128)(2,1)} fusion(bf16[4,4,80,512]{3,2,0,1:T(8,128)(2,1)S(1)} %pad_maximum_fusion, s32[1024]{0:T(1024)S(1)} %pad_clamp_fusion), kind=kCustom, calls=%fused_computation.1 | custom fusion | bytes 2621456 | tf_op jit(solution)/shard_map/jit(_take)/gather | solution.py:94
  37.7 1.4 %copy.14 = bf16[4,4,80,512]{3,2,1,0:T(8,128)(2,1)S(1)} copy(bf16[4,4,80,512]{3,2,0,1:T(8,128)(2,1)} %bitcast.23) | data formatting | bytes 2621440 | tf_op jit(solution)/shard_map/jit(_take)/gather | solution.py:94
  39.1 0.3 broadcast_in_dim.8
  39.4 5.8 %all_to_all.11 = bf16[4,4,2,80,512]{4,3,1,0,2:T(8,128)(2,1)S(1)} all-to-all(bf16[4,4,2,80,512]{4,3,1,0,2:T(8,128)(2,1)S(1)} %broadcast_in_dim.8), channel_id=1, replica_groups=mesh['grp'=1,'tok_o'=4,'tok_m'=4,'tok_c'=2] {'tok_c'}, dimensions={2} | all-to-all | bytes 5242880 | tf_op jit(solution)/shard_map/all_to_all | solution.py:83
  45.3 0.2 slice.12
  45.5 0.0 slice-start
  45.5 0.2 copy.19
  45.8 0.0 copy-done
  45.8 0.0 slice-start.1
  45.8 1.3 %fusion = f32[512,2048]{1,0:T(8,128)S(1)} fusion(bf16[512,512]{1,0:T(8,128)(2,1)S(1)} %bitcast.24, bf16[2048,512]{1,0:T(8,128)(2,1)S(1)} %copy-done), kind=kOutput, calls=%fused_computation.13 | convolution fusion | flops 1073741824 | bytes 6815744 | tf_op jit(solution)/shard_map/dot_general | solution.py:72
  47.1 0.5 slice-done
  47.7 1.4 %slice-done.1 = s8[4194304]{0:T(1024)(128)(4,1)S(1)} async-done(((s8[8388608]{0:T(1024)(128)(4,1)}), s8[4194304]{0:T(1024)(128)(4,1)S(1)}, s32[]{:S(2)}) %slice-start.1) | async-done | bytes 4194328
  49.0 4.8 %bitcast_reduce_fusion = f32[2048,16]{0,1:T(8,128)S(1)} fusion(f32[512,2048]{1,0:T(8,128)S(1)} %fusion, bf16[2048,512]{1,0:T(8,128)(2,1)S(1)} %bitcast.25, bf16[2048,2048]{1,0:T(8,128)(2,1)S(1)} %bitcast.35), kind=kOutput, calls=%fused_computation.2 | convolution fusion | flops 4297031680 | bytes 14811136 | tf_op jit(solution)/shard_map/dot_general | solution.py:72
  53.8 0.1 multiply_reduce_fusion
  54.0 11.2 %all_to_all.12 = f32[32,1,16]{2,1,0:T(1,128)S(1)} all-to-all(f32[32,1,16]{2,1,0:T(1,128)S(1)} %broadcast_in_dim.9), channel_id=1, replica_groups=mesh['grp'=1,'tok_o'=4,'tok_m'=4,'tok_c'=2] {'tok_o','tok_m','tok_c'}, dimensions={0} | all-to-all | bytes 4096 | tf_op jit(solution)/shard_map/all_to_all | solution.py:77
  65.2 0.1 reduce_sum.29
  65.3 0.7 %broadcast_divide_fusion = f32[2048,16]{0,1:T(8,128)} fusion(f32[2048,16]{0,1:T(8,128)S(1)} %bitcast_reduce_fusion, f32[16]{0:T(128)S(1)} %add_sqrt_fusion), kind=kLoop, calls=%fused_computation.7 | loop fusion | flops 32768 | bytes 262208 | tf_op jit(solution)/shard_map/div | solution.py:116
  (9 shorter events, 0.1 us)
Async XLA Ops:
  0.0 45.8 %copy-start = (bf16[2048,512]{1,0:T(8,128)(2,1)S(1)}, bf16[2048,512]{1,0:T(8,128)(2,1)}, u32[]{:S(2)}) copy-start(bf16[2048,512]{1,0:T(8,128)(2,1)} %param.6) | copy-start | bytes 6291460
  2.9 8.3 %collective-permute-start.2 = (bf16[80,512]{1,0:T(8,128)(2,1)}, bf16[80,512]{1,0:T(8,128)(2,1)S(1)}, u32[]{:S(2)}, u32[]{:S(2)}) collective-permute-start(bf16[80,512]{1,0:T(8,128)(2,1)} %shard_map.55), channel_id=1, source_target_pairs={{0,24},{8,16},{16,8},{24,0},{1,25},{9,17},{17,9},{25,1},{2,26},{10... | collective-permute-start | bytes 245768 | tf_op jit(solution)/shard_map/ppermute | solution.py:91
  8.1 7.1 %collective-permute-start.1 = (bf16[80,512]{1,0:T(8,128)(2,1)}, bf16[80,512]{1,0:T(8,128)(2,1)S(1)}, u32[]{:S(2)}, u32[]{:S(2)}) collective-permute-start(bf16[80,512]{1,0:T(8,128)(2,1)} %shard_map.55), channel_id=1, source_target_pairs={{0,16},{8,24},{16,0},{24,8},{1,17},{9,25},{17,1},{25,9},{2,18},{10... | collective-permute-start | bytes 245768 | tf_op jit(solution)/shard_map/ppermute | solution.py:91
  8.1 7.1 %collective-permute-start = (bf16[80,512]{1,0:T(8,128)(2,1)}, bf16[80,512]{1,0:T(8,128)(2,1)S(1)}, u32[]{:S(2)}, u32[]{:S(2)}) collective-permute-start(bf16[80,512]{1,0:T(8,128)(2,1)} %shard_map.55), channel_id=1, source_target_pairs={{0,8},{8,0},{16,24},{24,16},{1,9},{9,1},{17,25},{25,17},{2,10},{10... | collective-permute-start | bytes 245768 | tf_op jit(solution)/shard_map/ppermute | solution.py:91
  16.6 17.2 %copy-start.1 = (bf16[4,80,512]{2,1,0:T(8,128)(2,1)}, bf16[4,80,512]{2,1,0:T(8,128)(2,1)S(1)}, u32[]{:S(2)}) copy-start(bf16[4,80,512]{2,1,0:T(8,128)(2,1)S(1)} %gather_fusion) | copy-start | bytes 983044
  16.7 9.8 %collective-permute-start.4 = (bf16[4,80,512]{2,1,0:T(8,128)(2,1)S(1)}, bf16[4,80,512]{2,1,0:T(8,128)(2,1)S(1)}, u32[]{:S(2)}, u32[]{:S(2)}) collective-permute-start(bf16[4,80,512]{2,1,0:T(8,128)(2,1)S(1)} %gather_fusion), channel_id=1, source_target_pairs={{0,4},{2,6},{4,0},{6,2},{1,5},{3,7},{5,1},{7,3},{8,12},{10,14},{12... | collective-permute-start | bytes 983048 | tf_op jit(solution)/shard_map/ppermute | solution.py:91
  18.2 10.6 %collective-permute-start.3 = (bf16[4,80,512]{2,1,0:T(8,128)(2,1)S(1)}, bf16[4,80,512]{2,1,0:T(8,128)(2,1)S(1)}, u32[]{:S(2)}, u32[]{:S(2)}) collective-permute-start(bf16[4,80,512]{2,1,0:T(8,128)(2,1)S(1)} %gather_fusion), channel_id=1, source_target_pairs={{0,2},{2,0},{4,6},{6,4},{1,3},{3,1},{5,7},{7,5},{8,10},{10,8},{12,... | collective-permute-start | bytes 983048 | tf_op jit(solution)/shard_map/ppermute | solution.py:91
  19.7 14.1 %collective-permute-start.5 = (bf16[4,80,512]{2,1,0:T(8,128)(2,1)S(1)}, bf16[4,80,512]{2,1,0:T(8,128)(2,1)S(1)}, u32[]{:S(2)}, u32[]{:S(2)}) collective-permute-start(bf16[4,80,512]{2,1,0:T(8,128)(2,1)S(1)} %gather_fusion), channel_id=1, source_target_pairs={{0,6},{2,4},{4,2},{6,0},{1,7},{3,5},{5,3},{7,1},{8,14},{10,12},{12... | collective-permute-start | bytes 983048 | tf_op jit(solution)/shard_map/ppermute | solution.py:91
  26.5 7.4 %copy-start.2 = (bf16[4,80,512]{2,1,0:T(8,128)(2,1)}, bf16[4,80,512]{2,1,0:T(8,128)(2,1)S(1)}, u32[]{:S(2)}) copy-start(bf16[4,80,512]{2,1,0:T(8,128)(2,1)S(1)} %collective-permute-done.4) | copy-start | bytes 983044
  28.9 5.0 %copy-start.3 = (bf16[4,80,512]{2,1,0:T(8,128)(2,1)}, bf16[4,80,512]{2,1,0:T(8,128)(2,1)S(1)}, u32[]{:S(2)}) copy-start(bf16[4,80,512]{2,1,0:T(8,128)(2,1)S(1)} %collective-permute-done.3) | copy-start | bytes 983044
  33.8 0.7 %copy-start.4 = (bf16[4,80,512]{2,1,0:T(8,128)(2,1)}, bf16[4,80,512]{2,1,0:T(8,128)(2,1)S(1)}, u32[]{:S(2)}) copy-start(bf16[4,80,512]{2,1,0:T(8,128)(2,1)S(1)} %collective-permute-done.5) | copy-start | bytes 983044
  45.5 2.2 %slice-start = ((s8[8388608]{0:T(1024)(128)(4,1)}), s8[4194304]{0:T(1024)(128)(4,1)S(1)}, s32[]{:S(2)}) async-start(s8[8388608]{0:T(1024)(128)(4,1)} %bitcast.34), calls=%async_computation.2 | async-start | bytes 8388608
  45.8 3.2 %slice-start.1 = ((s8[8388608]{0:T(1024)(128)(4,1)}), s8[4194304]{0:T(1024)(128)(4,1)S(1)}, s32[]{:S(2)}) async-start(s8[8388608]{0:T(1024)(128)(4,1)} %bitcast.34), calls=%async_computation.3 | async-start | bytes 8388608

commit v19 on v17

--- a/solution.py
+++ b/solution.py
@@ -23,7 +23,7 @@
             copies.append(copy)
     for copy in copies:
         copy.wait()
-    bases = (0, v_buf.shape[1])
+    bases = (u_buf.shape[1], 0)
     for k, buf in enumerate((v_buf, u_buf)):
         rows = buf.shape[1]
         base = bases[k]
@@ -103,7 +103,8 @@
     held = shifted(both, OUTER, 0)
     held = shifted(held, MIDDLE, 1)
     held = spread(held, CORE, 2)
-    return held[:, :, :, :rows_v].reshape(-1, cols), held[:, :, :, rows_v:].reshape(-1, cols)
+    rows_u = held.shape[3] - rows_v
+    return held[:, :, :, rows_u:].reshape(-1, cols), held[:, :, :, :rows_u].reshape(-1, cols)
 
 
 def on_device(activations, out_grads, v_bank, u_bank, query_ids):

time: 61 us -> 61 us (level)
  no operation moved by 1% of the time
where the time goes in v19:
time: 61 us; the launch traced here: 60.8 us
  waiting for transfers between devices  19.3 us (32%)
  blocking collectives  17.3 us (28%)
  starting transfers between devices  9.17 us (15%)
  matrix products  6.12 us (10%)
  other arithmetic  3.01 us (5%)
  Pallas kernels  2.93 us (5%)
  local copies, waits for them, and re-layouts  2.83 us (5%)
    ppermute x6, waiting for transfers between devices, shifted(): lax.ppermute(x, axis, [(j, j ^ s) for j in range(k)])  19.3 us
    all_to_all x1, blocking collectives, total_over(): return lax.all_to_all(copies, axis, 0, 0, tiled=False).sum(axis=0)  11.5 us
    ppermute x6, starting transfers between devices, shifted(): lax.ppermute(x, axis, [(j, j ^ s) for j in range(k)])  9.17 us
    dot_general x2, matrix products, folder(): return jnp.dot(left, piece, preferred_element_type=jnp.float32)  6.12 us
    all_to_all x1, blocking collectives, spread(): return lax.all_to_all(copies, axis, at, at, tiled=True)  5.84 us
    pallas_call x1, Pallas kernels, pick_columns(): pl.pallas_call(pick_kernel, out_shape=jax.ShapeDtypeStruct((v_bank.shape[...  2.93 us
    unnamed x8, local copies, waits for them, and re-layouts  2.16 us
    another operation x5, other arithmetic, shifted(): return jnp.stack(slots, axis=at)  2.07 us
  transfers between devices with their start and end apart: 6, of which 4 were waited for; matrix products, arithmetic and copies ran while one was open for 0% of the time, Pallas kernels for 0%

profile of v19, /device:TPU:0, one launch (start us, length us, event | category | flops | bytes accessed | tf_op | source)
XLA Modules:
  0.0 60.8 jit_solution(14450846191819154249)
XLA Ops:
  0.0 0.0 copy-start
  0.0 2.9 %shard_map.55 = bf16[80,512]{1,0:T(8,128)(2,1)} custom-call(s32[16]{0:T(128)} %ids_ref.1, bf16[64,65536]{1,0:T(8,128)(2,1)} %v_ref.1, bf16[16,65536]{1,0:T(8,128)(2,1)} %u_ref.1), custom_call_target="tpu_custom_call" | custom-call | tf_op jit(solution)/shard_map/pallas_call | solution.py:48
  2.9 3.1 %collective-permute-start.2 = (bf16[80,512]{1,0:T(8,128)(2,1)}, bf16[80,512]{1,0:T(8,128)(2,1)S(1)}, u32[]{:S(2)}, u32[]{:S(2)}) collective-permute-start(bf16[80,512]{1,0:T(8,128)(2,1)} %shard_map.55), channel_id=1, source_target_pairs={{0,8},{8,0},{16,24},{24,16},{1,9},{9,1},{17,25},{25,17},{2,10},{10... | collective-permute-start | bytes 245768 | tf_op jit(solution)/shard_map/ppermute | solution.py:91
  6.0 2.6 %collective-permute-start.1 = (bf16[80,512]{1,0:T(8,128)(2,1)}, bf16[80,512]{1,0:T(8,128)(2,1)S(1)}, u32[]{:S(2)}, u32[]{:S(2)}) collective-permute-start(bf16[80,512]{1,0:T(8,128)(2,1)} %shard_map.55), channel_id=1, source_target_pairs={{0,16},{8,24},{16,0},{24,8},{1,17},{9,25},{17,1},{25,9},{2,18},{10... | collective-permute-start | bytes 245768 | tf_op jit(solution)/shard_map/ppermute | solution.py:91
  8.6 0.0 collective-permute-start
  8.6 0.1 collective-permute-done.2
  8.7 6.8 %collective-permute-done.1 = bf16[80,512]{1,0:T(8,128)(2,1)S(1)} collective-permute-done((bf16[80,512]{1,0:T(8,128)(2,1)}, bf16[80,512]{1,0:T(8,128)(2,1)S(1)}, u32[]{:S(2)}, u32[]{:S(2)}) %collective-permute-start.1) | collective-permute-done | bytes 81952 | tf_op jit(solution)/shard_map/ppermute | solution.py:91
  15.5 0.0 collective-permute-done
  15.5 0.9 %select_bitcast_fusion.7 = (bf16[1,80,512]{2,1,0:T(8,128)(2,1)S(1)}, bf16[1,80,512]{2,1,0:T(8,128)(2,1)S(1)}, bf16[1,80,512]{2,1,0:T(8,128)(2,1)S(1)}, bf16[1,80,512]{2,1,0:T(8,128)(2,1)S(1)}) fusion(bf16[80,512]{1,0:T(8,128)(2,1)S(1)} %collective-permute-done, bf16[80,512]{1,0:T(8,128)(2,1)S(1)} %collective-permute-done.1, ...), kind=kLoop, calls=%fused_computation.12 | loop fusion | flops 491520 | bytes 655372 | tf_op jit(solution)/shard_map/stack | solution.py:98
  16.4 0.8 %pad_maximum_fusion.1 = bf16[4,80,512]{2,1,0:T(8,128)(2,1)} fusion(bf16[1,80,512]{2,1,0:T(8,128)(2,1)S(1)} %get-tuple-element.10, bf16[1,80,512]{2,1,0:T(8,128)(2,1)S(1)} %get-tuple-element.11, bf16[1,80,512]{2,1,0:T(8,128)(2,1)S(1)} %get-tuple-element.12, bf16[1,80,512]{2,1,0:T(8,128)(2,1)S(1)} %get-tuple-element.9), kind=kLoop, calls=%fused_computation.3 | loop fusion | flops 491520 | bytes 655360 | tf_op jit(solution)/shard_map/stack | solution.py:98
  17.2 1.5 %collective-permute-start.5 = (bf16[4,80,512]{2,1,0:T(8,128)(2,1)}, bf16[4,80,512]{2,1,0:T(8,128)(2,1)S(1)}, u32[]{:S(2)}, u32[]{:S(2)}) collective-permute-start(bf16[4,80,512]{2,1,0:T(8,128)(2,1)} %pad_maximum_fusion.1), channel_id=1, source_target_pairs={{0,2},{2,0},{4,6},{6,4},{1,3},{3,1},{5,7},{7,5},{8,10},{10,8},{12,... | collective-permute-start | bytes 983048 | tf_op jit(solution)/shard_map/ppermute | solution.py:91
  18.7 1.5 %collective-permute-start.4 = (bf16[4,80,512]{2,1,0:T(8,128)(2,1)}, bf16[4,80,512]{2,1,0:T(8,128)(2,1)S(1)}, u32[]{:S(2)}, u32[]{:S(2)}) collective-permute-start(bf16[4,80,512]{2,1,0:T(8,128)(2,1)} %pad_maximum_fusion.1), channel_id=1, source_target_pairs={{0,4},{2,6},{4,0},{6,2},{1,5},{3,7},{5,1},{7,3},{8,12},{10,14},{12... | collective-permute-start | bytes 983048 | tf_op jit(solution)/shard_map/ppermute | solution.py:91
  20.2 0.5 collective-permute-start.3
  20.6 7.4 %collective-permute-done.5 = bf16[4,80,512]{2,1,0:T(8,128)(2,1)S(1)} collective-permute-done((bf16[4,80,512]{2,1,0:T(8,128)(2,1)}, bf16[4,80,512]{2,1,0:T(8,128)(2,1)S(1)}, u32[]{:S(2)}, u32[]{:S(2)}) %collective-permute-start.5) | collective-permute-done | bytes 327712 | tf_op jit(solution)/shard_map/ppermute | solution.py:91
  28.0 5.1 %collective-permute-done.4 = bf16[4,80,512]{2,1,0:T(8,128)(2,1)S(1)} collective-permute-done((bf16[4,80,512]{2,1,0:T(8,128)(2,1)}, bf16[4,80,512]{2,1,0:T(8,128)(2,1)S(1)}, u32[]{:S(2)}, u32[]{:S(2)}) %collective-permute-start.4) | collective-permute-done | bytes 327712 | tf_op jit(solution)/shard_map/ppermute | solution.py:91
  33.1 0.0 collective-permute-done.3
  33.1 0.1 select_bitcast_fusion.2
  33.2 0.1 select_bitcast_fusion.3
  33.3 0.2 pad_maximum_fusion
  33.5 0.1 copy.14
  33.6 0.3 broadcast_in_dim.4
  33.9 5.8 %all_to_all.11 = bf16[4,4,2,80,512]{4,3,1,0,2:T(8,128)(2,1)S(1)} all-to-all(bf16[4,4,2,80,512]{4,3,1,0,2:T(8,128)(2,1)S(1)} %broadcast_in_dim.4), channel_id=1, replica_groups=mesh['grp'=1,'tok_o'=4,'tok_m'=4,'tok_c'=2] {'tok_c'}, dimensions={2} | all-to-all | bytes 5242880 | tf_op jit(solution)/shard_map/all_to_all | solution.py:83
  39.8 0.2 slice.8
  40.0 0.0 slice-start
  40.0 0.2 copy.19
  40.3 0.0 copy-done
  40.3 0.0 slice-start.1
  40.3 1.3 %fusion = f32[512,2048]{1,0:T(8,128)S(1)} fusion(bf16[512,512]{1,0:T(8,128)(2,1)S(1)} %bitcast.26, bf16[2048,512]{1,0:T(8,128)(2,1)S(1)} %copy-done), kind=kOutput, calls=%fused_computation.15 | convolution fusion | flops 1073741824 | bytes 6815744 | tf_op jit(solution)/shard_map/dot_general | solution.py:72
  41.6 0.5 slice-done
  42.2 1.4 %slice-done.1 = s8[4194304]{0:T(1024)(128)(4,1)S(1)} async-done(((s8[8388608]{0:T(1024)(128)(4,1)}), s8[4194304]{0:T(1024)(128)(4,1)S(1)}, s32[]{:S(2)}) %slice-start.1) | async-done | bytes 4194328
  43.5 4.8 %bitcast_reduce_fusion = f32[2048,16]{0,1:T(8,128)S(1)} fusion(f32[512,2048]{1,0:T(8,128)S(1)} %fusion, bf16[2048,512]{1,0:T(8,128)(2,1)S(1)} %bitcast.27, bf16[2048,2048]{1,0:T(8,128)(2,1)S(1)} %bitcast.29), kind=kOutput, calls=%fused_computation | convolution fusion | flops 4297031680 | bytes 14811136 | tf_op jit(solution)/shard_map/dot_general | solution.py:72
  48.3 0.1 multiply_reduce_fusion
  48.5 11.5 %all_to_all.12 = f32[32,1,16]{2,1,0:T(1,128)S(1)} all-to-all(f32[32,1,16]{2,1,0:T(1,128)S(1)} %broadcast_in_dim.5), channel_id=1, replica_groups=mesh['grp'=1,'tok_o'=4,'tok_m'=4,'tok_c'=2] {'tok_o','tok_m','tok_c'}, dimensions={0} | all-to-all | bytes 4096 | tf_op jit(solution)/shard_map/all_to_all | solution.py:77
  60.0 0.1 reduce_sum.29
  60.0 0.7 %broadcast_divide_fusion = f32[2048,16]{0,1:T(8,128)} fusion(f32[2048,16]{0,1:T(8,128)S(1)} %bitcast_reduce_fusion, f32[16]{0:T(128)S(1)} %add_sqrt_fusion), kind=kLoop, calls=%fused_computation.13 | loop fusion | flops 32768 | bytes 262208 | tf_op jit(solution)/shard_map/div | solution.py:121
  (5 shorter events, 0.1 us)
Async XLA Ops:
  0.0 40.3 %copy-start = (bf16[2048,512]{1,0:T(8,128)(2,1)S(1)}, bf16[2048,512]{1,0:T(8,128)(2,1)}, u32[]{:S(2)}) copy-start(bf16[2048,512]{1,0:T(8,128)(2,1)} %param.6) | copy-start | bytes 6291460
  2.9 5.7 %collective-permute-start.2 = (bf16[80,512]{1,0:T(8,128)(2,1)}, bf16[80,512]{1,0:T(8,128)(2,1)S(1)}, u32[]{:S(2)}, u32[]{:S(2)}) collective-permute-start(bf16[80,512]{1,0:T(8,128)(2,1)} %shard_map.55), channel_id=1, source_target_pairs={{0,8},{8,0},{16,24},{24,16},{1,9},{9,1},{17,25},{25,17},{2,10},{10... | collective-permute-start | bytes 245768 | tf_op jit(solution)/shard_map/ppermute | solution.py:91
  6.0 9.4 %collective-permute-start.1 = (bf16[80,512]{1,0:T(8,128)(2,1)}, bf16[80,512]{1,0:T(8,128)(2,1)S(1)}, u32[]{:S(2)}, u32[]{:S(2)}) collective-permute-start(bf16[80,512]{1,0:T(8,128)(2,1)} %shard_map.55), channel_id=1, source_target_pairs={{0,16},{8,24},{16,0},{24,8},{1,17},{9,25},{17,1},{25,9},{2,18},{10... | collective-permute-start | bytes 245768 | tf_op jit(solution)/shard_map/ppermute | solution.py:91
  8.6 6.8 %collective-permute-start = (bf16[80,512]{1,0:T(8,128)(2,1)}, bf16[80,512]{1,0:T(8,128)(2,1)S(1)}, u32[]{:S(2)}, u32[]{:S(2)}) collective-permute-start(bf16[80,512]{1,0:T(8,128)(2,1)} %shard_map.55), channel_id=1, source_target_pairs={{0,24},{8,16},{16,8},{24,0},{1,25},{9,17},{17,9},{25,1},{2,26},{10... | collective-permute-start | bytes 245768 | tf_op jit(solution)/shard_map/ppermute | solution.py:91
  17.2 10.9 %collective-permute-start.5 = (bf16[4,80,512]{2,1,0:T(8,128)(2,1)}, bf16[4,80,512]{2,1,0:T(8,128)(2,1)S(1)}, u32[]{:S(2)}, u32[]{:S(2)}) collective-permute-start(bf16[4,80,512]{2,1,0:T(8,128)(2,1)} %pad_maximum_fusion.1), channel_id=1, source_target_pairs={{0,2},{2,0},{4,6},{6,4},{1,3},{3,1},{5,7},{7,5},{8,10},{10,8},{12,... | collective-permute-start | bytes 983048 | tf_op jit(solution)/shard_map/ppermute | solution.py:91
  18.7 14.4 %collective-permute-start.4 = (bf16[4,80,512]{2,1,0:T(8,128)(2,1)}, bf16[4,80,512]{2,1,0:T(8,128)(2,1)S(1)}, u32[]{:S(2)}, u32[]{:S(2)}) collective-permute-start(bf16[4,80,512]{2,1,0:T(8,128)(2,1)} %pad_maximum_fusion.1), channel_id=1, source_target_pairs={{0,4},{2,6},{4,0},{6,2},{1,5},{3,7},{5,1},{7,3},{8,12},{10,14},{12... | collective-permute-start | bytes 983048 | tf_op jit(solution)/shard_map/ppermute | solution.py:91
  20.2 12.9 %collective-permute-start.3 = (bf16[4,80,512]{2,1,0:T(8,128)(2,1)}, bf16[4,80,512]{2,1,0:T(8,128)(2,1)S(1)}, u32[]{:S(2)}, u32[]{:S(2)}) collective-permute-start(bf16[4,80,512]{2,1,0:T(8,128)(2,1)} %pad_maximum_fusion.1), channel_id=1, source_target_pairs={{0,6},{2,4},{4,2},{6,0},{1,7},{3,5},{5,3},{7,1},{8,14},{10,12},{12... | collective-permute-start | bytes 983048 | tf_op jit(solution)/shard_map/ppermute | solution.py:91
  40.0 2.2 %slice-start = ((s8[8388608]{0:T(1024)(128)(4,1)}), s8[4194304]{0:T(1024)(128)(4,1)S(1)}, s32[]{:S(2)}) async-start(s8[8388608]{0:T(1024)(128)(4,1)} %bitcast.28), calls=%async_computation.2 | async-start | bytes 8388608
  40.3 3.2 %slice-start.1 = ((s8[8388608]{0:T(1024)(128)(4,1)}), s8[4194304]{0:T(1024)(128)(4,1)S(1)}, s32[]{:S(2)}) async-start(s8[8388608]{0:T(1024)(128)(4,1)} %bitcast.28), calls=%async_computation.3 | async-start | bytes 8388608

commit v20 on v16

--- a/solution.py
+++ b/solution.py
@@ -23,6 +23,8 @@
             copies.append(copy)
     bases = (0, v_buf.shape[1])
     for k, buf in enumerate((v_buf, u_buf)):
+        for copy in copies[k * queries:(k + 1) * queries]:
+            copy.wait()
         rows = buf.shape[1]
         base = bases[k]
         lane = lax.broadcasted_iota(jnp.int32, (rows, LANES), 1)
@@ -30,7 +32,6 @@
             acc = jnp.zeros((rows, LANES), buf.dtype)
             for j in range(PER_TILE):
                 q = g * PER_TILE + j
-                copies[k * queries + q].wait()
                 x = buf[q]
                 off = (ids_ref[q] % PER_TILE) * RANK
                 shift = (RANK * j - off + LANES) % LANES

time: 62.8 us -> 61.1 us (0.973)
  Pallas kernels: 4.73 us -> 3.05 us
    pallas_call x1, Pallas kernels: 4.73 us -> 3.05 us  [pick_columns(): pl.pallas_call(pick_kernel, out_shape=jax.ShapeDtypeStruct((v_bank.shape[...]
where the time goes in v20:
time: 61.1 us; the launch traced here: 60.9 us
  waiting for transfers between devices  19.3 us (32%)
  blocking collectives  17.3 us (28%)
  starting transfers between devices  9.17 us (15%)
  matrix products  6.12 us (10%)
  Pallas kernels  3.05 us (5%)
  other arithmetic  3.01 us (5%)
  local copies, waits for them, and re-layouts  2.79 us (5%)
    ppermute x6, waiting for transfers between devices, shifted(): lax.ppermute(x, axis, [(j, j ^ s) for j in range(k)])  19.3 us
    all_to_all x1, blocking collectives, total_over(): return lax.all_to_all(copies, axis, 0, 0, tiled=False).sum(axis=0)  11.5 us
    ppermute x6, starting transfers between devices, shifted(): lax.ppermute(x, axis, [(j, j ^ s) for j in range(k)])  9.17 us
    dot_general x2, matrix products, folder(): return jnp.dot(left, piece, preferred_element_type=jnp.float32)  6.12 us
    all_to_all x1, blocking collectives, spread(): return lax.all_to_all(copies, axis, at, at, tiled=True)  5.84 us
    pallas_call x1, Pallas kernels, pick_columns(): pl.pallas_call(pick_kernel, out_shape=jax.ShapeDtypeStruct((v_bank.shape[...  3.05 us
    unnamed x8, local copies, waits for them, and re-layouts  2.16 us
    another operation x5, other arithmetic, shifted(): return jnp.stack(slots, axis=at)  2.07 us
  transfers between devices with their start and end apart: 6, of which 4 were waited for; matrix products, arithmetic and copies ran while one was open for 0% of the time, Pallas kernels for 0%

profile of v20, /device:TPU:0, one launch (start us, length us, event | category | flops | bytes accessed | tf_op | source)
XLA Modules:
  0.0 60.9 jit_solution(3020489037266929130)
XLA Ops:
  0.0 0.0 copy-start
  0.0 3.0 %shard_map.55 = bf16[80,512]{1,0:T(8,128)(2,1)} custom-call(s32[16]{0:T(128)} %ids_ref.1, bf16[64,65536]{1,0:T(8,128)(2,1)} %v_ref.1, bf16[16,65536]{1,0:T(8,128)(2,1)} %u_ref.1), custom_call_target="tpu_custom_call" | custom-call | tf_op jit(solution)/shard_map/pallas_call | solution.py:48
  3.1 3.1 %collective-permute-start.2 = (bf16[80,512]{1,0:T(8,128)(2,1)}, bf16[80,512]{1,0:T(8,128)(2,1)S(1)}, u32[]{:S(2)}, u32[]{:S(2)}) collective-permute-start(bf16[80,512]{1,0:T(8,128)(2,1)} %shard_map.55), channel_id=1, source_target_pairs={{0,8},{8,0},{16,24},{24,16},{1,9},{9,1},{17,25},{25,17},{2,10},{10... | collective-permute-start | bytes 245768 | tf_op jit(solution)/shard_map/ppermute | solution.py:91
  6.1 2.6 %collective-permute-start.1 = (bf16[80,512]{1,0:T(8,128)(2,1)}, bf16[80,512]{1,0:T(8,128)(2,1)S(1)}, u32[]{:S(2)}, u32[]{:S(2)}) collective-permute-start(bf16[80,512]{1,0:T(8,128)(2,1)} %shard_map.55), channel_id=1, source_target_pairs={{0,16},{8,24},{16,0},{24,8},{1,17},{9,25},{17,1},{25,9},{2,18},{10... | collective-permute-start | bytes 245768 | tf_op jit(solution)/shard_map/ppermute | solution.py:91
  8.7 0.0 collective-permute-start
  8.7 0.1 collective-permute-done.2
  8.8 6.8 %collective-permute-done.1 = bf16[80,512]{1,0:T(8,128)(2,1)S(1)} collective-permute-done((bf16[80,512]{1,0:T(8,128)(2,1)}, bf16[80,512]{1,0:T(8,128)(2,1)S(1)}, u32[]{:S(2)}, u32[]{:S(2)}) %collective-permute-start.1) | collective-permute-done | bytes 81952 | tf_op jit(solution)/shard_map/ppermute | solution.py:91
  15.6 0.0 collective-permute-done
  15.6 0.9 %select_bitcast_fusion.7 = (bf16[1,80,512]{2,1,0:T(8,128)(2,1)S(1)}, bf16[1,80,512]{2,1,0:T(8,128)(2,1)S(1)}, bf16[1,80,512]{2,1,0:T(8,128)(2,1)S(1)}, bf16[1,80,512]{2,1,0:T(8,128)(2,1)S(1)}) fusion(bf16[80,512]{1,0:T(8,128)(2,1)S(1)} %collective-permute-done, bf16[80,512]{1,0:T(8,128)(2,1)S(1)} %collective-permute-done.1, ...), kind=kLoop, calls=%fused_computation.12 | loop fusion | flops 491520 | bytes 655372 | tf_op jit(solution)/shard_map/stack | solution.py:98
  16.5 0.8 %pad_maximum_fusion.1 = bf16[4,80,512]{2,1,0:T(8,128)(2,1)} fusion(bf16[1,80,512]{2,1,0:T(8,128)(2,1)S(1)} %get-tuple-element.10, bf16[1,80,512]{2,1,0:T(8,128)(2,1)S(1)} %get-tuple-element.11, bf16[1,80,512]{2,1,0:T(8,128)(2,1)S(1)} %get-tuple-element.12, bf16[1,80,512]{2,1,0:T(8,128)(2,1)S(1)} %get-tuple-element.9), kind=kLoop, calls=%fused_computation.3 | loop fusion | flops 491520 | bytes 655360 | tf_op jit(solution)/shard_map/stack | solution.py:98
  17.3 1.5 %collective-permute-start.5 = (bf16[4,80,512]{2,1,0:T(8,128)(2,1)}, bf16[4,80,512]{2,1,0:T(8,128)(2,1)S(1)}, u32[]{:S(2)}, u32[]{:S(2)}) collective-permute-start(bf16[4,80,512]{2,1,0:T(8,128)(2,1)} %pad_maximum_fusion.1), channel_id=1, source_target_pairs={{0,2},{2,0},{4,6},{6,4},{1,3},{3,1},{5,7},{7,5},{8,10},{10,8},{12,... | collective-permute-start | bytes 983048 | tf_op jit(solution)/shard_map/ppermute | solution.py:91
  18.8 1.5 %collective-permute-start.4 = (bf16[4,80,512]{2,1,0:T(8,128)(2,1)}, bf16[4,80,512]{2,1,0:T(8,128)(2,1)S(1)}, u32[]{:S(2)}, u32[]{:S(2)}) collective-permute-start(bf16[4,80,512]{2,1,0:T(8,128)(2,1)} %pad_maximum_fusion.1), channel_id=1, source_target_pairs={{0,4},{2,6},{4,0},{6,2},{1,5},{3,7},{5,1},{7,3},{8,12},{10,14},{12... | collective-permute-start | bytes 983048 | tf_op jit(solution)/shard_map/ppermute | solution.py:91
  20.3 0.5 collective-permute-start.3
  20.8 7.4 %collective-permute-done.5 = bf16[4,80,512]{2,1,0:T(8,128)(2,1)S(1)} collective-permute-done((bf16[4,80,512]{2,1,0:T(8,128)(2,1)}, bf16[4,80,512]{2,1,0:T(8,128)(2,1)S(1)}, u32[]{:S(2)}, u32[]{:S(2)}) %collective-permute-start.5) | collective-permute-done | bytes 327712 | tf_op jit(solution)/shard_map/ppermute | solution.py:91
  28.1 5.1 %collective-permute-done.4 = bf16[4,80,512]{2,1,0:T(8,128)(2,1)S(1)} collective-permute-done((bf16[4,80,512]{2,1,0:T(8,128)(2,1)}, bf16[4,80,512]{2,1,0:T(8,128)(2,1)S(1)}, u32[]{:S(2)}, u32[]{:S(2)}) %collective-permute-start.4) | collective-permute-done | bytes 327712 | tf_op jit(solution)/shard_map/ppermute | solution.py:91
  33.2 0.0 collective-permute-done.3
  33.2 0.1 select_bitcast_fusion.2
  33.3 0.1 select_bitcast_fusion.3
  33.4 0.2 pad_maximum_fusion
  33.6 0.1 copy.14
  33.7 0.3 broadcast_in_dim.4
  34.0 5.8 %all_to_all.11 = bf16[4,4,2,80,512]{4,3,1,0,2:T(8,128)(2,1)S(1)} all-to-all(bf16[4,4,2,80,512]{4,3,1,0,2:T(8,128)(2,1)S(1)} %broadcast_in_dim.4), channel_id=1, replica_groups=mesh['grp'=1,'tok_o'=4,'tok_m'=4,'tok_c'=2] {'tok_c'}, dimensions={2} | all-to-all | bytes 5242880 | tf_op jit(solution)/shard_map/all_to_all | solution.py:83
  39.9 0.2 slice.8
  40.1 0.0 slice-start
  40.1 0.2 copy.19
  40.4 0.0 copy-done
  40.4 0.0 slice-start.1
  40.4 1.3 %fusion = f32[512,2048]{1,0:T(8,128)S(1)} fusion(bf16[512,512]{1,0:T(8,128)(2,1)S(1)} %bitcast.26, bf16[2048,512]{1,0:T(8,128)(2,1)S(1)} %copy-done), kind=kOutput, calls=%fused_computation.15 | convolution fusion | flops 1073741824 | bytes 6815744 | tf_op jit(solution)/shard_map/dot_general | solution.py:72
  41.7 0.5 slice-done
  42.2 1.4 %slice-done.1 = s8[4194304]{0:T(1024)(128)(4,1)S(1)} async-done(((s8[8388608]{0:T(1024)(128)(4,1)}), s8[4194304]{0:T(1024)(128)(4,1)S(1)}, s32[]{:S(2)}) %slice-start.1) | async-done | bytes 4194328
  43.6 4.8 %bitcast_reduce_fusion = f32[2048,16]{0,1:T(8,128)S(1)} fusion(f32[512,2048]{1,0:T(8,128)S(1)} %fusion, bf16[2048,512]{1,0:T(8,128)(2,1)S(1)} %bitcast.27, bf16[2048,2048]{1,0:T(8,128)(2,1)S(1)} %bitcast.29), kind=kOutput, calls=%fused_computation | convolution fusion | flops 4297031680 | bytes 14811136 | tf_op jit(solution)/shard_map/dot_general | solution.py:72
  48.4 0.1 multiply_reduce_fusion
  48.6 11.5 %all_to_all.12 = f32[32,1,16]{2,1,0:T(1,128)S(1)} all-to-all(f32[32,1,16]{2,1,0:T(1,128)S(1)} %broadcast_in_dim.5), channel_id=1, replica_groups=mesh['grp'=1,'tok_o'=4,'tok_m'=4,'tok_c'=2] {'tok_o','tok_m','tok_c'}, dimensions={0} | all-to-all | bytes 4096 | tf_op jit(solution)/shard_map/all_to_all | solution.py:77
  60.1 0.1 reduce_sum.29
  60.1 0.7 %broadcast_divide_fusion = f32[2048,16]{0,1:T(8,128)} fusion(f32[2048,16]{0,1:T(8,128)S(1)} %bitcast_reduce_fusion, f32[16]{0:T(128)S(1)} %add_sqrt_fusion), kind=kLoop, calls=%fused_computation.13 | loop fusion | flops 32768 | bytes 262208 | tf_op jit(solution)/shard_map/div | solution.py:120
  (5 shorter events, 0.1 us)
Async XLA Ops:
  0.0 40.4 %copy-start = (bf16[2048,512]{1,0:T(8,128)(2,1)S(1)}, bf16[2048,512]{1,0:T(8,128)(2,1)}, u32[]{:S(2)}) copy-start(bf16[2048,512]{1,0:T(8,128)(2,1)} %param.6) | copy-start | bytes 6291460
  3.1 5.7 %collective-permute-start.2 = (bf16[80,512]{1,0:T(8,128)(2,1)}, bf16[80,512]{1,0:T(8,128)(2,1)S(1)}, u32[]{:S(2)}, u32[]{:S(2)}) collective-permute-start(bf16[80,512]{1,0:T(8,128)(2,1)} %shard_map.55), channel_id=1, source_target_pairs={{0,8},{8,0},{16,24},{24,16},{1,9},{9,1},{17,25},{25,17},{2,10},{10... | collective-permute-start | bytes 245768 | tf_op jit(solution)/shard_map/ppermute | solution.py:91
  6.1 9.4 %collective-permute-start.1 = (bf16[80,512]{1,0:T(8,128)(2,1)}, bf16[80,512]{1,0:T(8,128)(2,1)S(1)}, u32[]{:S(2)}, u32[]{:S(2)}) collective-permute-start(bf16[80,512]{1,0:T(8,128)(2,1)} %shard_map.55), channel_id=1, source_target_pairs={{0,16},{8,24},{16,0},{24,8},{1,17},{9,25},{17,1},{25,9},{2,18},{10... | collective-permute-start | bytes 245768 | tf_op jit(solution)/shard_map/ppermute | solution.py:91
  8.7 6.8 %collective-permute-start = (bf16[80,512]{1,0:T(8,128)(2,1)}, bf16[80,512]{1,0:T(8,128)(2,1)S(1)}, u32[]{:S(2)}, u32[]{:S(2)}) collective-permute-start(bf16[80,512]{1,0:T(8,128)(2,1)} %shard_map.55), channel_id=1, source_target_pairs={{0,24},{8,16},{16,8},{24,0},{1,25},{9,17},{17,9},{25,1},{2,26},{10... | collective-permute-start | bytes 245768 | tf_op jit(solution)/shard_map/ppermute | solution.py:91
  17.3 10.9 %collective-permute-start.5 = (bf16[4,80,512]{2,1,0:T(8,128)(2,1)}, bf16[4,80,512]{2,1,0:T(8,128)(2,1)S(1)}, u32[]{:S(2)}, u32[]{:S(2)}) collective-permute-start(bf16[4,80,512]{2,1,0:T(8,128)(2,1)} %pad_maximum_fusion.1), channel_id=1, source_target_pairs={{0,2},{2,0},{4,6},{6,4},{1,3},{3,1},{5,7},{7,5},{8,10},{10,8},{12,... | collective-permute-start | bytes 983048 | tf_op jit(solution)/shard_map/ppermute | solution.py:91
  18.8 14.4 %collective-permute-start.4 = (bf16[4,80,512]{2,1,0:T(8,128)(2,1)}, bf16[4,80,512]{2,1,0:T(8,128)(2,1)S(1)}, u32[]{:S(2)}, u32[]{:S(2)}) collective-permute-start(bf16[4,80,512]{2,1,0:T(8,128)(2,1)} %pad_maximum_fusion.1), channel_id=1, source_target_pairs={{0,4},{2,6},{4,0},{6,2},{1,5},{3,7},{5,1},{7,3},{8,12},{10,14},{12... | collective-permute-start | bytes 983048 | tf_op jit(solution)/shard_map/ppermute | solution.py:91
  20.3 12.9 %collective-permute-start.3 = (bf16[4,80,512]{2,1,0:T(8,128)(2,1)}, bf16[4,80,512]{2,1,0:T(8,128)(2,1)S(1)}, u32[]{:S(2)}, u32[]{:S(2)}) collective-permute-start(bf16[4,80,512]{2,1,0:T(8,128)(2,1)} %pad_maximum_fusion.1), channel_id=1, source_target_pairs={{0,6},{2,4},{4,2},{6,0},{1,7},{3,5},{5,3},{7,1},{8,14},{10,12},{12... | collective-permute-start | bytes 983048 | tf_op jit(solution)/shard_map/ppermute | solution.py:91
  40.1 2.2 %slice-start = ((s8[8388608]{0:T(1024)(128)(4,1)}), s8[4194304]{0:T(1024)(128)(4,1)S(1)}, s32[]{:S(2)}) async-start(s8[8388608]{0:T(1024)(128)(4,1)} %bitcast.28), calls=%async_computation.2 | async-start | bytes 8388608
  40.4 3.2 %slice-start.1 = ((s8[8388608]{0:T(1024)(128)(4,1)}), s8[4194304]{0:T(1024)(128)(4,1)S(1)}, s32[]{:S(2)}) async-start(s8[8388608]{0:T(1024)(128)(4,1)} %bitcast.28), calls=%async_computation.3 | async-start | bytes 8388608

commit v21 on v17

--- a/solution.py
+++ b/solution.py
@@ -117,7 +117,7 @@
     scores = (proj_in * proj_out).reshape(tok_rows, queries, RANK).sum(axis=2)
     total = total_over(jnp.sum(scores * scores, axis=0), TOK, n)
     scale = jnp.sqrt(total / (tok_rows * n) + 1e-06)
-    return scores / scale[None, :]
+    return scores * (1.0 / scale)[None, :]
 
 
 def split_mesh(mesh):

time: 61 us -> 61 us (level)
    div x1 -> x0, other arithmetic: 0.75 us -> none  [on_device(): return scores / scale[None, :]]
    mul x0 -> x1, other arithmetic: none -> 0.74 us  [on_device(): return scores * (1.0 / scale)[None, :]]
where the time goes in v21:
time: 61 us; the launch traced here: 60.7 us
  waiting for transfers between devices  19.3 us (32%)
  blocking collectives  17.3 us (28%)
  starting transfers between devices  9.17 us (15%)
  matrix products  6.12 us (10%)
  other arithmetic  3 us (5%)
  Pallas kernels  2.93 us (5%)
  local copies, waits for them, and re-layouts  2.79 us (5%)
    ppermute x6, waiting for transfers between devices, shifted(): lax.ppermute(x, axis, [(j, j ^ s) for j in range(k)])  19.3 us
    all_to_all x1, blocking collectives, total_over(): return lax.all_to_all(copies, axis, 0, 0, tiled=False).sum(axis=0)  11.5 us
    ppermute x6, starting transfers between devices, shifted(): lax.ppermute(x, axis, [(j, j ^ s) for j in range(k)])  9.17 us
    dot_general x2, matrix products, folder(): return jnp.dot(left, piece, preferred_element_type=jnp.float32)  6.12 us
    all_to_all x1, blocking collectives, spread(): return lax.all_to_all(copies, axis, at, at, tiled=True)  5.84 us
    pallas_call x1, Pallas kernels, pick_columns(): pl.pallas_call(pick_kernel, out_shape=jax.ShapeDtypeStruct((v_bank.shape[...  2.93 us
    unnamed x8, local copies, waits for them, and re-layouts  2.16 us
    another operation x5, other arithmetic, shifted(): return jnp.stack(slots, axis=at)  2.07 us
  transfers between devices with their start and end apart: 6, of which 4 were waited for; matrix products, arithmetic and copies ran while one was open for 0% of the time, Pallas kernels for 0%

profile of v21, /device:TPU:0, one launch (start us, length us, event | category | flops | bytes accessed | tf_op | source)
XLA Modules:
  0.0 60.7 jit_solution(2114843894905663881)
XLA Ops:
  0.0 0.0 copy-start
  0.0 2.9 %shard_map.55 = bf16[80,512]{1,0:T(8,128)(2,1)} custom-call(s32[16]{0:T(128)} %ids_ref.1, bf16[64,65536]{1,0:T(8,128)(2,1)} %v_ref.1, bf16[16,65536]{1,0:T(8,128)(2,1)} %u_ref.1), custom_call_target="tpu_custom_call" | custom-call | tf_op jit(solution)/shard_map/pallas_call | solution.py:48
  2.9 3.1 %collective-permute-start.2 = (bf16[80,512]{1,0:T(8,128)(2,1)}, bf16[80,512]{1,0:T(8,128)(2,1)S(1)}, u32[]{:S(2)}, u32[]{:S(2)}) collective-permute-start(bf16[80,512]{1,0:T(8,128)(2,1)} %shard_map.55), channel_id=1, source_target_pairs={{0,8},{8,0},{16,24},{24,16},{1,9},{9,1},{17,25},{25,17},{2,10},{10... | collective-permute-start | bytes 245768 | tf_op jit(solution)/shard_map/ppermute | solution.py:91
  6.0 2.6 %collective-permute-start.1 = (bf16[80,512]{1,0:T(8,128)(2,1)}, bf16[80,512]{1,0:T(8,128)(2,1)S(1)}, u32[]{:S(2)}, u32[]{:S(2)}) collective-permute-start(bf16[80,512]{1,0:T(8,128)(2,1)} %shard_map.55), channel_id=1, source_target_pairs={{0,16},{8,24},{16,0},{24,8},{1,17},{9,25},{17,1},{25,9},{2,18},{10... | collective-permute-start | bytes 245768 | tf_op jit(solution)/shard_map/ppermute | solution.py:91
  8.6 0.0 collective-permute-start
  8.6 0.1 collective-permute-done.2
  8.7 6.8 %collective-permute-done.1 = bf16[80,512]{1,0:T(8,128)(2,1)S(1)} collective-permute-done((bf16[80,512]{1,0:T(8,128)(2,1)}, bf16[80,512]{1,0:T(8,128)(2,1)S(1)}, u32[]{:S(2)}, u32[]{:S(2)}) %collective-permute-start.1) | collective-permute-done | bytes 81952 | tf_op jit(solution)/shard_map/ppermute | solution.py:91
  15.5 0.0 collective-permute-done
  15.5 0.9 %select_bitcast_fusion.7 = (bf16[1,80,512]{2,1,0:T(8,128)(2,1)S(1)}, bf16[1,80,512]{2,1,0:T(8,128)(2,1)S(1)}, bf16[1,80,512]{2,1,0:T(8,128)(2,1)S(1)}, bf16[1,80,512]{2,1,0:T(8,128)(2,1)S(1)}) fusion(bf16[80,512]{1,0:T(8,128)(2,1)S(1)} %collective-permute-done, bf16[80,512]{1,0:T(8,128)(2,1)S(1)} %collective-permute-done.1, ...), kind=kLoop, calls=%fused_computation.12 | loop fusion | flops 491520 | bytes 655372 | tf_op jit(solution)/shard_map/stack | solution.py:98
  16.4 0.8 %pad_maximum_fusion.1 = bf16[4,80,512]{2,1,0:T(8,128)(2,1)} fusion(bf16[1,80,512]{2,1,0:T(8,128)(2,1)S(1)} %get-tuple-element.10, bf16[1,80,512]{2,1,0:T(8,128)(2,1)S(1)} %get-tuple-element.11, bf16[1,80,512]{2,1,0:T(8,128)(2,1)S(1)} %get-tuple-element.12, bf16[1,80,512]{2,1,0:T(8,128)(2,1)S(1)} %get-tuple-element.9), kind=kLoop, calls=%fused_computation.3 | loop fusion | flops 491520 | bytes 655360 | tf_op jit(solution)/shard_map/stack | solution.py:98
  17.2 1.5 %collective-permute-start.5 = (bf16[4,80,512]{2,1,0:T(8,128)(2,1)}, bf16[4,80,512]{2,1,0:T(8,128)(2,1)S(1)}, u32[]{:S(2)}, u32[]{:S(2)}) collective-permute-start(bf16[4,80,512]{2,1,0:T(8,128)(2,1)} %pad_maximum_fusion.1), channel_id=1, source_target_pairs={{0,2},{2,0},{4,6},{6,4},{1,3},{3,1},{5,7},{7,5},{8,10},{10,8},{12,... | collective-permute-start | bytes 983048 | tf_op jit(solution)/shard_map/ppermute | solution.py:91
  18.7 1.5 %collective-permute-start.4 = (bf16[4,80,512]{2,1,0:T(8,128)(2,1)}, bf16[4,80,512]{2,1,0:T(8,128)(2,1)S(1)}, u32[]{:S(2)}, u32[]{:S(2)}) collective-permute-start(bf16[4,80,512]{2,1,0:T(8,128)(2,1)} %pad_maximum_fusion.1), channel_id=1, source_target_pairs={{0,4},{2,6},{4,0},{6,2},{1,5},{3,7},{5,1},{7,3},{8,12},{10,14},{12... | collective-permute-start | bytes 983048 | tf_op jit(solution)/shard_map/ppermute | solution.py:91
  20.2 0.5 collective-permute-start.3
  20.6 7.4 %collective-permute-done.5 = bf16[4,80,512]{2,1,0:T(8,128)(2,1)S(1)} collective-permute-done((bf16[4,80,512]{2,1,0:T(8,128)(2,1)}, bf16[4,80,512]{2,1,0:T(8,128)(2,1)S(1)}, u32[]{:S(2)}, u32[]{:S(2)}) %collective-permute-start.5) | collective-permute-done | bytes 327712 | tf_op jit(solution)/shard_map/ppermute | solution.py:91
  28.0 5.1 %collective-permute-done.4 = bf16[4,80,512]{2,1,0:T(8,128)(2,1)S(1)} collective-permute-done((bf16[4,80,512]{2,1,0:T(8,128)(2,1)}, bf16[4,80,512]{2,1,0:T(8,128)(2,1)S(1)}, u32[]{:S(2)}, u32[]{:S(2)}) %collective-permute-start.4) | collective-permute-done | bytes 327712 | tf_op jit(solution)/shard_map/ppermute | solution.py:91
  33.1 0.0 collective-permute-done.3
  33.1 0.1 select_bitcast_fusion.2
  33.2 0.1 select_bitcast_fusion.3
  33.3 0.2 pad_maximum_fusion
  33.5 0.1 copy.14
  33.6 0.3 broadcast_in_dim.4
  33.9 5.8 %all_to_all.11 = bf16[4,4,2,80,512]{4,3,1,0,2:T(8,128)(2,1)S(1)} all-to-all(bf16[4,4,2,80,512]{4,3,1,0,2:T(8,128)(2,1)S(1)} %broadcast_in_dim.4), channel_id=1, replica_groups=mesh['grp'=1,'tok_o'=4,'tok_m'=4,'tok_c'=2] {'tok_c'}, dimensions={2} | all-to-all | bytes 5242880 | tf_op jit(solution)/shard_map/all_to_all | solution.py:83
  39.8 0.2 slice.8
  39.9 0.0 slice-start
  39.9 0.2 copy.19
  40.2 0.0 copy-done
  40.3 0.0 slice-start.1
  40.3 1.3 %fusion = f32[512,2048]{1,0:T(8,128)S(1)} fusion(bf16[512,512]{1,0:T(8,128)(2,1)S(1)} %bitcast.26, bf16[2048,512]{1,0:T(8,128)(2,1)S(1)} %copy-done), kind=kOutput, calls=%fused_computation.15 | convolution fusion | flops 1073741824 | bytes 6815744 | tf_op jit(solution)/shard_map/dot_general | solution.py:72
  41.6 0.5 slice-done
  42.1 1.4 %slice-done.1 = s8[4194304]{0:T(1024)(128)(4,1)S(1)} async-done(((s8[8388608]{0:T(1024)(128)(4,1)}), s8[4194304]{0:T(1024)(128)(4,1)S(1)}, s32[]{:S(2)}) %slice-start.1) | async-done | bytes 4194328
  43.5 4.8 %bitcast_reduce_fusion = f32[2048,16]{0,1:T(8,128)S(1)} fusion(f32[512,2048]{1,0:T(8,128)S(1)} %fusion, bf16[2048,512]{1,0:T(8,128)(2,1)S(1)} %bitcast.27, bf16[2048,2048]{1,0:T(8,128)(2,1)S(1)} %bitcast.29), kind=kOutput, calls=%fused_computation | convolution fusion | flops 4297031680 | bytes 14811136 | tf_op jit(solution)/shard_map/dot_general | solution.py:72
  48.3 0.1 multiply_reduce_fusion
  48.5 11.5 %all_to_all.12 = f32[32,1,16]{2,1,0:T(1,128)S(1)} all-to-all(f32[32,1,16]{2,1,0:T(1,128)S(1)} %broadcast_in_dim.5), channel_id=1, replica_groups=mesh['grp'=1,'tok_o'=4,'tok_m'=4,'tok_c'=2] {'tok_o','tok_m','tok_c'}, dimensions={0} | all-to-all | bytes 4096 | tf_op jit(solution)/shard_map/all_to_all | solution.py:77
  59.9 0.1 reduce_sum.29
  60.0 0.7 %broadcast_multiply_fusion = f32[2048,16]{0,1:T(8,128)} fusion(f32[2048,16]{0,1:T(8,128)S(1)} %bitcast_reduce_fusion, f32[16]{0:T(128)S(1)} %add_rsqrt_fusion), kind=kLoop, calls=%fused_computation.13 | loop fusion | flops 32768 | bytes 262208 | tf_op jit(solution)/shard_map/mul | solution.py:120
  (5 shorter events, 0.1 us)
Async XLA Ops:
  0.0 40.3 %copy-start = (bf16[2048,512]{1,0:T(8,128)(2,1)S(1)}, bf16[2048,512]{1,0:T(8,128)(2,1)}, u32[]{:S(2)}) copy-start(bf16[2048,512]{1,0:T(8,128)(2,1)} %param.6) | copy-start | bytes 6291460
  2.9 5.7 %collective-permute-start.2 = (bf16[80,512]{1,0:T(8,128)(2,1)}, bf16[80,512]{1,0:T(8,128)(2,1)S(1)}, u32[]{:S(2)}, u32[]{:S(2)}) collective-permute-start(bf16[80,512]{1,0:T(8,128)(2,1)} %shard_map.55), channel_id=1, source_target_pairs={{0,8},{8,0},{16,24},{24,16},{1,9},{9,1},{17,25},{25,17},{2,10},{10... | collective-permute-start | bytes 245768 | tf_op jit(solution)/shard_map/ppermute | solution.py:91
  6.0 9.4 %collective-permute-start.1 = (bf16[80,512]{1,0:T(8,128)(2,1)}, bf16[80,512]{1,0:T(8,128)(2,1)S(1)}, u32[]{:S(2)}, u32[]{:S(2)}) collective-permute-start(bf16[80,512]{1,0:T(8,128)(2,1)} %shard_map.55), channel_id=1, source_target_pairs={{0,16},{8,24},{16,0},{24,8},{1,17},{9,25},{17,1},{25,9},{2,18},{10... | collective-permute-start | bytes 245768 | tf_op jit(solution)/shard_map/ppermute | solution.py:91
  8.6 6.8 %collective-permute-start = (bf16[80,512]{1,0:T(8,128)(2,1)}, bf16[80,512]{1,0:T(8,128)(2,1)S(1)}, u32[]{:S(2)}, u32[]{:S(2)}) collective-permute-start(bf16[80,512]{1,0:T(8,128)(2,1)} %shard_map.55), channel_id=1, source_target_pairs={{0,24},{8,16},{16,8},{24,0},{1,25},{9,17},{17,9},{25,1},{2,26},{10... | collective-permute-start | bytes 245768 | tf_op jit(solution)/shard_map/ppermute | solution.py:91
  17.2 10.9 %collective-permute-start.5 = (bf16[4,80,512]{2,1,0:T(8,128)(2,1)}, bf16[4,80,512]{2,1,0:T(8,128)(2,1)S(1)}, u32[]{:S(2)}, u32[]{:S(2)}) collective-permute-start(bf16[4,80,512]{2,1,0:T(8,128)(2,1)} %pad_maximum_fusion.1), channel_id=1, source_target_pairs={{0,2},{2,0},{4,6},{6,4},{1,3},{3,1},{5,7},{7,5},{8,10},{10,8},{12,... | collective-permute-start | bytes 983048 | tf_op jit(solution)/shard_map/ppermute | solution.py:91
  18.7 14.4 %collective-permute-start.4 = (bf16[4,80,512]{2,1,0:T(8,128)(2,1)}, bf16[4,80,512]{2,1,0:T(8,128)(2,1)S(1)}, u32[]{:S(2)}, u32[]{:S(2)}) collective-permute-start(bf16[4,80,512]{2,1,0:T(8,128)(2,1)} %pad_maximum_fusion.1), channel_id=1, source_target_pairs={{0,4},{2,6},{4,0},{6,2},{1,5},{3,7},{5,1},{7,3},{8,12},{10,14},{12... | collective-permute-start | bytes 983048 | tf_op jit(solution)/shard_map/ppermute | solution.py:91
  20.2 12.9 %collective-permute-start.3 = (bf16[4,80,512]{2,1,0:T(8,128)(2,1)}, bf16[4,80,512]{2,1,0:T(8,128)(2,1)S(1)}, u32[]{:S(2)}, u32[]{:S(2)}) collective-permute-start(bf16[4,80,512]{2,1,0:T(8,128)(2,1)} %pad_maximum_fusion.1), channel_id=1, source_target_pairs={{0,6},{2,4},{4,2},{6,0},{1,7},{3,5},{5,3},{7,1},{8,14},{10,12},{12... | collective-permute-start | bytes 983048 | tf_op jit(solution)/shard_map/ppermute | solution.py:91
  39.9 2.2 %slice-start = ((s8[8388608]{0:T(1024)(128)(4,1)}), s8[4194304]{0:T(1024)(128)(4,1)S(1)}, s32[]{:S(2)}) async-start(s8[8388608]{0:T(1024)(128)(4,1)} %bitcast.28), calls=%async_computation.2 | async-start | bytes 8388608
  40.3 3.2 %slice-start.1 = ((s8[8388608]{0:T(1024)(128)(4,1)}), s8[4194304]{0:T(1024)(128)(4,1)S(1)}, s32[]{:S(2)}) async-start(s8[8388608]{0:T(1024)(128)(4,1)} %bitcast.28), calls=%async_computation.3 | async-start | bytes 8388608
